TPU v7x, 256 devices: a whole 4x4x8 slice. The times are simulated.
256 devices in a mesh: row: 16 (over y, x), col: 16 (over z, core).
Axes of the slice: x: 4, y: 4, z: 8, core: 2. Of those that a mesh axis runs over, the one named last changes fastest.
Arguments:
- probe_block: bfloat16 [64, 262144], P(None, ('row', 'col'))
- prior_blocks: bfloat16 [4, 64, 262144], P(None, None, ('row', 'col'))
- self_relatedness: float32 [262144], P(('row', 'col')), may hold values from 0.5 to 2
- tile_values: bfloat16 [1280, 1024, 1024], P(('row', 'col')), may hold values from -0.125 to 0.125
- tile_index: int32 [1280, 3], P(('row', 'col')), may hold values from 0 to 255, as said below
Outputs:
- residual_block: float32 [64, 262144], P(None, ('row', 'col'))
- coefficients: float32 [5, 64, 64], replicated
Inputs may be any that keep to these rules, and one draw needn't show every extreme that they name: `tile_index`: rows d * 5 to d * 5 + 4 belong to the device d = r * C + c at mesh position (r, c), C the size of the col axis. In a row with column 2 equal to 1 (live) the tile row lies in [r * C, r * C + C), the tile column j has j % C == c, and tile row <= tile column; live pairs of one device are distinct. Column 2 is 0 in dead rows, which repeat the indices of the device's first row. Live counts vary between devices (not all equal), and some device has all 5 rows live.
All inputs are finite; a program needn't handle non-finite values.
Results may differ from a plain program's by a relative error of at most 0.0003.
Values may be sent and summed in bfloat16 or wider, within the bound.
No kernel may reach another device: no remote copies, remote signals or barrier semaphores. Data moves between devices by JAX's collectives and lax.ppermute only.
A program may use at most 128 MiB of HBM per device.

v0:
```python
import jax
import jax.numpy as jnp
from jax import lax
from jax.sharding import PartitionSpec as P


def tile_products(tile_values, tile_index, row_probes, col_probes, col_count):
    tile_width = tile_values.shape[1]
    row_spans = row_probes.shape[1] // tile_width
    col_spans = col_probes.shape[1] // tile_width
    forwards, mirrors, row_spans_of, col_spans_of = [], [], [], []
    for slot_index in range(tile_values.shape[0]):
        current_tile = tile_values[slot_index]
        live = tile_index[slot_index, 2] > 0
        row_span = tile_index[slot_index, 0] % col_count
        col_span = tile_index[slot_index, 1] // col_count
        right = lax.dynamic_slice_in_dim(col_probes, col_span * tile_width, tile_width, 1)
        left = lax.dynamic_slice_in_dim(row_probes, row_span * tile_width, tile_width, 1)
        forward = lax.dot_general(
            right, current_tile, (((1,), (1,)), ((), ())), preferred_element_type=jnp.float32
        )
        mirror = jnp.dot(left, current_tile, preferred_element_type=jnp.float32)
        forwards.append(forward)
        mirrors.append(mirror)
        row_spans_of.append(jnp.where(live, row_span, -1))
        col_spans_of.append(jnp.where(live, col_span, -1))
    row_part = jnp.stack(spread_spans(forwards, row_spans_of, row_spans))
    col_part = jnp.concatenate(spread_spans(mirrors, col_spans_of, col_spans), axis=1)
    return row_part, col_part


def spread_spans(terms, spans_of, span_count):
    pieces = []
    for span in range(span_count):
        piece = None
        for term, span_of in zip(terms, spans_of):
            part = jnp.where(span_of == span, term, 0.0)
            piece = part if piece is None else piece + part
        pieces.append(piece)
    return pieces


def sum_rows(row_part):
    size = lax.axis_size("col")
    if size & (size - 1):
        flat = jnp.concatenate(list(row_part), axis=1)
        return lax.psum_scatter(flat, "col", scatter_dimension=1, tiled=True)
    stride = 1
    while stride < size:
        bit = lax.axis_index("col") // stride % 2
        grouped = row_part.reshape(row_part.shape[0] // 2, 2, *row_part.shape[1:])
        keep = lax.dynamic_index_in_dim(grouped, bit, 1, keepdims=False)
        give = lax.dynamic_index_in_dim(grouped, 1 - bit, 1, keepdims=False)
        pairs = [(index, index ^ stride) for index in range(size)]
        row_part = keep + lax.ppermute(give, "col", pairs)
        stride *= 2
    return row_part[0]


def sum_columns(col_part):
    return lax.psum_scatter(col_part, "row", scatter_dimension=1, tiled=True)


def hypercube_sum(value, axes):
    for axis in axes:
        size = lax.axis_size(axis)
        if size & (size - 1):
            value = lax.psum(value, axis)
            continue
        stride = 1
        while stride < size:
            pairs = [(index, index ^ stride) for index in range(size)]
            value = value + lax.ppermute(value, axis, pairs)
            stride *= 2
    return value


def radix_sum(value, axes, radix=4):
    for axis in axes:
        size = lax.axis_size(axis)
        stride = 1
        while stride < size:
            width = radix if size % (stride * radix) == 0 else 2
            position = lax.axis_index(axis) // stride % width
            received = [value]
            for distance in range(1, width):
                pairs = []
                for index in range(size):
                    member = index // stride % width
                    partner = index + ((member ^ distance) - member) * stride
                    pairs.append((index, partner))
                received.append(lax.ppermute(value, axis, pairs))
            stacked = jnp.stack(received)
            ordered = [
                lax.dynamic_index_in_dim(stacked, position ^ member, 0, keepdims=False)
                for member in range(width)
            ]
            while len(ordered) > 1:
                ordered = [ordered[n] + ordered[n + 1] for n in range(0, len(ordered), 2)]
            value = ordered[0]
            stride *= width
    return value


def exchange_rounds(axes):
    rounds = []
    for axis in axes:
        size = lax.axis_size(axis)
        stride = 1
        while stride < size:
            rounds.append((axis, stride, size))
            stride *= 2
    return rounds


def halving_sum(value, axes):
    shape = value.shape
    flat = value.reshape(-1)
    done = []
    for axis, stride, size in exchange_rounds(axes):
        bit = lax.axis_index(axis) // stride % 2
        halves = flat.reshape(2, -1)
        keep = lax.dynamic_index_in_dim(halves, bit, 0, keepdims=False)
        give = lax.dynamic_index_in_dim(halves, 1 - bit, 0, keepdims=False)
        pairs = [(index, index ^ stride) for index in range(size)]
        flat = keep + lax.ppermute(give, axis, pairs)
        done.append((axis, stride, size, bit))
    for axis, stride, size, bit in reversed(done):
        pairs = [(index, index ^ stride) for index in range(size)]
        other = lax.ppermute(flat, axis, pairs)
        first = jnp.where(bit == 0, flat, other)
        second = jnp.where(bit == 0, other, flat)
        flat = jnp.concatenate([first, second])
    return flat.reshape(shape)


def inverse_factors(gram_blocks):
    factors = jnp.linalg.cholesky(gram_blocks)
    identity = jnp.broadcast_to(jnp.eye(gram_blocks.shape[1], dtype=gram_blocks.dtype), gram_blocks.shape)
    return jax.scipy.linalg.solve_triangular(factors, identity, lower=True)


def shards(probe_block, prior_blocks, self_relatedness, tile_values, tile_index):
    col_count = lax.axis_size("col")
    block_count = prior_blocks.shape[0] + 1
    depth = probe_block.shape[0]
    highest = lax.Precision.HIGHEST
    basis = jnp.concatenate([prior_blocks, probe_block[None]], axis=0)
    flat_basis = basis.reshape(block_count * depth, basis.shape[2])
    wide_basis = flat_basis.astype(jnp.float32)
    gram_local = jnp.dot(flat_basis, flat_basis.T, preferred_element_type=jnp.float32)
    pairs = [(b, e) for b in range(block_count) for e in range(b + 1)]
    lower_local = jnp.stack(
        [gram_local[b * depth:(b + 1) * depth, e * depth:(e + 1) * depth] for b, e in pairs]
    )
    lower = halving_sum(lower_local, ("col", "row"))
    row_probes = lax.all_gather(probe_block, "col", axis=1, tiled=True)
    col_probes = lax.all_gather(probe_block, "row", axis=1, tiled=True)
    lower, row_probes, col_probes = lax.optimization_barrier((lower, row_probes, col_probes))
    gram = {pair: lower[n] for n, pair in enumerate(pairs)}
    inverses = inverse_factors(jnp.stack([gram[(b, b)] for b in range(block_count)]))
    row_part, col_part = tile_products(tile_values, tile_index, row_probes, col_probes, col_count)
    row_total = sum_rows(row_part)
    col_total = sum_columns(col_part)
    row_total, col_total, inverses = lax.optimization_barrier((row_total, col_total, inverses))
    product = self_relatedness[None, :] * probe_block.astype(jnp.float32) + row_total + col_total
    along_local = jnp.dot(wide_basis, product.T, precision=highest)
    along = radix_sum(along_local, ("col", "row"))
    solved = []
    for block_number in range(block_count):
        target = along[block_number * depth:(block_number + 1) * depth]
        for earlier in range(block_number):
            target = target - jnp.dot(gram[(block_number, earlier)], solved[earlier], precision=highest)
        inverse = inverses[block_number]
        half = jnp.dot(inverse, target, precision=highest)
        solved.append(jnp.dot(inverse.T, half, precision=highest))
    coefficients = jnp.concatenate(solved, axis=0)
    current = product - jnp.dot(coefficients.T, wide_basis, precision=highest)
    return (current, jnp.stack(solved))


def solution(mesh):
    in_specs = (
        P(None, ("row", "col")),
        P(None, None, ("row", "col")),
        P(("row", "col")),
        P(("row", "col"), None, None),
        P(("row", "col"), None),
    )
    out_specs = (P(None, ("row", "col")), P())
    return jax.shard_map(shards, mesh=mesh, in_specs=in_specs, out_specs=out_specs, check_vma=False)
```

profile of v0, /device:TPU:8, one launch (start us, length us, event | category | flops | bytes accessed | tf_op | source)
XLA Modules:
  0.0 304.4 jit_solution(9586940039352297064)
XLA Ops:
  8.0 1.2 pad_maximum_fusion
  10.8 1.3 collective-permute-done
  12.3 2.0 collective-permute-start.1
  14.3 2.3 collective-permute-done.1
  16.9 3.4 %collective-permute-start.2 = (f32[7680]{0:T(1024)S(1)}, f32[7680]{0:T(1024)S(1)}, u32[]{:S(2)}, u32[]{:S(2)}) collective-permute-start(f32[7680]{0:T(1024)S(1)} %get-tuple-element.22), channel_id=1, source_target_pairs={{0,4},{1,5},{2,6},{3,7},{4,0},{5,1},{6,2},{7,3},{8,12},{9,13},{10,... | collective-permute-start | bytes 92168 | tf_op jit(solution)/shard_map/ppermute | solution.py:126
  20.2 1.9 collective-permute-done.2
  22.3 6.9 %collective-permute-start.3 = (f32[3840]{0:T(1024)S(1)}, f32[3840]{0:T(1024)S(1)}, u32[]{:S(2)}, u32[]{:S(2)}) collective-permute-start(f32[3840]{0:T(1024)S(1)} %get-tuple-element.24), channel_id=1, source_target_pairs={{0,8},{1,9},{2,10},{3,11},{4,12},{5,13},{6,14},{7,15},{8,0},{9,1},... | collective-permute-start | bytes 46088 | tf_op jit(solution)/shard_map/ppermute | solution.py:126
  29.2 1.7 collective-permute-done.3
  31.0 1.6 collective-permute-start.4
  32.6 2.2 collective-permute-done.4
  34.9 3.1 %collective-permute-start.5 = (f32[960]{0:T(1024)S(1)}, f32[960]{0:T(1024)S(1)}, u32[]{:S(2)}, u32[]{:S(2)}) collective-permute-start(f32[960]{0:T(1024)S(1)} %bitcast.340), channel_id=1, source_target_pairs={{0,32},{16,48},{32,0},{48,16},{64,96},{80,112},{96,64},{112,80},{1... | collective-permute-start | bytes 11528 | tf_op jit(solution)/shard_map/ppermute | solution.py:126
  38.0 2.1 collective-permute-done.5
  40.1 1.3 collective-permute-start.6
  41.5 2.3 collective-permute-done.6
  43.9 2.4 collective-permute-start.7
  46.3 2.8 collective-permute-done.7
  49.1 2.3 collective-permute-start.8
  51.4 2.8 collective-permute-done.8
  54.2 1.3 collective-permute-start.9
  55.5 2.3 collective-permute-done.9
  58.0 3.0 collective-permute-start.10
  61.0 2.1 collective-permute-done.10
  63.3 1.5 collective-permute-start.11
  64.9 2.1 collective-permute-done.11
  67.0 6.2 %collective-permute-start.12 = (f32[3840]{0:T(1024)S(1)}, f32[3840]{0:T(1024)S(1)}, u32[]{:S(2)}, u32[]{:S(2)}) collective-permute-start(f32[3840]{0:T(1024)S(1)} %pad_maximum_fusion.9), channel_id=1, source_target_pairs={{0,8},{1,9},{2,10},{3,11},{4,12},{5,13},{6,14},{7,15},{8,0},{9,1},... | collective-permute-start | bytes 46088 | tf_op jit(solution)/shard_map/ppermute | solution.py:130
  73.2 1.7 collective-permute-done.12
  74.9 2.0 collective-permute-start.13
  77.0 2.9 collective-permute-done.13
  81.0 3.2 %collective-permute-done.14 = f32[15360]{0:T(1024)S(1)} collective-permute-done((f32[15360]{0:T(1024)S(1)}, f32[15360]{0:T(1024)S(1)}, u32[]{:S(2)}, u32[]{:S(2)}) %collective-permute-start.14) | collective-permute-done | bytes 61472 | tf_op jit(solution)/shard_map/ppermute | solution.py:130
  110.9 5.1 %all-gather.5.cloned.1.call-done = bf16[64,16384]{1,0:T(8,128)(2,1)} async-done(((bf16[64,1024]{1,0:T(8,128)(2,1)}), bf16[64,16384]{1,0:T(8,128)(2,1)}) %all-gather.5.cloned.1.call-update) | async-done | bytes 2097168 | tf_op jit(solution)/shard_map/all_gather | solution.py:158
  116.0 2.6 fusion.6
  118.5 3.0 fusion.10
  121.5 2.4 fusion.14
  124.0 2.4 fusion.18
  126.4 2.2 fusion.4
  128.6 1.4 fusion.8
  130.0 1.4 fusion.12
  131.4 1.4 fusion.16
  132.8 2.2 add_dynamic-update-slice_fusion.15
  147.4 2.4 bitcast_dynamic-update-slice_fusion.15
  151.9 4.1 %collective-permute-done.16 = f32[8,64,1024]{2,1,0:T(8,128)S(1)} collective-permute-done((f32[8,64,1024]{2,1,0:T(8,128)S(1)}, f32[8,64,1024]{2,1,0:T(8,128)S(1)}, u32[]{:S(2)}, u32[]{:S(2)}) %collective-permute-start.16) | collective-permute-done | bytes 2097184 | tf_op jit(solution)/shard_map/ppermute | solution.py:55
  157.5 1.6 collective-permute-start.17
  163.7 19.3 %collective-permute-done.17 = f32[4,64,1024]{2,1,0:T(8,128)} collective-permute-done((f32[4,64,1024]{2,1,0:T(8,128)}, f32[4,64,1024]{2,1,0:T(8,128)}, u32[]{:S(2)}, u32[]{:S(2)}) %collective-permute-start.17) | collective-permute-done | bytes 1048608 | tf_op jit(solution)/shard_map/ppermute | solution.py:55
  183.0 1.4 bitcast_add_fusion.1
  185.5 2.8 collective-permute-start.18
  189.2 29.3 %custom-call.8 = f32[5,64,64]{2,1,0:T(8,128)S(1)} custom-call(f32[5,64,64]{2,1,0:T(8,128)S(1)} %fusion.32), custom_call_target="Cholesky" | custom-call | tf_op jit(solution)/shard_map/jit(cholesky)/cholesky | solution.py:138
  219.8 4.2 %collective-permute-start.19 = (f32[1,64,1024]{2,1,0:T(8,128)S(1)}, f32[1,64,1024]{2,1,0:T(8,128)S(1)}, u32[]{:S(2)}, u32[]{:S(2)}) collective-permute-start(f32[1,64,1024]{2,1,0:T(8,128)S(1)} %constant_dynamic-slice_fusion), channel_id=1, source_target_pairs={{0,8},{1,9},{2,10},{3,11},{4,12},{5,13},{6,14},{7,15},{8,0},{9,1},... | collective-permute-start | bytes 786440 | tf_op jit(solution)/shard_map/ppermute | solution.py:55
  224.2 24.6 %custom-call.9 = f32[5,1,64,64]{2,3,1,0:T(8,128)S(1)} custom-call(f32[5,1,64,64]{3,2,1,0:T(8,128)S(1)} %select_bitcast_fusion), custom_call_target="InvertDiagBlocksLowerTriangular" | custom-call | tf_op jit(solution)/shard_map/jit(_solve_triangular)/vmap()/triangular_solve | solution.py:140
  248.7 1.2 fusion.30
  250.0 1.7 fusion.94
  252.4 1.3 collective-permute-start.20
  253.7 2.7 collective-permute-done.22
  257.6 1.4 collective-permute-start.25
  259.0 4.3 %collective-permute-start.24 = (f32[320,64]{0,1:T(8,128)S(1)}, f32[320,64]{0,1:T(8,128)S(1)}, u32[]{:S(2)}, u32[]{:S(2)}) collective-permute-start(f32[320,64]{0,1:T(8,128)S(1)} %fusion.136), channel_id=1, source_target_pairs={{0,8},{1,9},{2,10},{3,11},{4,12},{5,13},{6,14},{7,15},{8,0},{9,1},... | collective-permute-start | bytes 245768 | tf_op jit(solution)/shard_map/ppermute | solution.py:92
  264.9 5.0 %collective-permute-done.24 = f32[320,64]{0,1:T(8,128)S(1)} collective-permute-done((f32[320,64]{0,1:T(8,128)S(1)}, f32[320,64]{0,1:T(8,128)S(1)}, u32[]{:S(2)}, u32[]{:S(2)}) %collective-permute-start.24) | collective-permute-done | bytes 81952 | tf_op jit(solution)/shard_map/ppermute | solution.py:92
  269.9 4.4 %collective-permute-done.23 = f32[320,64]{0,1:T(8,128)S(1)} collective-permute-done((f32[320,64]{0,1:T(8,128)S(1)}, f32[320,64]{0,1:T(8,128)S(1)}, u32[]{:S(2)}, u32[]{:S(2)}) %collective-permute-start.23) | collective-permute-done | bytes 81952 | tf_op jit(solution)/shard_map/ppermute | solution.py:92
  275.5 1.3 collective-permute-start.27
  276.9 1.7 collective-permute-start.26
  278.6 3.7 %collective-permute-done.28 = f32[320,64]{0,1:T(8,128)S(1)} collective-permute-done((f32[320,64]{0,1:T(8,128)S(1)}, f32[320,64]{0,1:T(8,128)S(1)}, u32[]{:S(2)}, u32[]{:S(2)}) %collective-permute-start.28) | collective-permute-done | bytes 81952 | tf_op jit(solution)/shard_map/ppermute | solution.py:92
  283.1 1.2 collective-permute-start.31
  284.3 2.6 collective-permute-start.30
  287.4 1.6 collective-permute-done.31
  288.9 1.5 collective-permute-done.30
  295.9 1.2 convolution_subtract_fusion
  (180 shorter events, 42.0 us)
Async XLA Ops:
  7.2 103.7 %all-gather.3.cloned.1.call-start = ((), (), s32[]{:S(2)}) async-start(), calls=%async_computation.1 | async-start | bytes 2228224 | tf_op jit(solution)/shard_map/all_gather | solution.py:157
  7.9 108.1 %all-gather.5.cloned.1.call-start = ((), (), s32[]{:S(2)}) async-start(), calls=%async_computation.2 | async-start | bytes 2228224 | tf_op jit(solution)/shard_map/all_gather | solution.py:158
  8.0 76.5 %copy-start.4 = (s32[5,3]{0,1:T(4,128)S(1)}, s32[5,3]{0,1:T(4,128)}, u32[]{:S(2)}) copy-start(s32[5,3]{0,1:T(4,128)} %param.9) | copy-start | bytes 184
  10.7 1.4 collective-permute-start
  12.3 4.3 %collective-permute-start.1 = (f32[15360]{0:T(1024)S(1)}, f32[15360]{0:T(1024)S(1)}, u32[]{:S(2)}, u32[]{:S(2)}) collective-permute-start(f32[15360]{0:T(1024)S(1)} %bitcast.337), channel_id=1, source_target_pairs={{0,2},{1,3},{2,0},{3,1},{4,6},{5,7},{6,4},{7,5},{8,10},{9,11},{10,... | collective-permute-start | bytes 184328 | tf_op jit(solution)/shard_map/ppermute | solution.py:126
  16.9 5.2 %collective-permute-start.2 = (f32[7680]{0:T(1024)S(1)}, f32[7680]{0:T(1024)S(1)}, u32[]{:S(2)}, u32[]{:S(2)}) collective-permute-start(f32[7680]{0:T(1024)S(1)} %get-tuple-element.22), channel_id=1, source_target_pairs={{0,4},{1,5},{2,6},{3,7},{4,0},{5,1},{6,2},{7,3},{8,12},{9,13},{10,... | collective-permute-start | bytes 92168 | tf_op jit(solution)/shard_map/ppermute | solution.py:126
  22.3 8.7 %collective-permute-start.3 = (f32[3840]{0:T(1024)S(1)}, f32[3840]{0:T(1024)S(1)}, u32[]{:S(2)}, u32[]{:S(2)}) collective-permute-start(f32[3840]{0:T(1024)S(1)} %get-tuple-element.24), channel_id=1, source_target_pairs={{0,8},{1,9},{2,10},{3,11},{4,12},{5,13},{6,14},{7,15},{8,0},{9,1},... | collective-permute-start | bytes 46088 | tf_op jit(solution)/shard_map/ppermute | solution.py:126
  31.0 3.7 %collective-permute-start.4 = (f32[1920]{0:T(1024)S(1)}, f32[1920]{0:T(1024)S(1)}, u32[]{:S(2)}, u32[]{:S(2)}) collective-permute-start(f32[1920]{0:T(1024)S(1)} %get-tuple-element.26), channel_id=1, source_target_pairs={{0,16},{16,0},{32,48},{48,32},{64,80},{80,64},{96,112},{112,96},{1... | collective-permute-start | bytes 23048 | tf_op jit(solution)/shard_map/ppermute | solution.py:126
  34.9 5.2 %collective-permute-start.5 = (f32[960]{0:T(1024)S(1)}, f32[960]{0:T(1024)S(1)}, u32[]{:S(2)}, u32[]{:S(2)}) collective-permute-start(f32[960]{0:T(1024)S(1)} %bitcast.340), channel_id=1, source_target_pairs={{0,32},{16,48},{32,0},{48,16},{64,96},{80,112},{96,64},{112,80},{1... | collective-permute-start | bytes 11528 | tf_op jit(solution)/shard_map/ppermute | solution.py:126
  40.1 3.7 %collective-permute-start.6 = (f32[480]{0:T(512)S(1)}, f32[480]{0:T(512)S(1)}, u32[]{:S(2)}, u32[]{:S(2)}) collective-permute-start(f32[480]{0:T(512)S(1)} %bitcast.342), channel_id=1, source_target_pairs={{0,64},{16,80},{32,96},{48,112},{64,0},{80,16},{96,32},{112,48},{1... | collective-permute-start | bytes 5768 | tf_op jit(solution)/shard_map/ppermute | solution.py:126
  43.9 5.2 %collective-permute-start.7 = (f32[240]{0:T(256)S(1)}, f32[240]{0:T(256)S(1)}, u32[]{:S(2)}, u32[]{:S(2)}) collective-permute-start(f32[240]{0:T(256)S(1)} %bitcast.343), channel_id=1, source_target_pairs={{0,128},{16,144},{32,160},{48,176},{64,192},{80,208},{96,224},{112... | collective-permute-start | bytes 2888 | tf_op jit(solution)/shard_map/ppermute | solution.py:126
  49.1 5.1 %collective-permute-start.8 = (f32[240]{0:T(256)S(1)}, f32[240]{0:T(256)S(1)}, u32[]{:S(2)}, u32[]{:S(2)}) collective-permute-start(f32[240]{0:T(256)S(1)} %add.759), channel_id=1, source_target_pairs={{0,128},{16,144},{32,160},{48,176},{64,192},{80,208},{96,224},{112... | collective-permute-start | bytes 2888 | tf_op jit(solution)/shard_map/ppermute | solution.py:130
  54.2 3.6 %collective-permute-start.9 = (f32[480]{0:T(512)S(1)}, f32[480]{0:T(512)S(1)}, u32[]{:S(2)}, u32[]{:S(2)}) collective-permute-start(f32[480]{0:T(512)S(1)} %pad_maximum_fusion.12), channel_id=1, source_target_pairs={{0,64},{16,80},{32,96},{48,112},{64,0},{80,16},{96,32},{112,48},{1... | collective-permute-start | bytes 5768 | tf_op jit(solution)/shard_map/ppermute | solution.py:130
  58.0 5.1 %collective-permute-start.10 = (f32[960]{0:T(1024)S(1)}, f32[960]{0:T(1024)S(1)}, u32[]{:S(2)}, u32[]{:S(2)}) collective-permute-start(f32[960]{0:T(1024)S(1)} %pad_maximum_fusion.11), channel_id=1, source_target_pairs={{0,32},{16,48},{32,0},{48,16},{64,96},{80,112},{96,64},{112,80},{1... | collective-permute-start | bytes 11528 | tf_op jit(solution)/shard_map/ppermute | solution.py:130
  63.3 3.7 %collective-permute-start.11 = (f32[1920]{0:T(1024)S(1)}, f32[1920]{0:T(1024)S(1)}, u32[]{:S(2)}, u32[]{:S(2)}) collective-permute-start(f32[1920]{0:T(1024)S(1)} %pad_maximum_fusion.10), channel_id=1, source_target_pairs={{0,16},{16,0},{32,48},{48,32},{64,80},{80,64},{96,112},{112,96},{1... | collective-permute-start | bytes 23048 | tf_op jit(solution)/shard_map/ppermute | solution.py:130
  64.8 185.2 %reduce-scatter.2.cloned.1.call-start = ((), (), s32[]{:S(2)}) async-start(), calls=%async_computation.3 | async-start | bytes 4456448 | tf_op jit(solution)/shard_map/reduce_scatter | solution.py:61
  67.0 7.9 %collective-permute-start.12 = (f32[3840]{0:T(1024)S(1)}, f32[3840]{0:T(1024)S(1)}, u32[]{:S(2)}, u32[]{:S(2)}) collective-permute-start(f32[3840]{0:T(1024)S(1)} %pad_maximum_fusion.9), channel_id=1, source_target_pairs={{0,8},{1,9},{2,10},{3,11},{4,12},{5,13},{6,14},{7,15},{8,0},{9,1},... | collective-permute-start | bytes 46088 | tf_op jit(solution)/shard_map/ppermute | solution.py:130
  74.9 4.9 %collective-permute-start.13 = (f32[7680]{0:T(1024)S(1)}, f32[7680]{0:T(1024)S(1)}, u32[]{:S(2)}, u32[]{:S(2)}) collective-permute-start(f32[7680]{0:T(1024)S(1)} %pad_maximum_fusion.8), channel_id=1, source_target_pairs={{0,4},{1,5},{2,6},{3,7},{4,0},{5,1},{6,2},{7,3},{8,12},{9,13},{10,... | collective-permute-start | bytes 92168 | tf_op jit(solution)/shard_map/ppermute | solution.py:130
  79.9 4.3 %collective-permute-start.14 = (f32[15360]{0:T(1024)S(1)}, f32[15360]{0:T(1024)S(1)}, u32[]{:S(2)}, u32[]{:S(2)}) collective-permute-start(f32[15360]{0:T(1024)S(1)} %pad_maximum_fusion.7), channel_id=1, source_target_pairs={{0,2},{1,3},{2,0},{3,1},{4,6},{5,7},{6,4},{7,5},{8,10},{9,11},{10,... | collective-permute-start | bytes 184328 | tf_op jit(solution)/shard_map/ppermute | solution.py:130
  84.2 26.4 %collective-permute-start.15 = (f32[30720]{0:T(1024)S(1)}, f32[30720]{0:T(1024)S(1)}, u32[]{:S(2)}, u32[]{:S(2)}) collective-permute-start(f32[30720]{0:T(1024)S(1)} %pad_maximum_fusion.6), channel_id=1, source_target_pairs={{0,1},{1,0},{2,3},{3,2},{4,5},{5,4},{6,7},{7,6},{8,9},{9,8},{10,11... | collective-permute-start | bytes 368648 | tf_op jit(solution)/shard_map/ppermute | solution.py:130
  116.0 12.6 %copy-start.2 = (bf16[5,1024,1024]{2,1,0:T(8,128)(2,1)S(1)}, bf16[5,1024,1024]{2,1,0:T(8,128)(2,1)}, u32[]{:S(2)}) copy-start(bf16[5,1024,1024]{2,1,0:T(8,128)(2,1)} %param.8) | copy-start | bytes 31457284
  151.8 4.2 %collective-permute-start.16 = (f32[8,64,1024]{2,1,0:T(8,128)S(1)}, f32[8,64,1024]{2,1,0:T(8,128)S(1)}, u32[]{:S(2)}, u32[]{:S(2)}) collective-permute-start(f32[8,64,1024]{2,1,0:T(8,128)S(1)} %dynamic-slice_bitcast_fusion), channel_id=1, source_target_pairs={{0,1},{1,0},{2,3},{3,2},{4,5},{5,4},{6,7},{7,6},{8,9},{9,8},{10,11... | collective-permute-start | bytes 6291464 | tf_op jit(solution)/shard_map/ppermute | solution.py:55
  157.5 25.5 %collective-permute-start.17 = (f32[4,64,1024]{2,1,0:T(8,128)}, f32[4,64,1024]{2,1,0:T(8,128)}, u32[]{:S(2)}, u32[]{:S(2)}) collective-permute-start(f32[4,64,1024]{2,1,0:T(8,128)} %dynamic-slice_bitcast_fusion.1), channel_id=1, source_target_pairs={{0,2},{1,3},{2,0},{3,1},{4,6},{5,7},{6,4},{7,5},{8,10},{9,11},{10,... | collective-permute-start | bytes 3145736 | tf_op jit(solution)/shard_map/ppermute | solution.py:55
  163.7 86.3 %copy-start.1 = (bf16[64,1024]{1,0:T(8,128)(2,1)S(1)}, bf16[64,1024]{1,0:T(8,128)(2,1)}, u32[]{:S(2)}) copy-start(bf16[64,1024]{1,0:T(8,128)(2,1)} %param.5) | copy-start | bytes 393220
  184.4 1.0 copy-start
  185.5 33.2 %collective-permute-start.18 = (f32[2,64,1024]{2,1,0:T(8,128)S(1)}, f32[2,64,1024]{2,1,0:T(8,128)S(1)}, u32[]{:S(2)}, u32[]{:S(2)}) collective-permute-start(f32[2,64,1024]{2,1,0:T(8,128)S(1)} %dynamic-slice_bitcast_fusion.2), channel_id=1, source_target_pairs={{0,4},{1,5},{2,6},{3,7},{4,0},{5,1},{6,2},{7,3},{8,12},{9,13},{10,... | collective-permute-start | bytes 1572872 | tf_op jit(solution)/shard_map/ppermute | solution.py:55
  219.8 30.1 %collective-permute-start.19 = (f32[1,64,1024]{2,1,0:T(8,128)S(1)}, f32[1,64,1024]{2,1,0:T(8,128)S(1)}, u32[]{:S(2)}, u32[]{:S(2)}) collective-permute-start(f32[1,64,1024]{2,1,0:T(8,128)S(1)} %constant_dynamic-slice_fusion), channel_id=1, source_target_pairs={{0,8},{1,9},{2,10},{3,11},{4,12},{5,13},{6,14},{7,15},{8,0},{9,1},... | collective-permute-start | bytes 786440 | tf_op jit(solution)/shard_map/ppermute | solution.py:55
  251.7 4.7 %collective-permute-start.22 = (f32[320,64]{0,1:T(8,128)S(1)}, f32[320,64]{0,1:T(8,128)S(1)}, u32[]{:S(2)}, u32[]{:S(2)}) collective-permute-start(f32[320,64]{0,1:T(8,128)S(1)} %fusion.94), channel_id=1, source_target_pairs={{0,3},{1,2},{2,1},{3,0},{4,7},{5,6},{6,5},{7,4},{8,11},{9,10},{10,... | collective-permute-start | bytes 245768 | tf_op jit(solution)/shard_map/ppermute | solution.py:92
  251.8 5.7 %collective-permute-start.21 = (f32[320,64]{0,1:T(8,128)S(1)}, f32[320,64]{0,1:T(8,128)S(1)}, u32[]{:S(2)}, u32[]{:S(2)}) collective-permute-start(f32[320,64]{0,1:T(8,128)S(1)} %fusion.94), channel_id=1, source_target_pairs={{0,2},{1,3},{2,0},{3,1},{4,6},{5,7},{6,4},{7,5},{8,10},{9,11},{10,... | collective-permute-start | bytes 245768 | tf_op jit(solution)/shard_map/ppermute | solution.py:92
  252.4 5.2 %collective-permute-start.20 = (f32[320,64]{0,1:T(8,128)S(1)}, f32[320,64]{0,1:T(8,128)S(1)}, u32[]{:S(2)}, u32[]{:S(2)}) collective-permute-start(f32[320,64]{0,1:T(8,128)S(1)} %fusion.94), channel_id=1, source_target_pairs={{0,1},{1,0},{2,3},{3,2},{4,5},{5,4},{6,7},{7,6},{8,9},{9,8},{10,11... | collective-permute-start | bytes 245768 | tf_op jit(solution)/shard_map/ppermute | solution.py:92
  257.6 38.3 %copy-start.3 = (f32[64,1024]{1,0:T(8,128)S(1)}, f32[64,1024]{1,0:T(8,128)}, u32[]{:S(2)}) copy-start(f32[64,1024]{1,0:T(8,128)} %reduce-scatter.2.cloned.1.call-done) | copy-start | bytes 786436
  257.6 38.3 %copy-start.5 = (f32[1024]{0:T(1024)S(1)}, f32[1024]{0:T(1024)}, u32[]{:S(2)}) copy-start(f32[1024]{0:T(1024)} %param.7) | copy-start | bytes 12292
  257.6 7.3 %collective-permute-start.25 = (f32[320,64]{0,1:T(8,128)S(1)}, f32[320,64]{0,1:T(8,128)S(1)}, u32[]{:S(2)}, u32[]{:S(2)}) collective-permute-start(f32[320,64]{0,1:T(8,128)S(1)} %fusion.136), channel_id=1, source_target_pairs={{0,12},{1,13},{2,14},{3,15},{4,8},{5,9},{6,10},{7,11},{8,4},{9,5},... | collective-permute-start | bytes 245768 | tf_op jit(solution)/shard_map/ppermute | solution.py:92
  259.0 10.9 %collective-permute-start.24 = (f32[320,64]{0,1:T(8,128)S(1)}, f32[320,64]{0,1:T(8,128)S(1)}, u32[]{:S(2)}, u32[]{:S(2)}) collective-permute-start(f32[320,64]{0,1:T(8,128)S(1)} %fusion.136), channel_id=1, source_target_pairs={{0,8},{1,9},{2,10},{3,11},{4,12},{5,13},{6,14},{7,15},{8,0},{9,1},... | collective-permute-start | bytes 245768 | tf_op jit(solution)/shard_map/ppermute | solution.py:92
  263.3 11.0 %collective-permute-start.23 = (f32[320,64]{0,1:T(8,128)S(1)}, f32[320,64]{0,1:T(8,128)S(1)}, u32[]{:S(2)}, u32[]{:S(2)}) collective-permute-start(f32[320,64]{0,1:T(8,128)S(1)} %fusion.136), channel_id=1, source_target_pairs={{0,4},{1,5},{2,6},{3,7},{4,0},{5,1},{6,2},{7,3},{8,12},{9,13},{10,... | collective-permute-start | bytes 245768 | tf_op jit(solution)/shard_map/ppermute | solution.py:92
  274.4 7.9 %collective-permute-start.28 = (f32[320,64]{0,1:T(8,128)S(1)}, f32[320,64]{0,1:T(8,128)S(1)}, u32[]{:S(2)}, u32[]{:S(2)}) collective-permute-start(f32[320,64]{0,1:T(8,128)S(1)} %fusion.135), channel_id=1, source_target_pairs={{0,48},{16,32},{32,16},{48,0},{64,112},{80,96},{96,80},{112,64},{1... | collective-permute-start | bytes 245768 | tf_op jit(solution)/shard_map/ppermute | solution.py:92
  275.5 7.0 %collective-permute-start.27 = (f32[320,64]{0,1:T(8,128)S(1)}, f32[320,64]{0,1:T(8,128)S(1)}, u32[]{:S(2)}, u32[]{:S(2)}) collective-permute-start(f32[320,64]{0,1:T(8,128)S(1)} %fusion.135), channel_id=1, source_target_pairs={{0,32},{16,48},{32,0},{48,16},{64,96},{80,112},{96,64},{112,80},{1... | collective-permute-start | bytes 245768 | tf_op jit(solution)/shard_map/ppermute | solution.py:92
  276.9 6.2 %collective-permute-start.26 = (f32[320,64]{0,1:T(8,128)S(1)}, f32[320,64]{0,1:T(8,128)S(1)}, u32[]{:S(2)}, u32[]{:S(2)}) collective-permute-start(f32[320,64]{0,1:T(8,128)S(1)} %fusion.135), channel_id=1, source_target_pairs={{0,16},{16,0},{32,48},{48,32},{64,80},{80,64},{96,112},{112,96},{1... | collective-permute-start | bytes 245768 | tf_op jit(solution)/shard_map/ppermute | solution.py:92
  283.1 5.8 %collective-permute-start.31 = (f32[320,64]{0,1:T(8,128)S(1)}, f32[320,64]{0,1:T(8,128)S(1)}, u32[]{:S(2)}, u32[]{:S(2)}) collective-permute-start(f32[320,64]{0,1:T(8,128)S(1)} %fusion.134), channel_id=1, source_target_pairs={{0,192},{16,208},{32,224},{48,240},{64,128},{80,144},{96,160},{112... | collective-permute-start | bytes 245768 | tf_op jit(solution)/shard_map/ppermute | solution.py:92
  284.3 6.1 %collective-permute-start.30 = (f32[320,64]{0,1:T(8,128)S(1)}, f32[320,64]{0,1:T(8,128)S(1)}, u32[]{:S(2)}, u32[]{:S(2)}) collective-permute-start(f32[320,64]{0,1:T(8,128)S(1)} %fusion.134), channel_id=1, source_target_pairs={{0,128},{16,144},{32,160},{48,176},{64,192},{80,208},{96,224},{112... | collective-permute-start | bytes 245768 | tf_op jit(solution)/shard_map/ppermute | solution.py:92
  286.9 4.6 %collective-permute-start.29 = (f32[320,64]{0,1:T(8,128)S(1)}, f32[320,64]{0,1:T(8,128)S(1)}, u32[]{:S(2)}, u32[]{:S(2)}) collective-permute-start(f32[320,64]{0,1:T(8,128)S(1)} %fusion.134), channel_id=1, source_target_pairs={{0,64},{16,80},{32,96},{48,112},{64,0},{80,16},{96,32},{112,48},{1... | collective-permute-start | bytes 245768 | tf_op jit(solution)/shard_map/ppermute | solution.py:92
Sparse Core Ops, SparseCore 0:
  9.8 42.6 all-gather.2
  64.9 51.0 all-gather.4
  147.5 82.2 reduce-scatter.1
where the time goes:
time: 306 us; the launch traced here: 304 us
  waiting for transfers between devices  85.6 us (28%)
  other arithmetic  73.9 us (24%)
  starting transfers between devices  64.1 us (21%)
  between operations  40 us (13%)
  matrix products  30 us (10%)
  local copies, waits for them, and re-layouts  10.8 us (4%)
    another operation x4, other arithmetic, inverse_factors(): factors = jnp.linalg.cholesky(gram_blocks)  29.5 us
    another operation x3, other arithmetic, inverse_factors(): return jax.scipy.linalg.solve_triangular(factors, identity, lower=True)  24.7 us
    ppermute x4, waiting for transfers between devices, sum_rows(): row_part = keep + lax.ppermute(give, 'col', pairs)  23.4 us
    ppermute x12, waiting for transfers between devices, radix_sum(): received.append(lax.ppermute(value, axis, pairs))  22.6 us
    ppermute x8, starting transfers between devices, halving_sum(): flat = keep + lax.ppermute(give, axis, pairs)  20.7 us
    ppermute x8, starting transfers between devices, halving_sum(): other = lax.ppermute(flat, axis, pairs)  17.7 us
    ppermute x8, waiting for transfers between devices, halving_sum(): other = lax.ppermute(flat, axis, pairs)  17.1 us
    ppermute x12, starting transfers between devices, radix_sum(): received.append(lax.ppermute(value, axis, pairs))  16.9 us
  transfers between devices with their start and end apart: 35, of which 29 were waited for; matrix products, arithmetic and copies ran while one was open for 24% of the time, Pallas kernels for 0%

commit v1 on v0

--- a/solution.py
+++ b/solution.py
@@ -7,14 +7,14 @@
 def tile_products(tile_values, tile_index, row_probes, col_probes, col_count):
     tile_width = tile_values.shape[1]
     row_spans = row_probes.shape[1] // tile_width
-    col_spans = col_probes.shape[1] // tile_width
+    col_spans = col_probes.shape[0]
     forwards, mirrors, row_spans_of, col_spans_of = [], [], [], []
     for slot_index in range(tile_values.shape[0]):
         current_tile = tile_values[slot_index]
         live = tile_index[slot_index, 2] > 0
         row_span = tile_index[slot_index, 0] % col_count
         col_span = tile_index[slot_index, 1] // col_count
-        right = lax.dynamic_slice_in_dim(col_probes, col_span * tile_width, tile_width, 1)
+        right = lax.dynamic_index_in_dim(col_probes, col_span, 0, keepdims=False)
         left = lax.dynamic_slice_in_dim(row_probes, row_span * tile_width, tile_width, 1)
         forward = lax.dot_general(
             right, current_tile, (((1,), (1,)), ((), ())), preferred_element_type=jnp.float32
@@ -55,6 +55,21 @@
         row_part = keep + lax.ppermute(give, "col", pairs)
         stride *= 2
     return row_part[0]
+
+
+def gather_spans(block, axis):
+    size = lax.axis_size(axis)
+    if size & (size - 1):
+        return lax.all_gather(block, axis, axis=0, tiled=False)
+    spans = block[None]
+    stride = 1
+    while stride < size:
+        bit = lax.axis_index(axis) // stride % 2
+        pairs = [(index, index ^ stride) for index in range(size)]
+        other = lax.ppermute(spans, axis, pairs)
+        spans = jnp.where(bit == 0, jnp.concatenate([spans, other]), jnp.concatenate([other, spans]))
+        stride *= 2
+    return spans
 
 
 def sum_columns(col_part):
@@ -155,7 +170,7 @@
     )
     lower = halving_sum(lower_local, ("col", "row"))
     row_probes = lax.all_gather(probe_block, "col", axis=1, tiled=True)
-    col_probes = lax.all_gather(probe_block, "row", axis=1, tiled=True)
+    col_probes = gather_spans(probe_block, "row")
     lower, row_probes, col_probes = lax.optimization_barrier((lower, row_probes, col_probes))
     gram = {pair: lower[n] for n, pair in enumerate(pairs)}
     inverses = inverse_factors(jnp.stack([gram[(b, b)] for b in range(block_count)]))

time: 306 us -> 343 us (1.12); the launches traced: 304 us -> 338 us
  waiting for transfers between devices: 85.6 us -> 99.7 us
  starting transfers between devices: 64.1 us -> 76.8 us
    ppermute x0 -> x4, waiting for transfers between devices: none -> 28.6 us  [gather_spans(): other = lax.ppermute(spans, axis, pairs)]
    ppermute x8, waiting for transfers between devices: 17.1 us -> 6.97 us  [halving_sum(): other = lax.ppermute(flat, axis, pairs)]
    ppermute x0 -> x4, starting transfers between devices: none -> 8.79 us  [gather_spans(): other = lax.ppermute(spans, axis, pairs)]
    all_gather x1 -> x0, waiting for transfers between devices: 5.08 us -> none  [shards(): col_probes = lax.all_gather(probe_block, 'row', axis=1, tiled=True)]
    ppermute x4, starting transfers between devices: 8.71 us -> 12.3 us  [sum_rows(): row_part = keep + lax.ppermute(give, 'col', pairs)]
  transfers between devices with their start and end apart: 35 -> 38, of which waited for: 29 -> 26; matrix products, arithmetic and copies ran while one was open for 24% -> 22% of each run, Pallas kernels for 0% -> 0%
where the time goes in v1:
time: 343 us; the launch traced here: 338 us
  waiting for transfers between devices  99.7 us (29%)
  starting transfers between devices  76.8 us (22%)
  other arithmetic  76.5 us (22%)
  between operations  40.5 us (12%)
  matrix products  32.3 us (9%)
  local copies, waits for them, and re-layouts  11.7 us (3%)
    another operation x4, other arithmetic, inverse_factors(): factors = jnp.linalg.cholesky(gram_blocks)  29.5 us
    ppermute x4, waiting for transfers between devices, gather_spans(): other = lax.ppermute(spans, axis, pairs)  28.6 us
    another operation x3, other arithmetic, inverse_factors(): return jax.scipy.linalg.solve_triangular(factors, identity, lower=True)  24.7 us
    ppermute x4, waiting for transfers between devices, sum_rows(): row_part = keep + lax.ppermute(give, 'col', pairs)  24 us
    ppermute x12, waiting for transfers between devices, radix_sum(): received.append(lax.ppermute(value, axis, pairs))  23.6 us
    ppermute x8, starting transfers between devices, halving_sum(): flat = keep + lax.ppermute(give, axis, pairs)  20.8 us
    ppermute x12, starting transfers between devices, radix_sum(): received.append(lax.ppermute(value, axis, pairs))  17.7 us
    ppermute x8, starting transfers between devices, halving_sum(): other = lax.ppermute(flat, axis, pairs)  17.1 us
  transfers between devices with their start and end apart: 38, of which 26 were waited for; matrix products, arithmetic and copies ran while one was open for 22% of the time, Pallas kernels for 0%

profile of v1, /device:TPU:8, one launch (start us, length us, event | category | flops | bytes accessed | tf_op | source)
XLA Modules:
  0.0 337.6 jit_solution(10631632753681167327)
XLA Ops:
  7.2 1.2 pad_maximum_fusion
  10.1 1.3 collective-permute-done
  11.6 2.0 collective-permute-start.1
  13.6 2.3 collective-permute-done.1
  16.2 3.4 collective-permute-start.2
  19.5 1.9 collective-permute-done.2
  21.5 6.9 %collective-permute-start.3 = (f32[3840]{0:T(1024)S(1)}, f32[3840]{0:T(1024)S(1)}, u32[]{:S(2)}, u32[]{:S(2)}) collective-permute-start(f32[3840]{0:T(1024)S(1)} %get-tuple-element.24), channel_id=1, source_target_pairs={{0,8},{1,9},{2,10},{3,11},{4,12},{5,13},{6,14},{7,15},{8,0},{9,1},... | collective-permute-start | bytes 46088 | tf_op jit(solution)/shard_map/ppermute | solution.py:141
  28.5 1.7 collective-permute-done.3
  30.3 1.6 collective-permute-start.4
  31.8 2.2 collective-permute-done.4
  34.1 3.1 collective-permute-start.5
  37.2 2.1 collective-permute-done.5
  39.4 1.3 collective-permute-start.6
  40.7 2.3 collective-permute-done.6
  43.2 2.4 collective-permute-start.7
  45.5 2.8 collective-permute-done.7
  48.3 2.3 collective-permute-start.8
  50.6 2.8 collective-permute-done.8
  53.5 1.3 collective-permute-start.9
  54.7 2.3 collective-permute-done.9
  57.2 3.0 collective-permute-start.10
  61.0 1.3 collective-permute-done.10
  62.5 1.5 collective-permute-start.11
  75.1 6.0 %collective-permute-start.12 = (f32[3840]{0:T(1024)S(1)}, f32[3840]{0:T(1024)S(1)}, u32[]{:S(2)}, u32[]{:S(2)}) collective-permute-start(f32[3840]{0:T(1024)S(1)} %pad_maximum_fusion.9), channel_id=1, source_target_pairs={{0,8},{1,9},{2,10},{3,11},{4,12},{5,13},{6,14},{7,15},{8,0},{9,1},... | collective-permute-start | bytes 46088 | tf_op jit(solution)/shard_map/ppermute | solution.py:145
  96.4 1.6 collective-permute-start.13
  97.9 2.8 collective-permute-start.17
  101.3 1.3 collective-permute-start.14
  102.6 3.3 collective-permute-done.17
  106.7 11.3 %collective-permute-done.18 = bf16[4,64,1024]{2,1,0:T(8,128)(2,1)S(1)} collective-permute-done((bf16[4,64,1024]{2,1,0:T(8,128)(2,1)S(1)}, bf16[4,64,1024]{2,1,0:T(8,128)(2,1)S(1)}, u32[]{:S(2)}, u32[]{:S(2)}) %collective-permute-start.18) | collective-permute-done | bytes 524320 | tf_op jit(solution)/shard_map/ppermute | solution.py:69
  118.2 4.8 %collective-permute-start.19 = (bf16[8,64,1024]{2,1,0:T(8,128)(2,1)S(1)}, bf16[8,64,1024]{2,1,0:T(8,128)(2,1)S(1)}, u32[]{:S(2)}, u32[]{:S(2)}) collective-permute-start(bf16[8,64,1024]{2,1,0:T(8,128)(2,1)S(1)} %maximum_select_fusion.1), channel_id=1, source_target_pairs={{0,128},{16,144},{32,160},{48,176},{64,192},{80,208},{96,224},{112... | collective-permute-start | bytes 3145736 | tf_op jit(solution)/shard_map/ppermute | solution.py:69
  124.8 14.0 %collective-permute-done.19 = bf16[8,64,1024]{2,1,0:T(8,128)(2,1)S(1)} collective-permute-done((bf16[8,64,1024]{2,1,0:T(8,128)(2,1)S(1)}, bf16[8,64,1024]{2,1,0:T(8,128)(2,1)S(1)}, u32[]{:S(2)}, u32[]{:S(2)}) %collective-permute-start.19) | collective-permute-done | bytes 1048608 | tf_op jit(solution)/shard_map/ppermute | solution.py:69
  138.7 1.7 maximum_select_fusion
  140.5 2.4 fusion.6
  142.9 2.4 fusion.10
  145.3 2.4 fusion.14
  147.8 2.4 fusion.18
  150.2 2.2 fusion.4
  152.3 2.2 fusion.8
  154.5 2.2 fusion.12
  156.7 2.2 fusion.16
  158.8 2.9 add_dynamic-update-slice_fusion.15
  174.2 2.4 bitcast_dynamic-update-slice_fusion.15
  178.7 4.1 %collective-permute-done.20 = f32[8,64,1024]{2,1,0:T(8,128)S(1)} collective-permute-done((f32[8,64,1024]{2,1,0:T(8,128)S(1)}, f32[8,64,1024]{2,1,0:T(8,128)S(1)}, u32[]{:S(2)}, u32[]{:S(2)}) %collective-permute-start.20) | collective-permute-done | bytes 2097184 | tf_op jit(solution)/shard_map/ppermute | solution.py:55
  184.3 10.6 %collective-permute-start.21 = (f32[4,64,1024]{2,1,0:T(8,128)}, f32[4,64,1024]{2,1,0:T(8,128)}, u32[]{:S(2)}, u32[]{:S(2)}) collective-permute-start(f32[4,64,1024]{2,1,0:T(8,128)} %dynamic-slice_bitcast_fusion.1), channel_id=1, source_target_pairs={{0,2},{1,3},{2,0},{3,1},{4,6},{5,7},{6,4},{7,5},{8,10},{9,11},{10,... | collective-permute-start | bytes 3145736 | tf_op jit(solution)/shard_map/ppermute | solution.py:55
  199.5 19.8 %collective-permute-done.21 = f32[4,64,1024]{2,1,0:T(8,128)} collective-permute-done((f32[4,64,1024]{2,1,0:T(8,128)}, f32[4,64,1024]{2,1,0:T(8,128)}, u32[]{:S(2)}, u32[]{:S(2)}) %collective-permute-start.21) | collective-permute-done | bytes 1048608 | tf_op jit(solution)/shard_map/ppermute | solution.py:55
  219.3 1.4 bitcast_add_fusion.1
  221.7 1.6 collective-permute-start.22
  224.2 29.3 %custom-call.8 = f32[5,64,64]{2,1,0:T(8,128)S(1)} custom-call(f32[5,64,64]{2,1,0:T(8,128)S(1)} %fusion.32), custom_call_target="Cholesky" | custom-call | tf_op jit(solution)/shard_map/jit(cholesky)/cholesky | solution.py:153
  255.0 24.6 %custom-call.9 = f32[5,1,64,64]{2,3,1,0:T(8,128)S(1)} custom-call(f32[5,1,64,64]{3,2,1,0:T(8,128)S(1)} %select_bitcast_fusion), custom_call_target="InvertDiagBlocksLowerTriangular" | custom-call | tf_op jit(solution)/shard_map/jit(_solve_triangular)/vmap()/triangular_solve | solution.py:155
  279.6 1.2 fusion.30
  280.9 1.7 fusion.99
  284.5 3.1 collective-permute-done.26
  287.7 1.5 collective-permute-done.25
  289.3 5.0 %collective-permute-start.29 = (f32[320,64]{0,1:T(8,128)S(1)}, f32[320,64]{0,1:T(8,128)S(1)}, u32[]{:S(2)}, u32[]{:S(2)}) collective-permute-start(f32[320,64]{0,1:T(8,128)S(1)} %fusion.141), channel_id=1, source_target_pairs={{0,12},{1,13},{2,14},{3,15},{4,8},{5,9},{6,10},{7,11},{8,4},{9,5},... | collective-permute-start | bytes 245768 | tf_op jit(solution)/shard_map/ppermute | solution.py:107
  294.3 1.6 collective-permute-start.28
  296.8 6.3 %collective-permute-done.29 = f32[320,64]{0,1:T(8,128)S(1)} collective-permute-done((f32[320,64]{0,1:T(8,128)S(1)}, f32[320,64]{0,1:T(8,128)S(1)}, u32[]{:S(2)}, u32[]{:S(2)}) %collective-permute-start.29) | collective-permute-done | bytes 81952 | tf_op jit(solution)/shard_map/ppermute | solution.py:107
  303.0 3.8 %collective-permute-done.28 = f32[320,64]{0,1:T(8,128)S(1)} collective-permute-done((f32[320,64]{0,1:T(8,128)S(1)}, f32[320,64]{0,1:T(8,128)S(1)}, u32[]{:S(2)}, u32[]{:S(2)}) %collective-permute-start.28) | collective-permute-done | bytes 81952 | tf_op jit(solution)/shard_map/ppermute | solution.py:107
  306.9 2.4 collective-permute-start.32
  311.1 1.7 collective-permute-done.32
  312.8 2.6 collective-permute-done.31
  315.9 3.7 %collective-permute-start.34 = (f32[320,64]{0,1:T(8,128)S(1)}, f32[320,64]{0,1:T(8,128)S(1)}, u32[]{:S(2)}, u32[]{:S(2)}) collective-permute-start(f32[320,64]{0,1:T(8,128)S(1)} %fusion.139), channel_id=1, source_target_pairs={{0,128},{16,144},{32,160},{48,176},{64,192},{80,208},{96,224},{112... | collective-permute-start | bytes 245768 | tf_op jit(solution)/shard_map/ppermute | solution.py:107
  320.2 2.0 collective-permute-done.34
  322.2 2.0 collective-permute-done.33
  328.5 1.2 convolution_subtract_fusion
  (187 shorter events, 42.4 us)
Async XLA Ops:
  7.2 53.2 %copy-start.1 = (bf16[64,1024]{1,0:T(8,128)(2,1)S(1)}, bf16[64,1024]{1,0:T(8,128)(2,1)}, u32[]{:S(2)}) copy-start(bf16[64,1024]{1,0:T(8,128)(2,1)} %param.5) | copy-start | bytes 393220
  7.2 56.9 %copy-start.3 = (s32[5,3]{0,1:T(4,128)S(1)}, s32[5,3]{0,1:T(4,128)}, u32[]{:S(2)}) copy-start(s32[5,3]{0,1:T(4,128)} %param.9) | copy-start | bytes 184
  7.2 133.3 %all-gather.2.cloned.1.call-start = ((), (), s32[]{:S(2)}) async-start(), calls=%async_computation.1 | async-start | bytes 2228224 | tf_op jit(solution)/shard_map/all_gather | solution.py:172
  10.0 1.4 collective-permute-start
  11.6 4.3 %collective-permute-start.1 = (f32[15360]{0:T(1024)S(1)}, f32[15360]{0:T(1024)S(1)}, u32[]{:S(2)}, u32[]{:S(2)}) collective-permute-start(f32[15360]{0:T(1024)S(1)} %bitcast.356), channel_id=1, source_target_pairs={{0,2},{1,3},{2,0},{3,1},{4,6},{5,7},{6,4},{7,5},{8,10},{9,11},{10,... | collective-permute-start | bytes 184328 | tf_op jit(solution)/shard_map/ppermute | solution.py:141
  16.2 5.2 %collective-permute-start.2 = (f32[7680]{0:T(1024)S(1)}, f32[7680]{0:T(1024)S(1)}, u32[]{:S(2)}, u32[]{:S(2)}) collective-permute-start(f32[7680]{0:T(1024)S(1)} %get-tuple-element.22), channel_id=1, source_target_pairs={{0,4},{1,5},{2,6},{3,7},{4,0},{5,1},{6,2},{7,3},{8,12},{9,13},{10,... | collective-permute-start | bytes 92168 | tf_op jit(solution)/shard_map/ppermute | solution.py:141
  21.5 8.6 %collective-permute-start.3 = (f32[3840]{0:T(1024)S(1)}, f32[3840]{0:T(1024)S(1)}, u32[]{:S(2)}, u32[]{:S(2)}) collective-permute-start(f32[3840]{0:T(1024)S(1)} %get-tuple-element.24), channel_id=1, source_target_pairs={{0,8},{1,9},{2,10},{3,11},{4,12},{5,13},{6,14},{7,15},{8,0},{9,1},... | collective-permute-start | bytes 46088 | tf_op jit(solution)/shard_map/ppermute | solution.py:141
  30.3 3.7 %collective-permute-start.4 = (f32[1920]{0:T(1024)S(1)}, f32[1920]{0:T(1024)S(1)}, u32[]{:S(2)}, u32[]{:S(2)}) collective-permute-start(f32[1920]{0:T(1024)S(1)} %get-tuple-element.26), channel_id=1, source_target_pairs={{0,16},{16,0},{32,48},{48,32},{64,80},{80,64},{96,112},{112,96},{1... | collective-permute-start | bytes 23048 | tf_op jit(solution)/shard_map/ppermute | solution.py:141
  34.1 5.2 %collective-permute-start.5 = (f32[960]{0:T(1024)S(1)}, f32[960]{0:T(1024)S(1)}, u32[]{:S(2)}, u32[]{:S(2)}) collective-permute-start(f32[960]{0:T(1024)S(1)} %bitcast.359), channel_id=1, source_target_pairs={{0,32},{16,48},{32,0},{48,16},{64,96},{80,112},{96,64},{112,80},{1... | collective-permute-start | bytes 11528 | tf_op jit(solution)/shard_map/ppermute | solution.py:141
  39.4 3.7 %collective-permute-start.6 = (f32[480]{0:T(512)S(1)}, f32[480]{0:T(512)S(1)}, u32[]{:S(2)}, u32[]{:S(2)}) collective-permute-start(f32[480]{0:T(512)S(1)} %bitcast.361), channel_id=1, source_target_pairs={{0,64},{16,80},{32,96},{48,112},{64,0},{80,16},{96,32},{112,48},{1... | collective-permute-start | bytes 5768 | tf_op jit(solution)/shard_map/ppermute | solution.py:141
  43.2 5.2 %collective-permute-start.7 = (f32[240]{0:T(256)S(1)}, f32[240]{0:T(256)S(1)}, u32[]{:S(2)}, u32[]{:S(2)}) collective-permute-start(f32[240]{0:T(256)S(1)} %bitcast.362), channel_id=1, source_target_pairs={{0,128},{16,144},{32,160},{48,176},{64,192},{80,208},{96,224},{112... | collective-permute-start | bytes 2888 | tf_op jit(solution)/shard_map/ppermute | solution.py:141
  48.3 5.1 %collective-permute-start.8 = (f32[240]{0:T(256)S(1)}, f32[240]{0:T(256)S(1)}, u32[]{:S(2)}, u32[]{:S(2)}) collective-permute-start(f32[240]{0:T(256)S(1)} %add.764), channel_id=1, source_target_pairs={{0,128},{16,144},{32,160},{48,176},{64,192},{80,208},{96,224},{112... | collective-permute-start | bytes 2888 | tf_op jit(solution)/shard_map/ppermute | solution.py:145
  53.5 3.6 %collective-permute-start.9 = (f32[480]{0:T(512)S(1)}, f32[480]{0:T(512)S(1)}, u32[]{:S(2)}, u32[]{:S(2)}) collective-permute-start(f32[480]{0:T(512)S(1)} %pad_maximum_fusion.12), channel_id=1, source_target_pairs={{0,64},{16,80},{32,96},{48,112},{64,0},{80,16},{96,32},{112,48},{1... | collective-permute-start | bytes 5768 | tf_op jit(solution)/shard_map/ppermute | solution.py:145
  57.2 5.1 %collective-permute-start.10 = (f32[960]{0:T(1024)S(1)}, f32[960]{0:T(1024)S(1)}, u32[]{:S(2)}, u32[]{:S(2)}) collective-permute-start(f32[960]{0:T(1024)S(1)} %pad_maximum_fusion.11), channel_id=1, source_target_pairs={{0,32},{16,48},{32,0},{48,16},{64,96},{80,112},{96,64},{112,80},{1... | collective-permute-start | bytes 11528 | tf_op jit(solution)/shard_map/ppermute | solution.py:145
  60.3 220.6 %reduce-scatter.2.cloned.1.call-start = ((), (), s32[]{:S(2)}) async-start(), calls=%async_computation.2 | async-start | bytes 4456448 | tf_op jit(solution)/shard_map/reduce_scatter | solution.py:76
  60.4 37.5 %collective-permute-start.16 = (bf16[1,64,1024]{2,1,0:T(8,128)(2,1)S(1)}, bf16[1,64,1024]{2,1,0:T(8,128)(2,1)S(1)}, u32[]{:S(2)}, u32[]{:S(2)}) collective-permute-start(bf16[1,64,1024]{2,1,0:T(8,128)(2,1)S(1)} %bitcast.338), channel_id=1, source_target_pairs={{0,16},{16,0},{32,48},{48,32},{64,80},{80,64},{96,112},{112,96},{1... | collective-permute-start | bytes 393224 | tf_op jit(solution)/shard_map/ppermute | solution.py:69
  62.5 12.5 %collective-permute-start.11 = (f32[1920]{0:T(1024)S(1)}, f32[1920]{0:T(1024)S(1)}, u32[]{:S(2)}, u32[]{:S(2)}) collective-permute-start(f32[1920]{0:T(1024)S(1)} %pad_maximum_fusion.10), channel_id=1, source_target_pairs={{0,16},{16,0},{32,48},{48,32},{64,80},{80,64},{96,112},{112,96},{1... | collective-permute-start | bytes 23048 | tf_op jit(solution)/shard_map/ppermute | solution.py:145
  75.1 21.2 %collective-permute-start.12 = (f32[3840]{0:T(1024)S(1)}, f32[3840]{0:T(1024)S(1)}, u32[]{:S(2)}, u32[]{:S(2)}) collective-permute-start(f32[3840]{0:T(1024)S(1)} %pad_maximum_fusion.9), channel_id=1, source_target_pairs={{0,8},{1,9},{2,10},{3,11},{4,12},{5,13},{6,14},{7,15},{8,0},{9,1},... | collective-permute-start | bytes 46088 | tf_op jit(solution)/shard_map/ppermute | solution.py:145
  96.4 4.9 %collective-permute-start.13 = (f32[7680]{0:T(1024)S(1)}, f32[7680]{0:T(1024)S(1)}, u32[]{:S(2)}, u32[]{:S(2)}) collective-permute-start(f32[7680]{0:T(1024)S(1)} %pad_maximum_fusion.8), channel_id=1, source_target_pairs={{0,4},{1,5},{2,6},{3,7},{4,0},{5,1},{6,2},{7,3},{8,12},{9,13},{10,... | collective-permute-start | bytes 92168 | tf_op jit(solution)/shard_map/ppermute | solution.py:145
  97.9 8.0 %collective-permute-start.17 = (bf16[2,64,1024]{2,1,0:T(8,128)(2,1)S(1)}, bf16[2,64,1024]{2,1,0:T(8,128)(2,1)S(1)}, u32[]{:S(2)}, u32[]{:S(2)}) collective-permute-start(bf16[2,64,1024]{2,1,0:T(8,128)(2,1)S(1)} %maximum_select_fusion.3), channel_id=1, source_target_pairs={{0,32},{16,48},{32,0},{48,16},{64,96},{80,112},{96,64},{112,80},{1... | collective-permute-start | bytes 786440 | tf_op jit(solution)/shard_map/ppermute | solution.py:69
  101.3 5.2 %collective-permute-start.14 = (f32[15360]{0:T(1024)S(1)}, f32[15360]{0:T(1024)S(1)}, u32[]{:S(2)}, u32[]{:S(2)}) collective-permute-start(f32[15360]{0:T(1024)S(1)} %pad_maximum_fusion.7), channel_id=1, source_target_pairs={{0,2},{1,3},{2,0},{3,1},{4,6},{5,7},{6,4},{7,5},{8,10},{9,11},{10,... | collective-permute-start | bytes 184328 | tf_op jit(solution)/shard_map/ppermute | solution.py:145
  106.0 12.0 %collective-permute-start.18 = (bf16[4,64,1024]{2,1,0:T(8,128)(2,1)S(1)}, bf16[4,64,1024]{2,1,0:T(8,128)(2,1)S(1)}, u32[]{:S(2)}, u32[]{:S(2)}) collective-permute-start(bf16[4,64,1024]{2,1,0:T(8,128)(2,1)S(1)} %maximum_select_fusion.2), channel_id=1, source_target_pairs={{0,64},{16,80},{32,96},{48,112},{64,0},{80,16},{96,32},{112,48},{1... | collective-permute-start | bytes 1572872 | tf_op jit(solution)/shard_map/ppermute | solution.py:69
  106.6 16.4 %collective-permute-start.15 = (f32[30720]{0:T(1024)S(1)}, f32[30720]{0:T(1024)S(1)}, u32[]{:S(2)}, u32[]{:S(2)}) collective-permute-start(f32[30720]{0:T(1024)S(1)} %pad_maximum_fusion.6), channel_id=1, source_target_pairs={{0,1},{1,0},{2,3},{3,2},{4,5},{5,4},{6,7},{7,6},{8,9},{9,8},{10,11... | collective-permute-start | bytes 368648 | tf_op jit(solution)/shard_map/ppermute | solution.py:145
  118.2 20.6 %collective-permute-start.19 = (bf16[8,64,1024]{2,1,0:T(8,128)(2,1)S(1)}, bf16[8,64,1024]{2,1,0:T(8,128)(2,1)S(1)}, u32[]{:S(2)}, u32[]{:S(2)}) collective-permute-start(bf16[8,64,1024]{2,1,0:T(8,128)(2,1)S(1)} %maximum_select_fusion.1), channel_id=1, source_target_pairs={{0,128},{16,144},{32,160},{48,176},{64,192},{80,208},{96,224},{112... | collective-permute-start | bytes 3145736 | tf_op jit(solution)/shard_map/ppermute | solution.py:69
  178.6 4.2 %collective-permute-start.20 = (f32[8,64,1024]{2,1,0:T(8,128)S(1)}, f32[8,64,1024]{2,1,0:T(8,128)S(1)}, u32[]{:S(2)}, u32[]{:S(2)}) collective-permute-start(f32[8,64,1024]{2,1,0:T(8,128)S(1)} %dynamic-slice_bitcast_fusion), channel_id=1, source_target_pairs={{0,1},{1,0},{2,3},{3,2},{4,5},{5,4},{6,7},{7,6},{8,9},{9,8},{10,11... | collective-permute-start | bytes 6291464 | tf_op jit(solution)/shard_map/ppermute | solution.py:55
  184.3 35.1 %collective-permute-start.21 = (f32[4,64,1024]{2,1,0:T(8,128)}, f32[4,64,1024]{2,1,0:T(8,128)}, u32[]{:S(2)}, u32[]{:S(2)}) collective-permute-start(f32[4,64,1024]{2,1,0:T(8,128)} %dynamic-slice_bitcast_fusion.1), channel_id=1, source_target_pairs={{0,2},{1,3},{2,0},{3,1},{4,6},{5,7},{6,4},{7,5},{8,10},{9,11},{10,... | collective-permute-start | bytes 3145736 | tf_op jit(solution)/shard_map/ppermute | solution.py:55
  220.7 1.0 copy-start
  221.7 31.9 %collective-permute-start.22 = (f32[2,64,1024]{2,1,0:T(8,128)S(1)}, f32[2,64,1024]{2,1,0:T(8,128)S(1)}, u32[]{:S(2)}, u32[]{:S(2)}) collective-permute-start(f32[2,64,1024]{2,1,0:T(8,128)S(1)} %dynamic-slice_bitcast_fusion.2), channel_id=1, source_target_pairs={{0,4},{1,5},{2,6},{3,7},{4,0},{5,1},{6,2},{7,3},{8,12},{9,13},{10,... | collective-permute-start | bytes 1572872 | tf_op jit(solution)/shard_map/ppermute | solution.py:55
  254.8 26.0 %collective-permute-start.23 = (f32[1,64,1024]{2,1,0:T(8,128)S(1)}, f32[1,64,1024]{2,1,0:T(8,128)S(1)}, u32[]{:S(2)}, u32[]{:S(2)}) collective-permute-start(f32[1,64,1024]{2,1,0:T(8,128)S(1)} %constant_dynamic-slice_fusion), channel_id=1, source_target_pairs={{0,8},{1,9},{2,10},{3,11},{4,12},{5,13},{6,14},{7,15},{8,0},{9,1},... | collective-permute-start | bytes 786440 | tf_op jit(solution)/shard_map/ppermute | solution.py:55
  282.6 5.1 %collective-permute-start.26 = (f32[320,64]{0,1:T(8,128)S(1)}, f32[320,64]{0,1:T(8,128)S(1)}, u32[]{:S(2)}, u32[]{:S(2)}) collective-permute-start(f32[320,64]{0,1:T(8,128)S(1)} %fusion.99), channel_id=1, source_target_pairs={{0,3},{1,2},{2,1},{3,0},{4,7},{5,6},{6,5},{7,4},{8,11},{9,10},{10,... | collective-permute-start | bytes 245768 | tf_op jit(solution)/shard_map/ppermute | solution.py:107
  282.7 6.5 %collective-permute-start.25 = (f32[320,64]{0,1:T(8,128)S(1)}, f32[320,64]{0,1:T(8,128)S(1)}, u32[]{:S(2)}, u32[]{:S(2)}) collective-permute-start(f32[320,64]{0,1:T(8,128)S(1)} %fusion.99), channel_id=1, source_target_pairs={{0,2},{1,3},{2,0},{3,1},{4,6},{5,7},{6,4},{7,5},{8,10},{9,11},{10,... | collective-permute-start | bytes 245768 | tf_op jit(solution)/shard_map/ppermute | solution.py:107
  283.8 5.4 %collective-permute-start.24 = (f32[320,64]{0,1:T(8,128)S(1)}, f32[320,64]{0,1:T(8,128)S(1)}, u32[]{:S(2)}, u32[]{:S(2)}) collective-permute-start(f32[320,64]{0,1:T(8,128)S(1)} %fusion.99), channel_id=1, source_target_pairs={{0,1},{1,0},{2,3},{3,2},{4,5},{5,4},{6,7},{7,6},{8,9},{9,8},{10,11... | collective-permute-start | bytes 245768 | tf_op jit(solution)/shard_map/ppermute | solution.py:107
  289.2 39.3 %copy-start.2 = (f32[64,1024]{1,0:T(8,128)S(1)}, f32[64,1024]{1,0:T(8,128)}, u32[]{:S(2)}) copy-start(f32[64,1024]{1,0:T(8,128)} %reduce-scatter.2.cloned.1.call-done) | copy-start | bytes 786436
  289.3 39.3 %copy-start.4 = (f32[1024]{0:T(1024)S(1)}, f32[1024]{0:T(1024)}, u32[]{:S(2)}) copy-start(f32[1024]{0:T(1024)} %param.7) | copy-start | bytes 12292
  289.3 13.7 %collective-permute-start.29 = (f32[320,64]{0,1:T(8,128)S(1)}, f32[320,64]{0,1:T(8,128)S(1)}, u32[]{:S(2)}, u32[]{:S(2)}) collective-permute-start(f32[320,64]{0,1:T(8,128)S(1)} %fusion.141), channel_id=1, source_target_pairs={{0,12},{1,13},{2,14},{3,15},{4,8},{5,9},{6,10},{7,11},{8,4},{9,5},... | collective-permute-start | bytes 245768 | tf_op jit(solution)/shard_map/ppermute | solution.py:107
  294.3 12.5 %collective-permute-start.28 = (f32[320,64]{0,1:T(8,128)S(1)}, f32[320,64]{0,1:T(8,128)S(1)}, u32[]{:S(2)}, u32[]{:S(2)}) collective-permute-start(f32[320,64]{0,1:T(8,128)S(1)} %fusion.141), channel_id=1, source_target_pairs={{0,8},{1,9},{2,10},{3,11},{4,12},{5,13},{6,14},{7,15},{8,0},{9,1},... | collective-permute-start | bytes 245768 | tf_op jit(solution)/shard_map/ppermute | solution.py:107
  295.9 10.9 %collective-permute-start.27 = (f32[320,64]{0,1:T(8,128)S(1)}, f32[320,64]{0,1:T(8,128)S(1)}, u32[]{:S(2)}, u32[]{:S(2)}) collective-permute-start(f32[320,64]{0,1:T(8,128)S(1)} %fusion.141), channel_id=1, source_target_pairs={{0,4},{1,5},{2,6},{3,7},{4,0},{5,1},{6,2},{7,3},{8,12},{9,13},{10,... | collective-permute-start | bytes 245768 | tf_op jit(solution)/shard_map/ppermute | solution.py:107
  306.9 5.9 %collective-permute-start.32 = (f32[320,64]{0,1:T(8,128)S(1)}, f32[320,64]{0,1:T(8,128)S(1)}, u32[]{:S(2)}, u32[]{:S(2)}) collective-permute-start(f32[320,64]{0,1:T(8,128)S(1)} %fusion.140), channel_id=1, source_target_pairs={{0,48},{16,32},{32,16},{48,0},{64,112},{80,96},{96,80},{112,64},{1... | collective-permute-start | bytes 245768 | tf_op jit(solution)/shard_map/ppermute | solution.py:107
  309.3 6.1 %collective-permute-start.31 = (f32[320,64]{0,1:T(8,128)S(1)}, f32[320,64]{0,1:T(8,128)S(1)}, u32[]{:S(2)}, u32[]{:S(2)}) collective-permute-start(f32[320,64]{0,1:T(8,128)S(1)} %fusion.140), channel_id=1, source_target_pairs={{0,32},{16,48},{32,0},{48,16},{64,96},{80,112},{96,64},{112,80},{1... | collective-permute-start | bytes 245768 | tf_op jit(solution)/shard_map/ppermute | solution.py:107
  310.0 5.3 %collective-permute-start.30 = (f32[320,64]{0,1:T(8,128)S(1)}, f32[320,64]{0,1:T(8,128)S(1)}, u32[]{:S(2)}, u32[]{:S(2)}) collective-permute-start(f32[320,64]{0,1:T(8,128)S(1)} %fusion.140), channel_id=1, source_target_pairs={{0,16},{16,0},{32,48},{48,32},{64,80},{80,64},{96,112},{112,96},{1... | collective-permute-start | bytes 245768 | tf_op jit(solution)/shard_map/ppermute | solution.py:107
  315.5 4.7 %collective-permute-start.35 = (f32[320,64]{0,1:T(8,128)S(1)}, f32[320,64]{0,1:T(8,128)S(1)}, u32[]{:S(2)}, u32[]{:S(2)}) collective-permute-start(f32[320,64]{0,1:T(8,128)S(1)} %fusion.139), channel_id=1, source_target_pairs={{0,192},{16,208},{32,224},{48,240},{64,128},{80,144},{96,160},{112... | collective-permute-start | bytes 245768 | tf_op jit(solution)/shard_map/ppermute | solution.py:107
  315.9 6.3 %collective-permute-start.34 = (f32[320,64]{0,1:T(8,128)S(1)}, f32[320,64]{0,1:T(8,128)S(1)}, u32[]{:S(2)}, u32[]{:S(2)}) collective-permute-start(f32[320,64]{0,1:T(8,128)S(1)} %fusion.139), channel_id=1, source_target_pairs={{0,128},{16,144},{32,160},{48,176},{64,192},{80,208},{96,224},{112... | collective-permute-start | bytes 245768 | tf_op jit(solution)/shard_map/ppermute | solution.py:107
  319.6 4.6 %collective-permute-start.33 = (f32[320,64]{0,1:T(8,128)S(1)}, f32[320,64]{0,1:T(8,128)S(1)}, u32[]{:S(2)}, u32[]{:S(2)}) collective-permute-start(f32[320,64]{0,1:T(8,128)S(1)} %fusion.139), channel_id=1, source_target_pairs={{0,64},{16,80},{32,96},{48,112},{64,0},{80,16},{96,32},{112,48},{1... | collective-permute-start | bytes 245768 | tf_op jit(solution)/shard_map/ppermute | solution.py:107
Sparse Core Ops, SparseCore 0:
  60.4 39.4 all-gather.1
  174.3 78.8 reduce-scatter.1

commit v2 on v0

--- a/solution.py
+++ b/solution.py
@@ -134,9 +134,8 @@
     return flat.reshape(shape)
 
 
-def inverse_factors(gram_blocks):
-    factors = jnp.linalg.cholesky(gram_blocks)
-    identity = jnp.broadcast_to(jnp.eye(gram_blocks.shape[1], dtype=gram_blocks.dtype), gram_blocks.shape)
+def inverse_factors(factors):
+    identity = jnp.broadcast_to(jnp.eye(factors.shape[1], dtype=factors.dtype), factors.shape)
     return jax.scipy.linalg.solve_triangular(factors, identity, lower=True)
 
 
@@ -156,9 +155,10 @@
     lower = halving_sum(lower_local, ("col", "row"))
     row_probes = lax.all_gather(probe_block, "col", axis=1, tiled=True)
     col_probes = lax.all_gather(probe_block, "row", axis=1, tiled=True)
-    lower, row_probes, col_probes = lax.optimization_barrier((lower, row_probes, col_probes))
     gram = {pair: lower[n] for n, pair in enumerate(pairs)}
-    inverses = inverse_factors(jnp.stack([gram[(b, b)] for b in range(block_count)]))
+    factors = jnp.linalg.cholesky(jnp.stack([gram[(b, b)] for b in range(block_count)]))
+    factors, row_probes, col_probes = lax.optimization_barrier((factors, row_probes, col_probes))
+    inverses = inverse_factors(factors)
     row_part, col_part = tile_products(tile_values, tile_index, row_probes, col_probes, col_count)
     row_total = sum_rows(row_part)
     col_total = sum_columns(col_part)

time: 306 us -> 321 us (1.049)
  waiting for transfers between devices: 85.6 us -> 105 us
  local copies, waits for them, and re-layouts: 10.8 us -> 5.59 us
  other arithmetic: 73.9 us -> 70.6 us
    ppermute x4, waiting for transfers between devices: 23.4 us -> 52.5 us  [sum_rows(): row_part = keep + lax.ppermute(give, 'col', pairs)]
    all_gather x1, waiting for transfers between devices: 5.08 us -> 0.02 us  [shards(): col_probes = lax.all_gather(probe_block, 'row', axis=1, tiled=True)]
    unnamed x31 -> x27, local copies, waits for them, and re-layouts: 5.33 us -> 1.32 us
    ppermute x8, waiting for transfers between devices: 17.1 us -> 13.2 us  [halving_sum(): other = lax.ppermute(flat, axis, pairs)]
    another operation x3 -> x2, other arithmetic: 24.7 us -> 24.6 us  [inverse_factors(): return jax.scipy.linalg.solve_triangular(factors, identity, lower=True)]
  transfers between devices with their start and end apart: 35 -> 35, of which waited for: 29 -> 27; matrix products, arithmetic and copies ran while one was open for 24% -> 24% of each run, Pallas kernels for 0% -> 0%
where the time goes in v2:
time: 321 us; the launch traced here: 318 us
  waiting for transfers between devices  105 us (33%)
  other arithmetic  70.6 us (22%)
  starting transfers between devices  65.2 us (20%)
  between operations  40.1 us (12%)
  matrix products  31.5 us (10%)
  local copies, waits for them, and re-layouts  5.59 us (2%)
    ppermute x4, waiting for transfers between devices, sum_rows(): row_part = keep + lax.ppermute(give, 'col', pairs)  52.5 us
    another operation x4, other arithmetic, shards(): jnp.linalg.cholesky(jnp.stack([gram[b, b] for b in range(block_count)]))  29.5 us
    another operation x2, other arithmetic, inverse_factors(): return jax.scipy.linalg.solve_triangular(factors, identity, lower=True)  24.6 us
    ppermute x12, waiting for transfers between devices, radix_sum(): received.append(lax.ppermute(value, axis, pairs))  21.5 us
    ppermute x8, starting transfers between devices, halving_sum(): flat = keep + lax.ppermute(give, axis, pairs)  20.7 us
    ppermute x8, starting transfers between devices, halving_sum(): other = lax.ppermute(flat, axis, pairs)  18.7 us
    ppermute x12, starting transfers between devices, radix_sum(): received.append(lax.ppermute(value, axis, pairs))  16.9 us
    ppermute x8, waiting for transfers between devices, halving_sum(): flat = keep + lax.ppermute(give, axis, pairs)  16.6 us
  transfers between devices with their start and end apart: 35, of which 27 were waited for; matrix products, arithmetic and copies ran while one was open for 24% of the time, Pallas kernels for 0%

profile of v2, /device:TPU:8, one launch (start us, length us, event | category | flops | bytes accessed | tf_op | source)
XLA Modules:
  0.0 317.7 jit_solution(3339799934564443741)
XLA Ops:
  8.0 1.2 pad_maximum_fusion
  10.8 1.3 collective-permute-done
  12.3 2.0 collective-permute-start.1
  14.3 2.3 collective-permute-done.1
  16.9 3.4 %collective-permute-start.2 = (f32[7680]{0:T(1024)S(1)}, f32[7680]{0:T(1024)S(1)}, u32[]{:S(2)}, u32[]{:S(2)}) collective-permute-start(f32[7680]{0:T(1024)S(1)} %get-tuple-element.22), channel_id=1, source_target_pairs={{0,4},{1,5},{2,6},{3,7},{4,0},{5,1},{6,2},{7,3},{8,12},{9,13},{10,... | collective-permute-start | bytes 92168 | tf_op jit(solution)/shard_map/ppermute | solution.py:126
  20.3 1.9 collective-permute-done.2
  22.3 6.9 %collective-permute-start.3 = (f32[3840]{0:T(1024)S(1)}, f32[3840]{0:T(1024)S(1)}, u32[]{:S(2)}, u32[]{:S(2)}) collective-permute-start(f32[3840]{0:T(1024)S(1)} %get-tuple-element.24), channel_id=1, source_target_pairs={{0,8},{1,9},{2,10},{3,11},{4,12},{5,13},{6,14},{7,15},{8,0},{9,1},... | collective-permute-start | bytes 46088 | tf_op jit(solution)/shard_map/ppermute | solution.py:126
  29.2 1.7 collective-permute-done.3
  31.0 1.6 collective-permute-start.4
  32.6 2.2 collective-permute-done.4
  34.9 3.1 collective-permute-start.5
  38.0 2.1 collective-permute-done.5
  40.2 1.3 collective-permute-start.6
  41.5 2.3 collective-permute-done.6
  43.9 2.4 collective-permute-start.7
  46.3 2.8 collective-permute-done.7
  49.1 2.3 collective-permute-start.8
  51.4 2.8 collective-permute-done.8
  54.2 1.3 collective-permute-start.9
  55.5 2.3 collective-permute-done.9
  58.0 3.0 collective-permute-start.10
  61.0 2.1 collective-permute-done.10
  63.3 1.5 collective-permute-start.11
  64.8 2.2 collective-permute-done.11
  67.0 6.2 %collective-permute-start.12 = (f32[3840]{0:T(1024)S(1)}, f32[3840]{0:T(1024)S(1)}, u32[]{:S(2)}, u32[]{:S(2)}) collective-permute-start(f32[3840]{0:T(1024)S(1)} %pad_maximum_fusion.10), channel_id=1, source_target_pairs={{0,8},{1,9},{2,10},{3,11},{4,12},{5,13},{6,14},{7,15},{8,0},{9,1},... | collective-permute-start | bytes 46088 | tf_op jit(solution)/shard_map/ppermute | solution.py:130
  73.3 1.6 collective-permute-done.12
  74.9 2.0 collective-permute-start.13
  101.4 2.1 collective-permute-start.14
  103.5 2.2 collective-permute-done.14
  108.8 29.3 %custom-call.8 = f32[5,64,64]{2,1,0:T(8,128)S(1)} custom-call(f32[5,64,64]{2,1,0:T(8,128)S(1)} %fusion.37), custom_call_target="Cholesky" | custom-call | tf_op jit(solution)/shard_map/jit(cholesky)/cholesky | solution.py:159
  138.5 2.2 fusion.12
  140.6 2.2 fusion.16
  142.8 2.2 fusion.4
  144.9 2.2 fusion.8
  147.1 2.9 add_dynamic-update-slice_fusion.15
  155.6 0.8 add_dynamic-update-slice_fusion.7
  162.0 2.4 fusion.18
  164.4 2.4 fusion.14
  166.9 2.4 fusion.10
  169.3 2.4 fusion.6
  171.7 2.5 bitcast_dynamic-update-slice_fusion.15
  176.6 3.8 %collective-permute-done.16 = f32[8,64,1024]{2,1,0:T(8,128)S(1)} collective-permute-done((f32[8,64,1024]{2,1,0:T(8,128)S(1)}, f32[8,64,1024]{2,1,0:T(8,128)S(1)}, u32[]{:S(2)}, u32[]{:S(2)}) %collective-permute-start.16) | collective-permute-done | bytes 2097184 | tf_op jit(solution)/shard_map/ppermute | solution.py:55
  181.1 2.1 collective-permute-start.17
  183.2 23.7 %collective-permute-done.17 = f32[4,64,1024]{2,1,0:T(8,128)S(1)} collective-permute-done((f32[4,64,1024]{2,1,0:T(8,128)S(1)}, f32[4,64,1024]{2,1,0:T(8,128)S(1)}, u32[]{:S(2)}, u32[]{:S(2)}) %collective-permute-start.17) | collective-permute-done | bytes 1048608 | tf_op jit(solution)/shard_map/ppermute | solution.py:55
  207.9 25.0 %collective-permute-done.18 = f32[2,64,1024]{2,1,0:T(8,128)S(1)} collective-permute-done((f32[2,64,1024]{2,1,0:T(8,128)S(1)}, f32[2,64,1024]{2,1,0:T(8,128)S(1)}, u32[]{:S(2)}, u32[]{:S(2)}) %collective-permute-start.18) | collective-permute-done | bytes 524320 | tf_op jit(solution)/shard_map/ppermute | solution.py:55
  233.1 5.3 %collective-permute-start.19 = (f32[1,64,1024]{2,1,0:T(8,128)S(1)}, f32[1,64,1024]{2,1,0:T(8,128)S(1)}, u32[]{:S(2)}, u32[]{:S(2)}) collective-permute-start(f32[1,64,1024]{2,1,0:T(8,128)S(1)} %constant_dynamic-slice_fusion), channel_id=1, source_target_pairs={{0,8},{1,9},{2,10},{3,11},{4,12},{5,13},{6,14},{7,15},{8,0},{9,1},... | collective-permute-start | bytes 786440 | tf_op jit(solution)/shard_map/ppermute | solution.py:55
  238.4 24.6 %custom-call.9 = f32[5,1,64,64]{2,3,1,0:T(8,128)S(1)} custom-call(f32[5,1,64,64]{3,2,1,0:T(8,128)S(1)} %select_bitcast_fusion), custom_call_target="InvertDiagBlocksLowerTriangular" | custom-call | tf_op jit(solution)/shard_map/jit(_solve_triangular)/vmap()/triangular_solve | solution.py:139
  263.5 1.7 fusion.81
  265.4 1.8 collective-permute-start.22
  268.0 3.0 collective-permute-done.21
  271.0 1.2 collective-permute-done.22
  272.2 0.9 collective-permute-start.23
  273.5 5.3 %collective-permute-start.25 = (f32[320,64]{0,1:T(8,128)S(1)}, f32[320,64]{0,1:T(8,128)S(1)}, u32[]{:S(2)}, u32[]{:S(2)}) collective-permute-start(f32[320,64]{0,1:T(8,128)S(1)} %fusion.139), channel_id=1, source_target_pairs={{0,12},{1,13},{2,14},{3,15},{4,8},{5,9},{6,10},{7,11},{8,4},{9,5},... | collective-permute-start | bytes 245768 | tf_op jit(solution)/shard_map/ppermute | solution.py:92
  278.9 4.9 %collective-permute-done.23 = f32[320,64]{0,1:T(8,128)S(1)} collective-permute-done((f32[320,64]{0,1:T(8,128)S(1)}, f32[320,64]{0,1:T(8,128)S(1)}, u32[]{:S(2)}, u32[]{:S(2)}) %collective-permute-start.23) | collective-permute-done | bytes 81952 | tf_op jit(solution)/shard_map/ppermute | solution.py:92
  283.8 2.1 collective-permute-done.25
  285.9 1.5 collective-permute-start.26
  287.4 2.8 collective-permute-start.27
  291.2 3.5 %collective-permute-done.27 = f32[320,64]{0,1:T(8,128)S(1)} collective-permute-done((f32[320,64]{0,1:T(8,128)S(1)}, f32[320,64]{0,1:T(8,128)S(1)}, u32[]{:S(2)}, u32[]{:S(2)}) %collective-permute-start.27) | collective-permute-done | bytes 81952 | tf_op jit(solution)/shard_map/ppermute | solution.py:92
  294.7 1.6 collective-permute-done.28
  296.8 2.5 collective-permute-start.30
  299.9 1.1 collective-permute-done.29
  301.0 2.8 collective-permute-done.30
  303.8 1.0 collective-permute-done.31
  309.1 1.2 convolution_subtract_fusion
  (196 shorter events, 30.5 us)
Async XLA Ops:
  7.2 69.8 %copy-start.2 = (s32[5,3]{0,1:T(4,128)S(1)}, s32[5,3]{0,1:T(4,128)}, u32[]{:S(2)}) copy-start(s32[5,3]{0,1:T(4,128)} %param.9) | copy-start | bytes 184
  7.2 131.2 %all-gather.3.cloned.1.call-start = ((), (), s32[]{:S(2)}) async-start(), calls=%async_computation.1 | async-start | bytes 2228224 | tf_op jit(solution)/shard_map/all_gather | solution.py:156
  7.9 130.5 %all-gather.5.cloned.1.call-start = ((), (), s32[]{:S(2)}) async-start(), calls=%async_computation.2 | async-start | bytes 2228224 | tf_op jit(solution)/shard_map/all_gather | solution.py:157
  10.7 1.4 collective-permute-start
  12.3 4.3 %collective-permute-start.1 = (f32[15360]{0:T(1024)S(1)}, f32[15360]{0:T(1024)S(1)}, u32[]{:S(2)}, u32[]{:S(2)}) collective-permute-start(f32[15360]{0:T(1024)S(1)} %bitcast.316), channel_id=1, source_target_pairs={{0,2},{1,3},{2,0},{3,1},{4,6},{5,7},{6,4},{7,5},{8,10},{9,11},{10,... | collective-permute-start | bytes 184328 | tf_op jit(solution)/shard_map/ppermute | solution.py:126
  16.9 5.2 %collective-permute-start.2 = (f32[7680]{0:T(1024)S(1)}, f32[7680]{0:T(1024)S(1)}, u32[]{:S(2)}, u32[]{:S(2)}) collective-permute-start(f32[7680]{0:T(1024)S(1)} %get-tuple-element.22), channel_id=1, source_target_pairs={{0,4},{1,5},{2,6},{3,7},{4,0},{5,1},{6,2},{7,3},{8,12},{9,13},{10,... | collective-permute-start | bytes 92168 | tf_op jit(solution)/shard_map/ppermute | solution.py:126
  22.3 8.7 %collective-permute-start.3 = (f32[3840]{0:T(1024)S(1)}, f32[3840]{0:T(1024)S(1)}, u32[]{:S(2)}, u32[]{:S(2)}) collective-permute-start(f32[3840]{0:T(1024)S(1)} %get-tuple-element.24), channel_id=1, source_target_pairs={{0,8},{1,9},{2,10},{3,11},{4,12},{5,13},{6,14},{7,15},{8,0},{9,1},... | collective-permute-start | bytes 46088 | tf_op jit(solution)/shard_map/ppermute | solution.py:126
  31.0 3.7 %collective-permute-start.4 = (f32[1920]{0:T(1024)S(1)}, f32[1920]{0:T(1024)S(1)}, u32[]{:S(2)}, u32[]{:S(2)}) collective-permute-start(f32[1920]{0:T(1024)S(1)} %get-tuple-element.26), channel_id=1, source_target_pairs={{0,16},{16,0},{32,48},{48,32},{64,80},{80,64},{96,112},{112,96},{1... | collective-permute-start | bytes 23048 | tf_op jit(solution)/shard_map/ppermute | solution.py:126
  34.9 5.2 %collective-permute-start.5 = (f32[960]{0:T(1024)S(1)}, f32[960]{0:T(1024)S(1)}, u32[]{:S(2)}, u32[]{:S(2)}) collective-permute-start(f32[960]{0:T(1024)S(1)} %bitcast.319), channel_id=1, source_target_pairs={{0,32},{16,48},{32,0},{48,16},{64,96},{80,112},{96,64},{112,80},{1... | collective-permute-start | bytes 11528 | tf_op jit(solution)/shard_map/ppermute | solution.py:126
  40.2 3.7 %collective-permute-start.6 = (f32[480]{0:T(512)S(1)}, f32[480]{0:T(512)S(1)}, u32[]{:S(2)}, u32[]{:S(2)}) collective-permute-start(f32[480]{0:T(512)S(1)} %bitcast.321), channel_id=1, source_target_pairs={{0,64},{16,80},{32,96},{48,112},{64,0},{80,16},{96,32},{112,48},{1... | collective-permute-start | bytes 5768 | tf_op jit(solution)/shard_map/ppermute | solution.py:126
  43.9 5.2 %collective-permute-start.7 = (f32[240]{0:T(256)S(1)}, f32[240]{0:T(256)S(1)}, u32[]{:S(2)}, u32[]{:S(2)}) collective-permute-start(f32[240]{0:T(256)S(1)} %bitcast.322), channel_id=1, source_target_pairs={{0,128},{16,144},{32,160},{48,176},{64,192},{80,208},{96,224},{112... | collective-permute-start | bytes 2888 | tf_op jit(solution)/shard_map/ppermute | solution.py:126
  49.1 5.1 %collective-permute-start.8 = (f32[240]{0:T(256)S(1)}, f32[240]{0:T(256)S(1)}, u32[]{:S(2)}, u32[]{:S(2)}) collective-permute-start(f32[240]{0:T(256)S(1)} %add.759), channel_id=1, source_target_pairs={{0,128},{16,144},{32,160},{48,176},{64,192},{80,208},{96,224},{112... | collective-permute-start | bytes 2888 | tf_op jit(solution)/shard_map/ppermute | solution.py:130
  54.2 3.6 %collective-permute-start.9 = (f32[480]{0:T(512)S(1)}, f32[480]{0:T(512)S(1)}, u32[]{:S(2)}, u32[]{:S(2)}) collective-permute-start(f32[480]{0:T(512)S(1)} %pad_maximum_fusion.13), channel_id=1, source_target_pairs={{0,64},{16,80},{32,96},{48,112},{64,0},{80,16},{96,32},{112,48},{1... | collective-permute-start | bytes 5768 | tf_op jit(solution)/shard_map/ppermute | solution.py:130
  58.0 5.1 %collective-permute-start.10 = (f32[960]{0:T(1024)S(1)}, f32[960]{0:T(1024)S(1)}, u32[]{:S(2)}, u32[]{:S(2)}) collective-permute-start(f32[960]{0:T(1024)S(1)} %pad_maximum_fusion.12), channel_id=1, source_target_pairs={{0,32},{16,48},{32,0},{48,16},{64,96},{80,112},{96,64},{112,80},{1... | collective-permute-start | bytes 11528 | tf_op jit(solution)/shard_map/ppermute | solution.py:130
  63.3 3.7 %collective-permute-start.11 = (f32[1920]{0:T(1024)S(1)}, f32[1920]{0:T(1024)S(1)}, u32[]{:S(2)}, u32[]{:S(2)}) collective-permute-start(f32[1920]{0:T(1024)S(1)} %pad_maximum_fusion.11), channel_id=1, source_target_pairs={{0,16},{16,0},{32,48},{48,32},{64,80},{80,64},{96,112},{112,96},{1... | collective-permute-start | bytes 23048 | tf_op jit(solution)/shard_map/ppermute | solution.py:130
  67.0 7.9 %collective-permute-start.12 = (f32[3840]{0:T(1024)S(1)}, f32[3840]{0:T(1024)S(1)}, u32[]{:S(2)}, u32[]{:S(2)}) collective-permute-start(f32[3840]{0:T(1024)S(1)} %pad_maximum_fusion.10), channel_id=1, source_target_pairs={{0,8},{1,9},{2,10},{3,11},{4,12},{5,13},{6,14},{7,15},{8,0},{9,1},... | collective-permute-start | bytes 46088 | tf_op jit(solution)/shard_map/ppermute | solution.py:130
  73.2 190.3 %reduce-scatter.2.cloned.1.call-start = ((), (), s32[]{:S(2)}) async-start(), calls=%async_computation.3 | async-start | bytes 4456448 | tf_op jit(solution)/shard_map/reduce_scatter | solution.py:61
  74.9 26.4 %collective-permute-start.13 = (f32[7680]{0:T(1024)S(1)}, f32[7680]{0:T(1024)S(1)}, u32[]{:S(2)}, u32[]{:S(2)}) collective-permute-start(f32[7680]{0:T(1024)S(1)} %pad_maximum_fusion.9), channel_id=1, source_target_pairs={{0,4},{1,5},{2,6},{3,7},{4,0},{5,1},{6,2},{7,3},{8,12},{9,13},{10,... | collective-permute-start | bytes 92168 | tf_op jit(solution)/shard_map/ppermute | solution.py:130
  101.4 4.3 %collective-permute-start.14 = (f32[15360]{0:T(1024)S(1)}, f32[15360]{0:T(1024)S(1)}, u32[]{:S(2)}, u32[]{:S(2)}) collective-permute-start(f32[15360]{0:T(1024)S(1)} %pad_maximum_fusion.6), channel_id=1, source_target_pairs={{0,2},{1,3},{2,0},{3,1},{4,6},{5,7},{6,4},{7,5},{8,10},{9,11},{10,... | collective-permute-start | bytes 184328 | tf_op jit(solution)/shard_map/ppermute | solution.py:130
  105.7 2.1 collective-permute-start.15
  176.1 4.4 %collective-permute-start.16 = (f32[8,64,1024]{2,1,0:T(8,128)S(1)}, f32[8,64,1024]{2,1,0:T(8,128)S(1)}, u32[]{:S(2)}, u32[]{:S(2)}) collective-permute-start(f32[8,64,1024]{2,1,0:T(8,128)S(1)} %dynamic-slice_bitcast_fusion), channel_id=1, source_target_pairs={{0,1},{1,0},{2,3},{3,2},{4,5},{5,4},{6,7},{7,6},{8,9},{9,8},{10,11... | collective-permute-start | bytes 6291464 | tf_op jit(solution)/shard_map/ppermute | solution.py:55
  181.1 82.4 %copy-start = (bf16[64,1024]{1,0:T(8,128)(2,1)S(1)}, bf16[64,1024]{1,0:T(8,128)(2,1)}, u32[]{:S(2)}) copy-start(bf16[64,1024]{1,0:T(8,128)(2,1)} %param.5) | copy-start | bytes 393220
  181.1 82.4 %copy-start.3 = (f32[1024]{0:T(1024)S(1)}, f32[1024]{0:T(1024)}, u32[]{:S(2)}) copy-start(f32[1024]{0:T(1024)} %param.7) | copy-start | bytes 12292
  181.1 25.8 %collective-permute-start.17 = (f32[4,64,1024]{2,1,0:T(8,128)S(1)}, f32[4,64,1024]{2,1,0:T(8,128)S(1)}, u32[]{:S(2)}, u32[]{:S(2)}) collective-permute-start(f32[4,64,1024]{2,1,0:T(8,128)S(1)} %dynamic-slice_bitcast_fusion.1), channel_id=1, source_target_pairs={{0,2},{1,3},{2,0},{3,1},{4,6},{5,7},{6,4},{7,5},{8,10},{9,11},{10,... | collective-permute-start | bytes 3145736 | tf_op jit(solution)/shard_map/ppermute | solution.py:55
  207.1 25.8 %collective-permute-start.18 = (f32[2,64,1024]{2,1,0:T(8,128)S(1)}, f32[2,64,1024]{2,1,0:T(8,128)S(1)}, u32[]{:S(2)}, u32[]{:S(2)}) collective-permute-start(f32[2,64,1024]{2,1,0:T(8,128)S(1)} %dynamic-slice_bitcast_fusion.2), channel_id=1, source_target_pairs={{0,4},{1,5},{2,6},{3,7},{4,0},{5,1},{6,2},{7,3},{8,12},{9,13},{10,... | collective-permute-start | bytes 1572872 | tf_op jit(solution)/shard_map/ppermute | solution.py:55
  233.1 30.4 %collective-permute-start.19 = (f32[1,64,1024]{2,1,0:T(8,128)S(1)}, f32[1,64,1024]{2,1,0:T(8,128)S(1)}, u32[]{:S(2)}, u32[]{:S(2)}) collective-permute-start(f32[1,64,1024]{2,1,0:T(8,128)S(1)} %constant_dynamic-slice_fusion), channel_id=1, source_target_pairs={{0,8},{1,9},{2,10},{3,11},{4,12},{5,13},{6,14},{7,15},{8,0},{9,1},... | collective-permute-start | bytes 786440 | tf_op jit(solution)/shard_map/ppermute | solution.py:55
  265.2 2.8 collective-permute-start.20
  265.3 5.7 %collective-permute-start.21 = (f32[320,64]{0,1:T(8,128)S(1)}, f32[320,64]{0,1:T(8,128)S(1)}, u32[]{:S(2)}, u32[]{:S(2)}) collective-permute-start(f32[320,64]{0,1:T(8,128)S(1)} %fusion.81), channel_id=1, source_target_pairs={{0,2},{1,3},{2,0},{3,1},{4,6},{5,7},{6,4},{7,5},{8,10},{9,11},{10,... | collective-permute-start | bytes 245768 | tf_op jit(solution)/shard_map/ppermute | solution.py:92
  265.4 6.7 %collective-permute-start.22 = (f32[320,64]{0,1:T(8,128)S(1)}, f32[320,64]{0,1:T(8,128)S(1)}, u32[]{:S(2)}, u32[]{:S(2)}) collective-permute-start(f32[320,64]{0,1:T(8,128)S(1)} %fusion.81), channel_id=1, source_target_pairs={{0,3},{1,2},{2,1},{3,0},{4,7},{5,6},{6,5},{7,4},{8,11},{9,10},{10,... | collective-permute-start | bytes 245768 | tf_op jit(solution)/shard_map/ppermute | solution.py:92
  272.2 36.9 %copy-start.1 = (f32[64,1024]{1,0:T(8,128)S(1)}, f32[64,1024]{1,0:T(8,128)}, u32[]{:S(2)}) copy-start(f32[64,1024]{1,0:T(8,128)} %reduce-scatter.2.cloned.1.call-done) | copy-start | bytes 786436
  272.2 11.5 %collective-permute-start.23 = (f32[320,64]{0,1:T(8,128)S(1)}, f32[320,64]{0,1:T(8,128)S(1)}, u32[]{:S(2)}, u32[]{:S(2)}) collective-permute-start(f32[320,64]{0,1:T(8,128)S(1)} %fusion.139), channel_id=1, source_target_pairs={{0,4},{1,5},{2,6},{3,7},{4,0},{5,1},{6,2},{7,3},{8,12},{9,13},{10,... | collective-permute-start | bytes 245768 | tf_op jit(solution)/shard_map/ppermute | solution.py:92
  273.1 10.7 %collective-permute-start.24 = (f32[320,64]{0,1:T(8,128)S(1)}, f32[320,64]{0,1:T(8,128)S(1)}, u32[]{:S(2)}, u32[]{:S(2)}) collective-permute-start(f32[320,64]{0,1:T(8,128)S(1)} %fusion.139), channel_id=1, source_target_pairs={{0,8},{1,9},{2,10},{3,11},{4,12},{5,13},{6,14},{7,15},{8,0},{9,1},... | collective-permute-start | bytes 245768 | tf_op jit(solution)/shard_map/ppermute | solution.py:92
  273.5 12.3 %collective-permute-start.25 = (f32[320,64]{0,1:T(8,128)S(1)}, f32[320,64]{0,1:T(8,128)S(1)}, u32[]{:S(2)}, u32[]{:S(2)}) collective-permute-start(f32[320,64]{0,1:T(8,128)S(1)} %fusion.139), channel_id=1, source_target_pairs={{0,12},{1,13},{2,14},{3,15},{4,8},{5,9},{6,10},{7,11},{8,4},{9,5},... | collective-permute-start | bytes 245768 | tf_op jit(solution)/shard_map/ppermute | solution.py:92
  285.9 5.3 %collective-permute-start.26 = (f32[320,64]{0,1:T(8,128)S(1)}, f32[320,64]{0,1:T(8,128)S(1)}, u32[]{:S(2)}, u32[]{:S(2)}) collective-permute-start(f32[320,64]{0,1:T(8,128)S(1)} %fusion.138), channel_id=1, source_target_pairs={{0,16},{16,0},{32,48},{48,32},{64,80},{80,64},{96,112},{112,96},{1... | collective-permute-start | bytes 245768 | tf_op jit(solution)/shard_map/ppermute | solution.py:92
  287.4 7.3 %collective-permute-start.27 = (f32[320,64]{0,1:T(8,128)S(1)}, f32[320,64]{0,1:T(8,128)S(1)}, u32[]{:S(2)}, u32[]{:S(2)}) collective-permute-start(f32[320,64]{0,1:T(8,128)S(1)} %fusion.138), channel_id=1, source_target_pairs={{0,32},{16,48},{32,0},{48,16},{64,96},{80,112},{96,64},{112,80},{1... | collective-permute-start | bytes 245768 | tf_op jit(solution)/shard_map/ppermute | solution.py:92
  290.2 6.0 %collective-permute-start.28 = (f32[320,64]{0,1:T(8,128)S(1)}, f32[320,64]{0,1:T(8,128)S(1)}, u32[]{:S(2)}, u32[]{:S(2)}) collective-permute-start(f32[320,64]{0,1:T(8,128)S(1)} %fusion.138), channel_id=1, source_target_pairs={{0,48},{16,32},{32,16},{48,0},{64,112},{80,96},{96,80},{112,64},{1... | collective-permute-start | bytes 245768 | tf_op jit(solution)/shard_map/ppermute | solution.py:92
  296.3 4.7 %collective-permute-start.29 = (f32[320,64]{0,1:T(8,128)S(1)}, f32[320,64]{0,1:T(8,128)S(1)}, u32[]{:S(2)}, u32[]{:S(2)}) collective-permute-start(f32[320,64]{0,1:T(8,128)S(1)} %fusion.137), channel_id=1, source_target_pairs={{0,64},{16,80},{32,96},{48,112},{64,0},{80,16},{96,32},{112,48},{1... | collective-permute-start | bytes 245768 | tf_op jit(solution)/shard_map/ppermute | solution.py:92
  296.8 7.0 %collective-permute-start.30 = (f32[320,64]{0,1:T(8,128)S(1)}, f32[320,64]{0,1:T(8,128)S(1)}, u32[]{:S(2)}, u32[]{:S(2)}) collective-permute-start(f32[320,64]{0,1:T(8,128)S(1)} %fusion.137), channel_id=1, source_target_pairs={{0,128},{16,144},{32,160},{48,176},{64,192},{80,208},{96,224},{112... | collective-permute-start | bytes 245768 | tf_op jit(solution)/shard_map/ppermute | solution.py:92
  299.3 5.5 %collective-permute-start.31 = (f32[320,64]{0,1:T(8,128)S(1)}, f32[320,64]{0,1:T(8,128)S(1)}, u32[]{:S(2)}, u32[]{:S(2)}) collective-permute-start(f32[320,64]{0,1:T(8,128)S(1)} %fusion.137), channel_id=1, source_target_pairs={{0,192},{16,208},{32,224},{48,240},{64,128},{80,144},{96,160},{112... | collective-permute-start | bytes 245768 | tf_op jit(solution)/shard_map/ppermute | solution.py:92
Sparse Core Ops, SparseCore 0:
  9.9 42.8 all-gather.2
  73.3 47.5 all-gather.4
  162.1 83.7 reduce-scatter.1

commit v3 on v0

--- a/solution.py
+++ b/solution.py
@@ -8,24 +8,26 @@
     tile_width = tile_values.shape[1]
     row_spans = row_probes.shape[1] // tile_width
     col_spans = col_probes.shape[1] // tile_width
-    forwards, mirrors, row_spans_of, col_spans_of = [], [], [], []
-    for slot_index in range(tile_values.shape[0]):
-        current_tile = tile_values[slot_index]
-        live = tile_index[slot_index, 2] > 0
-        row_span = tile_index[slot_index, 0] % col_count
-        col_span = tile_index[slot_index, 1] // col_count
-        right = lax.dynamic_slice_in_dim(col_probes, col_span * tile_width, tile_width, 1)
-        left = lax.dynamic_slice_in_dim(row_probes, row_span * tile_width, tile_width, 1)
-        forward = lax.dot_general(
-            right, current_tile, (((1,), (1,)), ((), ())), preferred_element_type=jnp.float32
-        )
-        mirror = jnp.dot(left, current_tile, preferred_element_type=jnp.float32)
-        forwards.append(forward)
-        mirrors.append(mirror)
-        row_spans_of.append(jnp.where(live, row_span, -1))
-        col_spans_of.append(jnp.where(live, col_span, -1))
-    row_part = jnp.stack(spread_spans(forwards, row_spans_of, row_spans))
-    col_part = jnp.concatenate(spread_spans(mirrors, col_spans_of, col_spans), axis=1)
+    live = [tile_index[slot, 2] > 0 for slot in range(tile_values.shape[0])]
+    row_of = [tile_index[slot, 0] % col_count for slot in range(tile_values.shape[0])]
+    col_of = [tile_index[slot, 1] // col_count for slot in range(tile_values.shape[0])]
+    forwards = []
+    for slot in range(tile_values.shape[0]):
+        right = lax.dynamic_slice_in_dim(col_probes, col_of[slot] * tile_width, tile_width, 1)
+        forwards.append(lax.dot_general(
+            right, tile_values[slot], (((1,), (1,)), ((), ())), preferred_element_type=jnp.float32
+        ))
+    row_part = jnp.stack(spread_spans(
+        forwards, [jnp.where(l, r, -1) for l, r in zip(live, row_of)], row_spans
+    ))
+    row_part, (tile_values, row_probes) = sum_rows(row_part, (tile_values, row_probes))
+    mirrors = []
+    for slot in range(tile_values.shape[0]):
+        left = lax.dynamic_slice_in_dim(row_probes, row_of[slot] * tile_width, tile_width, 1)
+        mirrors.append(jnp.dot(left, tile_values[slot], preferred_element_type=jnp.float32))
+    col_part = jnp.concatenate(spread_spans(
+        mirrors, [jnp.where(l, c, -1) for l, c in zip(live, col_of)], col_spans
+    ), axis=1)
     return row_part, col_part
 
 
@@ -40,11 +42,11 @@
     return pieces
 
 
-def sum_rows(row_part):
+def sum_rows(row_part, riders):
     size = lax.axis_size("col")
     if size & (size - 1):
         flat = jnp.concatenate(list(row_part), axis=1)
-        return lax.psum_scatter(flat, "col", scatter_dimension=1, tiled=True)
+        return lax.psum_scatter(flat, "col", scatter_dimension=1, tiled=True), riders
     stride = 1
     while stride < size:
         bit = lax.axis_index("col") // stride % 2
@@ -53,8 +55,10 @@
         give = lax.dynamic_index_in_dim(grouped, 1 - bit, 1, keepdims=False)
         pairs = [(index, index ^ stride) for index in range(size)]
         row_part = keep + lax.ppermute(give, "col", pairs)
+        if stride == 1:
+            row_part, riders = lax.optimization_barrier((row_part, riders))
         stride *= 2
-    return row_part[0]
+    return row_part[0], riders
 
 
 def sum_columns(col_part):
@@ -160,7 +164,7 @@
     gram = {pair: lower[n] for n, pair in enumerate(pairs)}
     inverses = inverse_factors(jnp.stack([gram[(b, b)] for b in range(block_count)]))
     row_part, col_part = tile_products(tile_values, tile_index, row_probes, col_probes, col_count)
-    row_total = sum_rows(row_part)
+    row_total = row_part
     col_total = sum_columns(col_part)
     row_total, col_total, inverses = lax.optimization_barrier((row_total, col_total, inverses))
     product = self_relatedness[None, :] * probe_block.astype(jnp.float32) + row_total + col_total

time: 306 us -> 312 us (1.020)
  transfers between devices with their start and end apart: 35 -> 35, of which waited for: 29 -> 29; matrix products, arithmetic and copies ran while one was open for 24% -> 22% of each run, Pallas kernels for 0% -> 0%
where the time goes in v3:
time: 312 us; the launch traced here: 311 us
  waiting for transfers between devices  86.3 us (28%)
  other arithmetic  75.9 us (24%)
  starting transfers between devices  63.9 us (20%)
  between operations  39.7 us (13%)
  matrix products  32.3 us (10%)
  local copies, waits for them, and re-layouts  12.8 us (4%)
    another operation x4, other arithmetic, inverse_factors(): factors = jnp.linalg.cholesky(gram_blocks)  29.5 us
    another operation x3, other arithmetic, inverse_factors(): return jax.scipy.linalg.solve_triangular(factors, identity, lower=True)  24.7 us
    ppermute x4, waiting for transfers between devices, sum_rows(): row_part = keep + lax.ppermute(give, 'col', pairs)  23.3 us
    ppermute x12, waiting for transfers between devices, radix_sum(): received.append(lax.ppermute(value, axis, pairs))  22.8 us
    ppermute x8, starting transfers between devices, halving_sum(): flat = keep + lax.ppermute(give, axis, pairs)  20.7 us
    ppermute x8, starting transfers between devices, halving_sum(): other = lax.ppermute(flat, axis, pairs)  17.7 us
    ppermute x8, waiting for transfers between devices, halving_sum(): other = lax.ppermute(flat, axis, pairs)  17.1 us
    ppermute x12, starting transfers between devices, radix_sum(): received.append(lax.ppermute(value, axis, pairs))  16.9 us
  transfers between devices with their start and end apart: 35, of which 29 were waited for; matrix products, arithmetic and copies ran while one was open for 22% of the time, Pallas kernels for 0%

profile of v3, /device:TPU:8, one launch (start us, length us, event | category | flops | bytes accessed | tf_op | source)
XLA Modules:
  0.0 310.9 jit_solution(1108148965038143818)
XLA Ops:
  10.8 1.3 collective-permute-done
  12.3 2.0 collective-permute-start.1
  14.3 2.3 collective-permute-done.1
  16.9 3.4 %collective-permute-start.2 = (f32[7680]{0:T(1024)S(1)}, f32[7680]{0:T(1024)S(1)}, u32[]{:S(2)}, u32[]{:S(2)}) collective-permute-start(f32[7680]{0:T(1024)S(1)} %get-tuple-element.28), channel_id=1, source_target_pairs={{0,4},{1,5},{2,6},{3,7},{4,0},{5,1},{6,2},{7,3},{8,12},{9,13},{10,... | collective-permute-start | bytes 92168 | tf_op jit(solution)/shard_map/ppermute | solution.py:130
  20.2 1.9 collective-permute-done.2
  22.3 6.9 %collective-permute-start.3 = (f32[3840]{0:T(1024)S(1)}, f32[3840]{0:T(1024)S(1)}, u32[]{:S(2)}, u32[]{:S(2)}) collective-permute-start(f32[3840]{0:T(1024)S(1)} %get-tuple-element.30), channel_id=1, source_target_pairs={{0,8},{1,9},{2,10},{3,11},{4,12},{5,13},{6,14},{7,15},{8,0},{9,1},... | collective-permute-start | bytes 46088 | tf_op jit(solution)/shard_map/ppermute | solution.py:130
  29.2 1.7 collective-permute-done.3
  31.0 1.6 collective-permute-start.4
  32.6 2.2 collective-permute-done.4
  34.9 3.1 collective-permute-start.5
  38.0 2.1 collective-permute-done.5
  40.1 1.3 collective-permute-start.6
  41.5 2.3 collective-permute-done.6
  43.9 2.4 collective-permute-start.7
  46.3 2.8 collective-permute-done.7
  49.1 2.3 collective-permute-start.8
  51.4 2.8 collective-permute-done.8
  54.2 1.3 collective-permute-start.9
  55.5 2.3 collective-permute-done.9
  58.0 3.0 collective-permute-start.10
  61.0 2.1 collective-permute-done.10
  63.3 1.5 collective-permute-start.11
  64.9 2.1 collective-permute-done.11
  67.0 6.2 %collective-permute-start.12 = (f32[3840]{0:T(1024)S(1)}, f32[3840]{0:T(1024)S(1)}, u32[]{:S(2)}, u32[]{:S(2)}) collective-permute-start(f32[3840]{0:T(1024)S(1)} %pad_maximum_fusion.9), channel_id=1, source_target_pairs={{0,8},{1,9},{2,10},{3,11},{4,12},{5,13},{6,14},{7,15},{8,0},{9,1},... | collective-permute-start | bytes 46088 | tf_op jit(solution)/shard_map/ppermute | solution.py:134
  73.2 1.7 collective-permute-done.12
  74.9 2.0 collective-permute-start.13
  77.0 2.9 collective-permute-done.13
  81.0 3.2 %collective-permute-done.14 = f32[15360]{0:T(1024)S(1)} collective-permute-done((f32[15360]{0:T(1024)S(1)}, f32[15360]{0:T(1024)S(1)}, u32[]{:S(2)}, u32[]{:S(2)}) %collective-permute-start.14) | collective-permute-done | bytes 61472 | tf_op jit(solution)/shard_map/ppermute | solution.py:134
  110.3 5.7 %all-gather.5.cloned.1.call-done = bf16[64,16384]{1,0:T(8,128)(2,1)} async-done(((bf16[64,1024]{1,0:T(8,128)(2,1)}), bf16[64,16384]{1,0:T(8,128)(2,1)}) %all-gather.5.cloned.1.call-update) | async-done | bytes 2097168 | tf_op jit(solution)/shard_map/all_gather | solution.py:162
  116.0 2.4 fusion.12
  118.4 2.4 fusion.14
  120.8 2.4 fusion.16
  123.3 2.4 fusion.18
  125.7 2.5 bitcast_dynamic-update-slice_fusion.15
  129.8 2.0 copy-done
  132.3 4.0 %collective-permute-done.16 = f32[8,64,1024]{2,1,0:T(8,128)} collective-permute-done((f32[8,64,1024]{2,1,0:T(8,128)S(1)}, f32[8,64,1024]{2,1,0:T(8,128)}, u32[]{:S(2)}, u32[]{:S(2)}) %collective-permute-start.16) | collective-permute-done | bytes 2097184 | tf_op jit(solution)/shard_map/ppermute | solution.py:57
  136.4 2.6 bitcast_add_fusion
  139.0 2.2 fusion.2
  141.2 2.2 fusion.4
  143.3 2.2 fusion.6
  145.5 2.2 fusion.8
  147.6 2.9 add_dynamic-update-slice_fusion.15
  164.1 1.6 collective-permute-start.17
  170.3 19.3 %collective-permute-done.17 = f32[4,64,1024]{2,1,0:T(8,128)} collective-permute-done((f32[4,64,1024]{2,1,0:T(8,128)}, f32[4,64,1024]{2,1,0:T(8,128)}, u32[]{:S(2)}, u32[]{:S(2)}) %collective-permute-start.17) | collective-permute-done | bytes 1048608 | tf_op jit(solution)/shard_map/ppermute | solution.py:57
  189.6 1.4 bitcast_add_fusion.1
  192.0 2.8 collective-permute-start.18
  195.8 29.3 %custom-call.8 = f32[5,64,64]{2,1,0:T(8,128)S(1)} custom-call(f32[5,64,64]{2,1,0:T(8,128)S(1)} %fusion.32), custom_call_target="Cholesky" | custom-call | tf_op jit(solution)/shard_map/jit(cholesky)/cholesky | solution.py:142
  226.4 4.0 %collective-permute-start.19 = (f32[1,64,1024]{2,1,0:T(8,128)S(1)}, f32[1,64,1024]{2,1,0:T(8,128)S(1)}, u32[]{:S(2)}, u32[]{:S(2)}) collective-permute-start(f32[1,64,1024]{2,1,0:T(8,128)S(1)} %constant_dynamic-slice_fusion), channel_id=1, source_target_pairs={{0,8},{1,9},{2,10},{3,11},{4,12},{5,13},{6,14},{7,15},{8,0},{9,1},... | collective-permute-start | bytes 786440 | tf_op jit(solution)/shard_map/ppermute | solution.py:57
  230.5 24.6 %custom-call.9 = f32[5,1,64,64]{2,3,1,0:T(8,128)S(1)} custom-call(f32[5,1,64,64]{3,2,1,0:T(8,128)S(1)} %select_bitcast_fusion), custom_call_target="InvertDiagBlocksLowerTriangular" | custom-call | tf_op jit(solution)/shard_map/jit(_solve_triangular)/vmap()/triangular_solve | solution.py:144
  255.1 1.2 fusion.30
  256.4 1.7 fusion.94
  260.0 3.2 %collective-permute-done.22 = f32[320,64]{0,1:T(8,128)S(1)} collective-permute-done((f32[320,64]{0,1:T(8,128)S(1)}, f32[320,64]{0,1:T(8,128)S(1)}, u32[]{:S(2)}, u32[]{:S(2)}) %collective-permute-start.22) | collective-permute-done | bytes 81952 | tf_op jit(solution)/shard_map/ppermute | solution.py:96
  264.0 1.6 collective-permute-start.25
  265.6 4.2 %collective-permute-start.24 = (f32[320,64]{0,1:T(8,128)S(1)}, f32[320,64]{0,1:T(8,128)S(1)}, u32[]{:S(2)}, u32[]{:S(2)}) collective-permute-start(f32[320,64]{0,1:T(8,128)S(1)} %fusion.136), channel_id=1, source_target_pairs={{0,8},{1,9},{2,10},{3,11},{4,12},{5,13},{6,14},{7,15},{8,0},{9,1},... | collective-permute-start | bytes 245768 | tf_op jit(solution)/shard_map/ppermute | solution.py:96
  271.5 4.9 %collective-permute-done.24 = f32[320,64]{0,1:T(8,128)S(1)} collective-permute-done((f32[320,64]{0,1:T(8,128)S(1)}, f32[320,64]{0,1:T(8,128)S(1)}, u32[]{:S(2)}, u32[]{:S(2)}) %collective-permute-start.24) | collective-permute-done | bytes 81952 | tf_op jit(solution)/shard_map/ppermute | solution.py:96
  276.4 4.4 %collective-permute-done.23 = f32[320,64]{0,1:T(8,128)S(1)} collective-permute-done((f32[320,64]{0,1:T(8,128)S(1)}, f32[320,64]{0,1:T(8,128)S(1)}, u32[]{:S(2)}, u32[]{:S(2)}) %collective-permute-start.23) | collective-permute-done | bytes 81952 | tf_op jit(solution)/shard_map/ppermute | solution.py:96
  280.9 1.2 collective-permute-start.28
  283.1 1.9 collective-permute-start.26
  285.1 3.6 %collective-permute-done.28 = f32[320,64]{0,1:T(8,128)S(1)} collective-permute-done((f32[320,64]{0,1:T(8,128)S(1)}, f32[320,64]{0,1:T(8,128)S(1)}, u32[]{:S(2)}, u32[]{:S(2)}) %collective-permute-start.28) | collective-permute-done | bytes 81952 | tf_op jit(solution)/shard_map/ppermute | solution.py:96
  290.7 2.8 collective-permute-start.30
  293.8 1.6 collective-permute-done.31
  295.4 1.4 collective-permute-done.30
  296.8 1.3 collective-permute-done.29
  302.4 1.2 convolution_subtract_fusion
  (180 shorter events, 43.4 us)
Async XLA Ops:
  7.2 103.2 %all-gather.3.cloned.1.call-start = ((), (), s32[]{:S(2)}) async-start(), calls=%async_computation.1 | async-start | bytes 2228224 | tf_op jit(solution)/shard_map/all_gather | solution.py:161
  7.9 108.1 %all-gather.5.cloned.1.call-start = ((), (), s32[]{:S(2)}) async-start(), calls=%async_computation.2 | async-start | bytes 2228224 | tf_op jit(solution)/shard_map/all_gather | solution.py:162
  8.0 76.5 %copy-start.4 = (s32[5,3]{0,1:T(4,128)S(1)}, s32[5,3]{0,1:T(4,128)}, u32[]{:S(2)}) copy-start(s32[5,3]{0,1:T(4,128)} %param.9) | copy-start | bytes 184
  10.7 1.4 collective-permute-start
  12.3 4.3 %collective-permute-start.1 = (f32[15360]{0:T(1024)S(1)}, f32[15360]{0:T(1024)S(1)}, u32[]{:S(2)}, u32[]{:S(2)}) collective-permute-start(f32[15360]{0:T(1024)S(1)} %bitcast.342), channel_id=1, source_target_pairs={{0,2},{1,3},{2,0},{3,1},{4,6},{5,7},{6,4},{7,5},{8,10},{9,11},{10,... | collective-permute-start | bytes 184328 | tf_op jit(solution)/shard_map/ppermute | solution.py:130
  16.9 5.2 %collective-permute-start.2 = (f32[7680]{0:T(1024)S(1)}, f32[7680]{0:T(1024)S(1)}, u32[]{:S(2)}, u32[]{:S(2)}) collective-permute-start(f32[7680]{0:T(1024)S(1)} %get-tuple-element.28), channel_id=1, source_target_pairs={{0,4},{1,5},{2,6},{3,7},{4,0},{5,1},{6,2},{7,3},{8,12},{9,13},{10,... | collective-permute-start | bytes 92168 | tf_op jit(solution)/shard_map/ppermute | solution.py:130
  22.3 8.7 %collective-permute-start.3 = (f32[3840]{0:T(1024)S(1)}, f32[3840]{0:T(1024)S(1)}, u32[]{:S(2)}, u32[]{:S(2)}) collective-permute-start(f32[3840]{0:T(1024)S(1)} %get-tuple-element.30), channel_id=1, source_target_pairs={{0,8},{1,9},{2,10},{3,11},{4,12},{5,13},{6,14},{7,15},{8,0},{9,1},... | collective-permute-start | bytes 46088 | tf_op jit(solution)/shard_map/ppermute | solution.py:130
  31.0 3.7 %collective-permute-start.4 = (f32[1920]{0:T(1024)S(1)}, f32[1920]{0:T(1024)S(1)}, u32[]{:S(2)}, u32[]{:S(2)}) collective-permute-start(f32[1920]{0:T(1024)S(1)} %get-tuple-element.32), channel_id=1, source_target_pairs={{0,16},{16,0},{32,48},{48,32},{64,80},{80,64},{96,112},{112,96},{1... | collective-permute-start | bytes 23048 | tf_op jit(solution)/shard_map/ppermute | solution.py:130
  34.9 5.2 %collective-permute-start.5 = (f32[960]{0:T(1024)S(1)}, f32[960]{0:T(1024)S(1)}, u32[]{:S(2)}, u32[]{:S(2)}) collective-permute-start(f32[960]{0:T(1024)S(1)} %bitcast.345), channel_id=1, source_target_pairs={{0,32},{16,48},{32,0},{48,16},{64,96},{80,112},{96,64},{112,80},{1... | collective-permute-start | bytes 11528 | tf_op jit(solution)/shard_map/ppermute | solution.py:130
  40.1 3.7 %collective-permute-start.6 = (f32[480]{0:T(512)S(1)}, f32[480]{0:T(512)S(1)}, u32[]{:S(2)}, u32[]{:S(2)}) collective-permute-start(f32[480]{0:T(512)S(1)} %bitcast.347), channel_id=1, source_target_pairs={{0,64},{16,80},{32,96},{48,112},{64,0},{80,16},{96,32},{112,48},{1... | collective-permute-start | bytes 5768 | tf_op jit(solution)/shard_map/ppermute | solution.py:130
  43.9 5.2 %collective-permute-start.7 = (f32[240]{0:T(256)S(1)}, f32[240]{0:T(256)S(1)}, u32[]{:S(2)}, u32[]{:S(2)}) collective-permute-start(f32[240]{0:T(256)S(1)} %bitcast.348), channel_id=1, source_target_pairs={{0,128},{16,144},{32,160},{48,176},{64,192},{80,208},{96,224},{112... | collective-permute-start | bytes 2888 | tf_op jit(solution)/shard_map/ppermute | solution.py:130
  49.1 5.1 %collective-permute-start.8 = (f32[240]{0:T(256)S(1)}, f32[240]{0:T(256)S(1)}, u32[]{:S(2)}, u32[]{:S(2)}) collective-permute-start(f32[240]{0:T(256)S(1)} %add.759), channel_id=1, source_target_pairs={{0,128},{16,144},{32,160},{48,176},{64,192},{80,208},{96,224},{112... | collective-permute-start | bytes 2888 | tf_op jit(solution)/shard_map/ppermute | solution.py:134
  54.2 3.6 %collective-permute-start.9 = (f32[480]{0:T(512)S(1)}, f32[480]{0:T(512)S(1)}, u32[]{:S(2)}, u32[]{:S(2)}) collective-permute-start(f32[480]{0:T(512)S(1)} %pad_maximum_fusion.12), channel_id=1, source_target_pairs={{0,64},{16,80},{32,96},{48,112},{64,0},{80,16},{96,32},{112,48},{1... | collective-permute-start | bytes 5768 | tf_op jit(solution)/shard_map/ppermute | solution.py:134
  58.0 5.1 %collective-permute-start.10 = (f32[960]{0:T(1024)S(1)}, f32[960]{0:T(1024)S(1)}, u32[]{:S(2)}, u32[]{:S(2)}) collective-permute-start(f32[960]{0:T(1024)S(1)} %pad_maximum_fusion.11), channel_id=1, source_target_pairs={{0,32},{16,48},{32,0},{48,16},{64,96},{80,112},{96,64},{112,80},{1... | collective-permute-start | bytes 11528 | tf_op jit(solution)/shard_map/ppermute | solution.py:134
  63.3 3.7 %collective-permute-start.11 = (f32[1920]{0:T(1024)S(1)}, f32[1920]{0:T(1024)S(1)}, u32[]{:S(2)}, u32[]{:S(2)}) collective-permute-start(f32[1920]{0:T(1024)S(1)} %pad_maximum_fusion.10), channel_id=1, source_target_pairs={{0,16},{16,0},{32,48},{48,32},{64,80},{80,64},{96,112},{112,96},{1... | collective-permute-start | bytes 23048 | tf_op jit(solution)/shard_map/ppermute | solution.py:134
  64.8 191.6 %reduce-scatter.2.cloned.1.call-start = ((), (), s32[]{:S(2)}) async-start(), calls=%async_computation.3 | async-start | bytes 4456448 | tf_op jit(solution)/shard_map/reduce_scatter | solution.py:65
  67.0 7.9 %collective-permute-start.12 = (f32[3840]{0:T(1024)S(1)}, f32[3840]{0:T(1024)S(1)}, u32[]{:S(2)}, u32[]{:S(2)}) collective-permute-start(f32[3840]{0:T(1024)S(1)} %pad_maximum_fusion.9), channel_id=1, source_target_pairs={{0,8},{1,9},{2,10},{3,11},{4,12},{5,13},{6,14},{7,15},{8,0},{9,1},... | collective-permute-start | bytes 46088 | tf_op jit(solution)/shard_map/ppermute | solution.py:134
  74.9 4.9 %collective-permute-start.13 = (f32[7680]{0:T(1024)S(1)}, f32[7680]{0:T(1024)S(1)}, u32[]{:S(2)}, u32[]{:S(2)}) collective-permute-start(f32[7680]{0:T(1024)S(1)} %pad_maximum_fusion.8), channel_id=1, source_target_pairs={{0,4},{1,5},{2,6},{3,7},{4,0},{5,1},{6,2},{7,3},{8,12},{9,13},{10,... | collective-permute-start | bytes 92168 | tf_op jit(solution)/shard_map/ppermute | solution.py:134
  79.9 4.3 %collective-permute-start.14 = (f32[15360]{0:T(1024)S(1)}, f32[15360]{0:T(1024)S(1)}, u32[]{:S(2)}, u32[]{:S(2)}) collective-permute-start(f32[15360]{0:T(1024)S(1)} %pad_maximum_fusion.7), channel_id=1, source_target_pairs={{0,2},{1,3},{2,0},{3,1},{4,6},{5,7},{6,4},{7,5},{8,10},{9,11},{10,... | collective-permute-start | bytes 184328 | tf_op jit(solution)/shard_map/ppermute | solution.py:134
  84.2 25.9 %collective-permute-start.15 = (f32[30720]{0:T(1024)S(1)}, f32[30720]{0:T(1024)S(1)}, u32[]{:S(2)}, u32[]{:S(2)}) collective-permute-start(f32[30720]{0:T(1024)S(1)} %pad_maximum_fusion.6), channel_id=1, source_target_pairs={{0,1},{1,0},{2,3},{3,2},{4,5},{5,4},{6,7},{7,6},{8,9},{9,8},{10,11... | collective-permute-start | bytes 368648 | tf_op jit(solution)/shard_map/ppermute | solution.py:134
  129.8 2.0 copy-start
  132.0 4.4 %collective-permute-start.16 = (f32[8,64,1024]{2,1,0:T(8,128)S(1)}, f32[8,64,1024]{2,1,0:T(8,128)}, u32[]{:S(2)}, u32[]{:S(2)}) collective-permute-start(f32[8,64,1024]{2,1,0:T(8,128)S(1)} %dynamic-slice_bitcast_fusion), channel_id=1, source_target_pairs={{0,1},{1,0},{2,3},{3,2},{4,5},{5,4},{6,7},{7,6},{8,9},{9,8},{10,11... | collective-permute-start | bytes 6291464 | tf_op jit(solution)/shard_map/ppermute | solution.py:57
  164.1 25.5 %collective-permute-start.17 = (f32[4,64,1024]{2,1,0:T(8,128)}, f32[4,64,1024]{2,1,0:T(8,128)}, u32[]{:S(2)}, u32[]{:S(2)}) collective-permute-start(f32[4,64,1024]{2,1,0:T(8,128)} %dynamic-slice_bitcast_fusion.1), channel_id=1, source_target_pairs={{0,2},{1,3},{2,0},{3,1},{4,6},{5,7},{6,4},{7,5},{8,10},{9,11},{10,... | collective-permute-start | bytes 3145736 | tf_op jit(solution)/shard_map/ppermute | solution.py:57
  170.3 86.1 %copy-start.2 = (bf16[64,1024]{1,0:T(8,128)(2,1)S(1)}, bf16[64,1024]{1,0:T(8,128)(2,1)}, u32[]{:S(2)}) copy-start(bf16[64,1024]{1,0:T(8,128)(2,1)} %param.5) | copy-start | bytes 393220
  191.0 1.0 copy-start.1
  192.0 33.2 %collective-permute-start.18 = (f32[2,64,1024]{2,1,0:T(8,128)S(1)}, f32[2,64,1024]{2,1,0:T(8,128)S(1)}, u32[]{:S(2)}, u32[]{:S(2)}) collective-permute-start(f32[2,64,1024]{2,1,0:T(8,128)S(1)} %dynamic-slice_bitcast_fusion.2), channel_id=1, source_target_pairs={{0,4},{1,5},{2,6},{3,7},{4,0},{5,1},{6,2},{7,3},{8,12},{9,13},{10,... | collective-permute-start | bytes 1572872 | tf_op jit(solution)/shard_map/ppermute | solution.py:57
  226.4 29.9 %collective-permute-start.19 = (f32[1,64,1024]{2,1,0:T(8,128)S(1)}, f32[1,64,1024]{2,1,0:T(8,128)S(1)}, u32[]{:S(2)}, u32[]{:S(2)}) collective-permute-start(f32[1,64,1024]{2,1,0:T(8,128)S(1)} %constant_dynamic-slice_fusion), channel_id=1, source_target_pairs={{0,8},{1,9},{2,10},{3,11},{4,12},{5,13},{6,14},{7,15},{8,0},{9,1},... | collective-permute-start | bytes 786440 | tf_op jit(solution)/shard_map/ppermute | solution.py:57
  258.1 5.1 %collective-permute-start.22 = (f32[320,64]{0,1:T(8,128)S(1)}, f32[320,64]{0,1:T(8,128)S(1)}, u32[]{:S(2)}, u32[]{:S(2)}) collective-permute-start(f32[320,64]{0,1:T(8,128)S(1)} %fusion.94), channel_id=1, source_target_pairs={{0,3},{1,2},{2,1},{3,0},{4,7},{5,6},{6,5},{7,4},{8,11},{9,10},{10,... | collective-permute-start | bytes 245768 | tf_op jit(solution)/shard_map/ppermute | solution.py:96
  258.2 5.7 %collective-permute-start.21 = (f32[320,64]{0,1:T(8,128)S(1)}, f32[320,64]{0,1:T(8,128)S(1)}, u32[]{:S(2)}, u32[]{:S(2)}) collective-permute-start(f32[320,64]{0,1:T(8,128)S(1)} %fusion.94), channel_id=1, source_target_pairs={{0,2},{1,3},{2,0},{3,1},{4,6},{5,7},{6,4},{7,5},{8,10},{9,11},{10,... | collective-permute-start | bytes 245768 | tf_op jit(solution)/shard_map/ppermute | solution.py:96
  258.9 4.9 %collective-permute-start.20 = (f32[320,64]{0,1:T(8,128)S(1)}, f32[320,64]{0,1:T(8,128)S(1)}, u32[]{:S(2)}, u32[]{:S(2)}) collective-permute-start(f32[320,64]{0,1:T(8,128)S(1)} %fusion.94), channel_id=1, source_target_pairs={{0,1},{1,0},{2,3},{3,2},{4,5},{5,4},{6,7},{7,6},{8,9},{9,8},{10,11... | collective-permute-start | bytes 245768 | tf_op jit(solution)/shard_map/ppermute | solution.py:96
  263.9 38.4 %copy-start.3 = (f32[64,1024]{1,0:T(8,128)S(1)}, f32[64,1024]{1,0:T(8,128)}, u32[]{:S(2)}) copy-start(f32[64,1024]{1,0:T(8,128)} %reduce-scatter.2.cloned.1.call-done) | copy-start | bytes 786436
  263.9 38.4 %copy-start.5 = (f32[1024]{0:T(1024)S(1)}, f32[1024]{0:T(1024)}, u32[]{:S(2)}) copy-start(f32[1024]{0:T(1024)} %param.7) | copy-start | bytes 12292
  264.0 7.5 %collective-permute-start.25 = (f32[320,64]{0,1:T(8,128)S(1)}, f32[320,64]{0,1:T(8,128)S(1)}, u32[]{:S(2)}, u32[]{:S(2)}) collective-permute-start(f32[320,64]{0,1:T(8,128)S(1)} %fusion.136), channel_id=1, source_target_pairs={{0,12},{1,13},{2,14},{3,15},{4,8},{5,9},{6,10},{7,11},{8,4},{9,5},... | collective-permute-start | bytes 245768 | tf_op jit(solution)/shard_map/ppermute | solution.py:96
  265.6 10.8 %collective-permute-start.24 = (f32[320,64]{0,1:T(8,128)S(1)}, f32[320,64]{0,1:T(8,128)S(1)}, u32[]{:S(2)}, u32[]{:S(2)}) collective-permute-start(f32[320,64]{0,1:T(8,128)S(1)} %fusion.136), channel_id=1, source_target_pairs={{0,8},{1,9},{2,10},{3,11},{4,12},{5,13},{6,14},{7,15},{8,0},{9,1},... | collective-permute-start | bytes 245768 | tf_op jit(solution)/shard_map/ppermute | solution.py:96
  269.8 11.0 %collective-permute-start.23 = (f32[320,64]{0,1:T(8,128)S(1)}, f32[320,64]{0,1:T(8,128)S(1)}, u32[]{:S(2)}, u32[]{:S(2)}) collective-permute-start(f32[320,64]{0,1:T(8,128)S(1)} %fusion.136), channel_id=1, source_target_pairs={{0,4},{1,5},{2,6},{3,7},{4,0},{5,1},{6,2},{7,3},{8,12},{9,13},{10,... | collective-permute-start | bytes 245768 | tf_op jit(solution)/shard_map/ppermute | solution.py:96
  280.9 7.8 %collective-permute-start.28 = (f32[320,64]{0,1:T(8,128)S(1)}, f32[320,64]{0,1:T(8,128)S(1)}, u32[]{:S(2)}, u32[]{:S(2)}) collective-permute-start(f32[320,64]{0,1:T(8,128)S(1)} %fusion.135), channel_id=1, source_target_pairs={{0,48},{16,32},{32,16},{48,0},{64,112},{80,96},{96,80},{112,64},{1... | collective-permute-start | bytes 245768 | tf_op jit(solution)/shard_map/ppermute | solution.py:96
  282.1 7.0 %collective-permute-start.27 = (f32[320,64]{0,1:T(8,128)S(1)}, f32[320,64]{0,1:T(8,128)S(1)}, u32[]{:S(2)}, u32[]{:S(2)}) collective-permute-start(f32[320,64]{0,1:T(8,128)S(1)} %fusion.135), channel_id=1, source_target_pairs={{0,32},{16,48},{32,0},{48,16},{64,96},{80,112},{96,64},{112,80},{1... | collective-permute-start | bytes 245768 | tf_op jit(solution)/shard_map/ppermute | solution.py:96
  283.1 6.5 %collective-permute-start.26 = (f32[320,64]{0,1:T(8,128)S(1)}, f32[320,64]{0,1:T(8,128)S(1)}, u32[]{:S(2)}, u32[]{:S(2)}) collective-permute-start(f32[320,64]{0,1:T(8,128)S(1)} %fusion.135), channel_id=1, source_target_pairs={{0,16},{16,0},{32,48},{48,32},{64,80},{80,64},{96,112},{112,96},{1... | collective-permute-start | bytes 245768 | tf_op jit(solution)/shard_map/ppermute | solution.py:96
  289.6 5.8 %collective-permute-start.31 = (f32[320,64]{0,1:T(8,128)S(1)}, f32[320,64]{0,1:T(8,128)S(1)}, u32[]{:S(2)}, u32[]{:S(2)}) collective-permute-start(f32[320,64]{0,1:T(8,128)S(1)} %fusion.134), channel_id=1, source_target_pairs={{0,192},{16,208},{32,224},{48,240},{64,128},{80,144},{96,160},{112... | collective-permute-start | bytes 245768 | tf_op jit(solution)/shard_map/ppermute | solution.py:96
  290.7 6.1 %collective-permute-start.30 = (f32[320,64]{0,1:T(8,128)S(1)}, f32[320,64]{0,1:T(8,128)S(1)}, u32[]{:S(2)}, u32[]{:S(2)}) collective-permute-start(f32[320,64]{0,1:T(8,128)S(1)} %fusion.134), channel_id=1, source_target_pairs={{0,128},{16,144},{32,160},{48,176},{64,192},{80,208},{96,224},{112... | collective-permute-start | bytes 245768 | tf_op jit(solution)/shard_map/ppermute | solution.py:96
  293.4 4.6 %collective-permute-start.29 = (f32[320,64]{0,1:T(8,128)S(1)}, f32[320,64]{0,1:T(8,128)S(1)}, u32[]{:S(2)}, u32[]{:S(2)}) collective-permute-start(f32[320,64]{0,1:T(8,128)S(1)} %fusion.134), channel_id=1, source_target_pairs={{0,64},{16,80},{32,96},{48,112},{64,0},{80,16},{96,32},{112,48},{1... | collective-permute-start | bytes 245768 | tf_op jit(solution)/shard_map/ppermute | solution.py:96
Sparse Core Ops, SparseCore 0:
  9.8 42.6 all-gather.2
  64.9 51.0 all-gather.4
  163.1 82.5 reduce-scatter.1

commit v4 on v0

--- a/solution.py
+++ b/solution.py
@@ -156,7 +156,6 @@
     lower = halving_sum(lower_local, ("col", "row"))
     row_probes = lax.all_gather(probe_block, "col", axis=1, tiled=True)
     col_probes = lax.all_gather(probe_block, "row", axis=1, tiled=True)
-    lower, row_probes, col_probes = lax.optimization_barrier((lower, row_probes, col_probes))
     gram = {pair: lower[n] for n, pair in enumerate(pairs)}
     inverses = inverse_factors(jnp.stack([gram[(b, b)] for b in range(block_count)]))
     row_part, col_part = tile_products(tile_values, tile_index, row_probes, col_probes, col_count)

time: 306 us -> 288 us (0.941)
  waiting for transfers between devices: 85.6 us -> 66 us
  starting transfers between devices: 64.1 us -> 60.2 us
  other arithmetic: 73.9 us -> 77.3 us
    ppermute x8, waiting for transfers between devices: 16.6 us -> 10.3 us  [halving_sum(): flat = keep + lax.ppermute(give, axis, pairs)]
    ppermute x8, waiting for transfers between devices: 17.1 us -> 11 us  [halving_sum(): other = lax.ppermute(flat, axis, pairs)]
    all_gather x1, waiting for transfers between devices: 5.08 us -> 0.11 us  [shards(): col_probes = lax.all_gather(probe_block, 'row', axis=1, tiled=True)]
    ppermute x8, starting transfers between devices: 17.7 us -> 14.4 us  [halving_sum(): other = lax.ppermute(flat, axis, pairs)]
    dot_general x5, matrix products: 8.53 us -> 11.6 us  [tile_products(): mirror = jnp.dot(left, current_tile, preferred_element_type=jnp.float32)]
  transfers between devices with their start and end apart: 35 -> 35, of which waited for: 29 -> 23; matrix products, arithmetic and copies ran while one was open for 24% -> 38% of each run, Pallas kernels for 0% -> 0%
where the time goes in v4:
time: 288 us; the launch traced here: 287 us
  other arithmetic  77.3 us (27%)
  waiting for transfers between devices  66 us (23%)
  starting transfers between devices  60.2 us (21%)
  between operations  40.5 us (14%)
  matrix products  32.4 us (11%)
  local copies, waits for them, and re-layouts  10.2 us (4%)
    another operation x4, other arithmetic, inverse_factors(): factors = jnp.linalg.cholesky(gram_blocks)  30 us
    another operation x3, other arithmetic, inverse_factors(): return jax.scipy.linalg.solve_triangular(factors, identity, lower=True)  25.3 us
    ppermute x4, waiting for transfers between devices, sum_rows(): row_part = keep + lax.ppermute(give, 'col', pairs)  22.9 us
    ppermute x12, waiting for transfers between devices, radix_sum(): received.append(lax.ppermute(value, axis, pairs))  21 us
    ppermute x8, starting transfers between devices, halving_sum(): flat = keep + lax.ppermute(give, axis, pairs)  19.7 us
    ppermute x12, starting transfers between devices, radix_sum(): received.append(lax.ppermute(value, axis, pairs))  16.9 us
    ppermute x8, starting transfers between devices, halving_sum(): other = lax.ppermute(flat, axis, pairs)  14.4 us
    unnamed x28, other arithmetic  13 us
  transfers between devices with their start and end apart: 35, of which 23 were waited for; matrix products, arithmetic and copies ran while one was open for 38% of the time, Pallas kernels for 0%

profile of v4, /device:TPU:8, one launch (start us, length us, event | category | flops | bytes accessed | tf_op | source)
XLA Modules:
  0.0 286.6 jit_solution(18423591785643895218)
XLA Ops:
  8.0 1.2 pad_maximum_fusion
  10.8 1.3 collective-permute-done.4
  12.3 2.0 collective-permute-start.5
  14.3 2.3 collective-permute-done.5
  16.9 3.4 %collective-permute-start.6 = (f32[7680]{0:T(1024)S(1)}, f32[7680]{0:T(1024)S(1)}, u32[]{:S(2)}, u32[]{:S(2)}) collective-permute-start(f32[7680]{0:T(1024)S(1)} %get-tuple-element.16), channel_id=1, source_target_pairs={{0,4},{1,5},{2,6},{3,7},{4,0},{5,1},{6,2},{7,3},{8,12},{9,13},{10,... | collective-permute-start | bytes 92168 | tf_op jit(solution)/shard_map/ppermute | solution.py:126
  20.2 1.9 collective-permute-done.6
  22.3 6.9 %collective-permute-start.7 = (f32[3840]{0:T(1024)S(1)}, f32[3840]{0:T(1024)S(1)}, u32[]{:S(2)}, u32[]{:S(2)}) collective-permute-start(f32[3840]{0:T(1024)S(1)} %get-tuple-element.18), channel_id=1, source_target_pairs={{0,8},{1,9},{2,10},{3,11},{4,12},{5,13},{6,14},{7,15},{8,0},{9,1},... | collective-permute-start | bytes 46088 | tf_op jit(solution)/shard_map/ppermute | solution.py:126
  29.3 1.6 collective-permute-done.7
  31.0 1.6 collective-permute-start.8
  38.5 2.8 collective-permute-start.9
  46.9 3.1 %collective-permute-done.10 = f32[480]{0:T(512)S(1)} collective-permute-done((f32[480]{0:T(512)S(1)}, f32[480]{0:T(512)S(1)}, u32[]{:S(2)}, u32[]{:S(2)}) %collective-permute-start.10) | collective-permute-done | bytes 1952 | tf_op jit(solution)/shard_map/ppermute | solution.py:126
  50.1 2.4 collective-permute-start.11
  56.3 1.3 collective-permute-start.12
  59.5 1.9 collective-permute-done.12
  61.5 1.4 collective-permute-start.13
  75.4 3.3 %collective-permute-done.15 = f32[1920]{0:T(1024)S(1)} collective-permute-done((f32[1920]{0:T(1024)S(1)}, f32[1920]{0:T(1024)S(1)}, u32[]{:S(2)}, u32[]{:S(2)}) %collective-permute-start.15) | collective-permute-done | bytes 7712 | tf_op jit(solution)/shard_map/ppermute | solution.py:130
  78.7 2.1 fusion.4
  80.9 2.2 fusion.8
  83.0 2.2 fusion.12
  85.2 2.2 fusion.16
  87.4 3.0 %add_dynamic-update-slice_fusion.15 = (f32[64,16384]{1,0:T(8,128)}, f32[64,1024]{1,0:T(8,128)S(1)}) fusion(f32[64,1024]{1,0:T(8,128)S(1)} %fusion.4, f32[64,1024]{1,0:T(8,128)S(1)} %fusion.8, f32[64,1024]{1,0:T(8,128)S(1)} %fusion.12, f32[64,1024]{1,0:T(8,128)S(1)} %fusion.16, pred[]{:T(512)S(6)} %eq.619, pred[]{:T(512)S(6)} %eq.618, pred[]{:T(512)S(6)} %eq.617, ...), kind=kOutput, calls=%fused_computation.84 | convolution fusion | flops 134807552 | bytes 3801097 | tf_op jit(solution)/shard_map/dot_general | solution.py:22
  103.0 2.4 fusion.6
  105.4 2.4 fusion.10
  107.8 2.4 fusion.14
  110.3 2.4 fusion.18
  112.7 2.5 bitcast_dynamic-update-slice_fusion.15
  116.8 2.0 copy-done
  119.1 6.1 %collective-permute-start.16 = (f32[3840]{0:T(1024)S(1)}, f32[3840]{0:T(1024)S(1)}, u32[]{:S(2)}, u32[]{:S(2)}) collective-permute-start(f32[3840]{0:T(1024)S(1)} %pad_maximum_fusion.10), channel_id=1, source_target_pairs={{0,8},{1,9},{2,10},{3,11},{4,12},{5,13},{6,14},{7,15},{8,0},{9,1},... | collective-permute-start | bytes 46088 | tf_op jit(solution)/shard_map/ppermute | solution.py:130
  125.8 1.1 collective-permute-done.16
  126.9 2.6 collective-permute-start.17
  130.2 1.7 collective-permute-done.17
  131.9 1.6 collective-permute-start.18
  134.1 2.1 collective-permute-done.18
  136.3 2.8 bitcast_add_fusion
  139.1 1.1 dynamic-slice_bitcast_fusion.1
  140.3 1.5 collective-permute-start.1
  143.3 22.9 %collective-permute-done.1 = f32[4,64,1024]{2,1,0:T(8,128)} collective-permute-done((f32[4,64,1024]{2,1,0:T(8,128)}, f32[4,64,1024]{2,1,0:T(8,128)}, u32[]{:S(2)}, u32[]{:S(2)}) %collective-permute-start.1) | collective-permute-done | bytes 1048608 | tf_op jit(solution)/shard_map/ppermute | solution.py:55
  166.3 1.4 bitcast_add_fusion.1
  168.7 2.8 collective-permute-start.2
  171.6 29.3 %custom-call.8 = f32[5,64,64]{2,1,0:T(8,128)S(1)} custom-call(f32[5,64,64]{2,1,0:T(8,128)S(1)} %fusion.37), custom_call_target="Cholesky" | custom-call | tf_op jit(solution)/shard_map/jit(cholesky)/cholesky | solution.py:138
  201.1 1.1 bitcast_add_fusion.2
  202.2 4.8 %collective-permute-start.3 = (f32[1,64,1024]{2,1,0:T(8,128)S(1)}, f32[1,64,1024]{2,1,0:T(8,128)S(1)}, u32[]{:S(2)}, u32[]{:S(2)}) collective-permute-start(f32[1,64,1024]{2,1,0:T(8,128)S(1)} %constant_dynamic-slice_fusion.12), channel_id=1, source_target_pairs={{0,8},{1,9},{2,10},{3,11},{4,12},{5,13},{6,14},{7,15},{8,0},{9,1},... | collective-permute-start | bytes 786440 | tf_op jit(solution)/shard_map/ppermute | solution.py:55
  207.1 24.6 %custom-call.9 = f32[5,1,64,64]{2,3,1,0:T(8,128)S(1)} custom-call(f32[5,1,64,64]{3,2,1,0:T(8,128)S(1)} %select_bitcast_fusion), custom_call_target="InvertDiagBlocksLowerTriangular" | custom-call | tf_op jit(solution)/shard_map/jit(_solve_triangular)/vmap()/triangular_solve | solution.py:140
  231.7 1.2 fusion.35
  233.0 1.7 fusion.81
  234.7 1.1 collective-permute-start.21
  237.5 2.3 collective-permute-done.22
  239.7 1.5 collective-permute-done.21
  241.5 5.1 %collective-permute-start.24 = (f32[320,64]{0,1:T(8,128)S(1)}, f32[320,64]{0,1:T(8,128)S(1)}, u32[]{:S(2)}, u32[]{:S(2)}) collective-permute-start(f32[320,64]{0,1:T(8,128)S(1)} %fusion.139), channel_id=1, source_target_pairs={{0,8},{1,9},{2,10},{3,11},{4,12},{5,13},{6,14},{7,15},{8,0},{9,1},... | collective-permute-start | bytes 245768 | tf_op jit(solution)/shard_map/ppermute | solution.py:92
  246.5 1.4 collective-permute-start.23
  248.0 4.5 %collective-permute-done.25 = f32[320,64]{0,1:T(8,128)S(1)} collective-permute-done((f32[320,64]{0,1:T(8,128)S(1)}, f32[320,64]{0,1:T(8,128)S(1)}, u32[]{:S(2)}, u32[]{:S(2)}) %collective-permute-start.25) | collective-permute-done | bytes 81952 | tf_op jit(solution)/shard_map/ppermute | solution.py:92
  252.5 1.6 collective-permute-done.24
  254.1 3.1 %collective-permute-done.23 = f32[320,64]{0,1:T(8,128)S(1)} collective-permute-done((f32[320,64]{0,1:T(8,128)S(1)}, f32[320,64]{0,1:T(8,128)S(1)}, u32[]{:S(2)}, u32[]{:S(2)}) %collective-permute-start.23) | collective-permute-done | bytes 81952 | tf_op jit(solution)/shard_map/ppermute | solution.py:92
  257.2 1.5 collective-permute-start.28
  258.8 1.1 collective-permute-start.27
  259.9 1.6 collective-permute-start.26
  261.5 3.1 %collective-permute-done.28 = f32[320,64]{0,1:T(8,128)S(1)} collective-permute-done((f32[320,64]{0,1:T(8,128)S(1)}, f32[320,64]{0,1:T(8,128)S(1)}, u32[]{:S(2)}, u32[]{:S(2)}) %collective-permute-start.28) | collective-permute-done | bytes 81952 | tf_op jit(solution)/shard_map/ppermute | solution.py:92
  264.6 1.2 collective-permute-done.27
  266.5 2.3 collective-permute-start.30
  268.8 1.2 collective-permute-start.29
  270.1 1.4 collective-permute-done.31
  271.5 1.2 collective-permute-done.30
  272.7 1.1 collective-permute-done.29
  278.1 1.2 convolution_subtract_fusion
  (221 shorter events, 34.1 us)
Async XLA Ops:
  7.2 25.4 %copy-start.15 = (s32[5,3]{0,1:T(4,128)S(1)}, s32[5,3]{0,1:T(4,128)}, u32[]{:S(2)}) copy-start(s32[5,3]{0,1:T(4,128)} %param.9) | copy-start | bytes 184
  7.2 71.6 %all-gather.5.cloned.1.call-start = ((), (), s32[]{:S(2)}) async-start(), calls=%async_computation.2 | async-start | bytes 2228224 | tf_op jit(solution)/shard_map/all_gather | solution.py:157
  7.9 95.1 %all-gather.3.cloned.1.call-start = ((), (), s32[]{:S(2)}) async-start(), calls=%async_computation.1 | async-start | bytes 2228224 | tf_op jit(solution)/shard_map/all_gather | solution.py:158
  10.7 1.4 collective-permute-start.4
  12.3 4.3 %collective-permute-start.5 = (f32[15360]{0:T(1024)S(1)}, f32[15360]{0:T(1024)S(1)}, u32[]{:S(2)}, u32[]{:S(2)}) collective-permute-start(f32[15360]{0:T(1024)S(1)} %bitcast.316), channel_id=1, source_target_pairs={{0,2},{1,3},{2,0},{3,1},{4,6},{5,7},{6,4},{7,5},{8,10},{9,11},{10,... | collective-permute-start | bytes 184328 | tf_op jit(solution)/shard_map/ppermute | solution.py:126
  16.9 5.2 %collective-permute-start.6 = (f32[7680]{0:T(1024)S(1)}, f32[7680]{0:T(1024)S(1)}, u32[]{:S(2)}, u32[]{:S(2)}) collective-permute-start(f32[7680]{0:T(1024)S(1)} %get-tuple-element.16), channel_id=1, source_target_pairs={{0,4},{1,5},{2,6},{3,7},{4,0},{5,1},{6,2},{7,3},{8,12},{9,13},{10,... | collective-permute-start | bytes 92168 | tf_op jit(solution)/shard_map/ppermute | solution.py:126
  22.3 8.7 %collective-permute-start.7 = (f32[3840]{0:T(1024)S(1)}, f32[3840]{0:T(1024)S(1)}, u32[]{:S(2)}, u32[]{:S(2)}) collective-permute-start(f32[3840]{0:T(1024)S(1)} %get-tuple-element.18), channel_id=1, source_target_pairs={{0,8},{1,9},{2,10},{3,11},{4,12},{5,13},{6,14},{7,15},{8,0},{9,1},... | collective-permute-start | bytes 46088 | tf_op jit(solution)/shard_map/ppermute | solution.py:126
  29.2 203.7 %reduce-scatter.2.cloned.1.call-start = ((), (), s32[]{:S(2)}) async-start(), calls=%async_computation.3 | async-start | bytes 4456448 | tf_op jit(solution)/shard_map/reduce_scatter | solution.py:61
  31.0 7.4 %collective-permute-start.8 = (f32[1920]{0:T(1024)S(1)}, f32[1920]{0:T(1024)S(1)}, u32[]{:S(2)}, u32[]{:S(2)}) collective-permute-start(f32[1920]{0:T(1024)S(1)} %get-tuple-element.20), channel_id=1, source_target_pairs={{0,16},{16,0},{32,48},{48,32},{64,80},{80,64},{96,112},{112,96},{1... | collective-permute-start | bytes 23048 | tf_op jit(solution)/shard_map/ppermute | solution.py:126
  38.5 7.7 %collective-permute-start.9 = (f32[960]{0:T(1024)S(1)}, f32[960]{0:T(1024)S(1)}, u32[]{:S(2)}, u32[]{:S(2)}) collective-permute-start(f32[960]{0:T(1024)S(1)} %bitcast.319), channel_id=1, source_target_pairs={{0,32},{16,48},{32,0},{48,16},{64,96},{80,112},{96,64},{112,80},{1... | collective-permute-start | bytes 11528 | tf_op jit(solution)/shard_map/ppermute | solution.py:126
  46.3 3.7 %collective-permute-start.10 = (f32[480]{0:T(512)S(1)}, f32[480]{0:T(512)S(1)}, u32[]{:S(2)}, u32[]{:S(2)}) collective-permute-start(f32[480]{0:T(512)S(1)} %bitcast.321), channel_id=1, source_target_pairs={{0,64},{16,80},{32,96},{48,112},{64,0},{80,16},{96,32},{112,48},{1... | collective-permute-start | bytes 5768 | tf_op jit(solution)/shard_map/ppermute | solution.py:126
  50.1 6.1 %collective-permute-start.11 = (f32[240]{0:T(256)S(1)}, f32[240]{0:T(256)S(1)}, u32[]{:S(2)}, u32[]{:S(2)}) collective-permute-start(f32[240]{0:T(256)S(1)} %bitcast.322), channel_id=1, source_target_pairs={{0,128},{16,144},{32,160},{48,176},{64,192},{80,208},{96,224},{112... | collective-permute-start | bytes 2888 | tf_op jit(solution)/shard_map/ppermute | solution.py:126
  56.3 5.2 %collective-permute-start.12 = (f32[240]{0:T(256)S(1)}, f32[240]{0:T(256)S(1)}, u32[]{:S(2)}, u32[]{:S(2)}) collective-permute-start(f32[240]{0:T(256)S(1)} %add.905), channel_id=1, source_target_pairs={{0,128},{16,144},{32,160},{48,176},{64,192},{80,208},{96,224},{112... | collective-permute-start | bytes 2888 | tf_op jit(solution)/shard_map/ppermute | solution.py:130
  61.5 7.8 %collective-permute-start.13 = (f32[480]{0:T(512)S(1)}, f32[480]{0:T(512)S(1)}, u32[]{:S(2)}, u32[]{:S(2)}) collective-permute-start(f32[480]{0:T(512)S(1)} %pad_maximum_fusion.13), channel_id=1, source_target_pairs={{0,64},{16,80},{32,96},{48,112},{64,0},{80,16},{96,32},{112,48},{1... | collective-permute-start | bytes 5768 | tf_op jit(solution)/shard_map/ppermute | solution.py:130
  69.5 5.1 %collective-permute-start.14 = (f32[960]{0:T(1024)S(1)}, f32[960]{0:T(1024)S(1)}, u32[]{:S(2)}, u32[]{:S(2)}) collective-permute-start(f32[960]{0:T(1024)S(1)} %pad_maximum_fusion.12), channel_id=1, source_target_pairs={{0,32},{16,48},{32,0},{48,16},{64,96},{80,112},{96,64},{112,80},{1... | collective-permute-start | bytes 11528 | tf_op jit(solution)/shard_map/ppermute | solution.py:130
  74.8 3.9 %collective-permute-start.15 = (f32[1920]{0:T(1024)S(1)}, f32[1920]{0:T(1024)S(1)}, u32[]{:S(2)}, u32[]{:S(2)}) collective-permute-start(f32[1920]{0:T(1024)S(1)} %pad_maximum_fusion.11), channel_id=1, source_target_pairs={{0,16},{16,0},{32,48},{48,32},{64,80},{80,64},{96,112},{112,96},{1... | collective-permute-start | bytes 23048 | tf_op jit(solution)/shard_map/ppermute | solution.py:130
  116.8 2.0 copy-start
  119.0 17.3 %collective-permute-start = (f32[8,64,1024]{2,1,0:T(8,128)S(1)}, f32[8,64,1024]{2,1,0:T(8,128)}, u32[]{:S(2)}, u32[]{:S(2)}) collective-permute-start(f32[8,64,1024]{2,1,0:T(8,128)S(1)} %dynamic-slice_bitcast_fusion), channel_id=1, source_target_pairs={{0,1},{1,0},{2,3},{3,2},{4,5},{5,4},{6,7},{7,6},{8,9},{9,8},{10,11... | collective-permute-start | bytes 6291464 | tf_op jit(solution)/shard_map/ppermute | solution.py:55
  119.1 7.8 %collective-permute-start.16 = (f32[3840]{0:T(1024)S(1)}, f32[3840]{0:T(1024)S(1)}, u32[]{:S(2)}, u32[]{:S(2)}) collective-permute-start(f32[3840]{0:T(1024)S(1)} %pad_maximum_fusion.10), channel_id=1, source_target_pairs={{0,8},{1,9},{2,10},{3,11},{4,12},{5,13},{6,14},{7,15},{8,0},{9,1},... | collective-permute-start | bytes 46088 | tf_op jit(solution)/shard_map/ppermute | solution.py:130
  126.9 4.9 %collective-permute-start.17 = (f32[7680]{0:T(1024)S(1)}, f32[7680]{0:T(1024)S(1)}, u32[]{:S(2)}, u32[]{:S(2)}) collective-permute-start(f32[7680]{0:T(1024)S(1)} %pad_maximum_fusion.9), channel_id=1, source_target_pairs={{0,4},{1,5},{2,6},{3,7},{4,0},{5,1},{6,2},{7,3},{8,12},{9,13},{10,... | collective-permute-start | bytes 92168 | tf_op jit(solution)/shard_map/ppermute | solution.py:130
  131.9 4.3 %collective-permute-start.18 = (f32[15360]{0:T(1024)S(1)}, f32[15360]{0:T(1024)S(1)}, u32[]{:S(2)}, u32[]{:S(2)}) collective-permute-start(f32[15360]{0:T(1024)S(1)} %pad_maximum_fusion.6), channel_id=1, source_target_pairs={{0,2},{1,3},{2,0},{3,1},{4,6},{5,7},{6,4},{7,5},{8,10},{9,11},{10,... | collective-permute-start | bytes 184328 | tf_op jit(solution)/shard_map/ppermute | solution.py:130
  136.2 5.6 %collective-permute-start.19 = (f32[30720]{0:T(1024)S(1)}, f32[30720]{0:T(1024)S(1)}, u32[]{:S(2)}, u32[]{:S(2)}) collective-permute-start(f32[30720]{0:T(1024)S(1)} %pad_maximum_fusion.5), channel_id=1, source_target_pairs={{0,1},{1,0},{2,3},{3,2},{4,5},{5,4},{6,7},{7,6},{8,9},{9,8},{10,11... | collective-permute-start | bytes 368648 | tf_op jit(solution)/shard_map/ppermute | solution.py:130
  139.1 61.8 %copy-start.13 = (pred[64,64]{1,0:T(8,128)(4,1)S(1)}, pred[64,64]{1,0:T(8,128)(4,1)}, u32[]{:S(2)}) copy-start(pred[64,64]{1,0:T(8,128)(4,1)} %iota_compare_fusion) | copy-start | bytes 12292
  140.3 26.0 %collective-permute-start.1 = (f32[4,64,1024]{2,1,0:T(8,128)}, f32[4,64,1024]{2,1,0:T(8,128)}, u32[]{:S(2)}, u32[]{:S(2)}) collective-permute-start(f32[4,64,1024]{2,1,0:T(8,128)} %dynamic-slice_bitcast_fusion.1), channel_id=1, source_target_pairs={{0,2},{1,3},{2,0},{3,1},{4,6},{5,7},{6,4},{7,5},{8,10},{9,11},{10,... | collective-permute-start | bytes 3145736 | tf_op jit(solution)/shard_map/ppermute | solution.py:55
  142.5 64.5 %copy-start.14 = (pred[64,64]{1,0:T(8,128)(4,1)S(1)}, pred[64,64]{1,0:T(8,128)(4,1)}, u32[]{:S(2)}) copy-start(pred[64,64]{1,0:T(8,128)(4,1)} %iota_compare_fusion.1) | copy-start | bytes 12292
  143.3 89.6 %copy-start.2 = (bf16[64,1024]{1,0:T(8,128)(2,1)S(1)}, bf16[64,1024]{1,0:T(8,128)(2,1)}, u32[]{:S(2)}) copy-start(bf16[64,1024]{1,0:T(8,128)(2,1)} %param.5) | copy-start | bytes 393220
  167.6 1.0 copy-start.1
  167.6 69.2 %copy-start.12 = (f32[4096]{0:T(1024)S(1)}, f32[4096]{0:T(1024)}, u32[]{:S(2)}) copy-start(f32[4096]{0:T(1024)} %get-tuple-element.94) | copy-start | bytes 49156
  167.6 69.2 %copy-start.11 = (f32[4096]{0:T(1024)S(1)}, f32[4096]{0:T(1024)}, u32[]{:S(2)}) copy-start(f32[4096]{0:T(1024)} %get-tuple-element.96) | copy-start | bytes 49156
  167.7 69.3 %copy-start.10 = (f32[4096]{0:T(1024)S(1)}, f32[4096]{0:T(1024)}, u32[]{:S(2)}) copy-start(f32[4096]{0:T(1024)} %get-tuple-element.95) | copy-start | bytes 49156
  167.7 69.4 %copy-start.9 = (f32[4096]{0:T(1024)S(1)}, f32[4096]{0:T(1024)}, u32[]{:S(2)}) copy-start(f32[4096]{0:T(1024)} %get-tuple-element.97) | copy-start | bytes 49156
  167.7 69.4 %copy-start.8 = (f32[4096]{0:T(1024)S(1)}, f32[4096]{0:T(1024)}, u32[]{:S(2)}) copy-start(f32[4096]{0:T(1024)} %get-tuple-element.30) | copy-start | bytes 49156
  167.7 69.5 %copy-start.7 = (f32[4096]{0:T(1024)S(1)}, f32[4096]{0:T(1024)}, u32[]{:S(2)}) copy-start(f32[4096]{0:T(1024)} %get-tuple-element.27) | copy-start | bytes 49156
  167.7 69.6 %copy-start.6 = (f32[4096]{0:T(1024)S(1)}, f32[4096]{0:T(1024)}, u32[]{:S(2)}) copy-start(f32[4096]{0:T(1024)} %get-tuple-element.28) | copy-start | bytes 49156
  167.7 69.6 %copy-start.5 = (f32[4096]{0:T(1024)S(1)}, f32[4096]{0:T(1024)}, u32[]{:S(2)}) copy-start(f32[4096]{0:T(1024)} %get-tuple-element.29) | copy-start | bytes 49156
  168.6 68.8 %copy-start.4 = (f32[4096]{0:T(1024)S(1)}, f32[4096]{0:T(1024)}, u32[]{:S(2)}) copy-start(f32[4096]{0:T(1024)} %get-tuple-element.26) | copy-start | bytes 49156
  168.7 32.4 %collective-permute-start.2 = (f32[2,64,1024]{2,1,0:T(8,128)S(1)}, f32[2,64,1024]{2,1,0:T(8,128)S(1)}, u32[]{:S(2)}, u32[]{:S(2)}) collective-permute-start(f32[2,64,1024]{2,1,0:T(8,128)S(1)} %dynamic-slice_bitcast_fusion.2), channel_id=1, source_target_pairs={{0,4},{1,5},{2,6},{3,7},{4,0},{5,1},{6,2},{7,3},{8,12},{9,13},{10,... | collective-permute-start | bytes 1572872 | tf_op jit(solution)/shard_map/ppermute | solution.py:55
  202.2 30.7 %collective-permute-start.3 = (f32[1,64,1024]{2,1,0:T(8,128)S(1)}, f32[1,64,1024]{2,1,0:T(8,128)S(1)}, u32[]{:S(2)}, u32[]{:S(2)}) collective-permute-start(f32[1,64,1024]{2,1,0:T(8,128)S(1)} %constant_dynamic-slice_fusion.12), channel_id=1, source_target_pairs={{0,8},{1,9},{2,10},{3,11},{4,12},{5,13},{6,14},{7,15},{8,0},{9,1},... | collective-permute-start | bytes 786440 | tf_op jit(solution)/shard_map/ppermute | solution.py:55
  234.6 5.1 %collective-permute-start.22 = (f32[320,64]{0,1:T(8,128)S(1)}, f32[320,64]{0,1:T(8,128)S(1)}, u32[]{:S(2)}, u32[]{:S(2)}) collective-permute-start(f32[320,64]{0,1:T(8,128)S(1)} %fusion.81), channel_id=1, source_target_pairs={{0,3},{1,2},{2,1},{3,0},{4,7},{5,6},{6,5},{7,4},{8,11},{9,10},{10,... | collective-permute-start | bytes 245768 | tf_op jit(solution)/shard_map/ppermute | solution.py:92
  234.7 6.5 %collective-permute-start.21 = (f32[320,64]{0,1:T(8,128)S(1)}, f32[320,64]{0,1:T(8,128)S(1)}, u32[]{:S(2)}, u32[]{:S(2)}) collective-permute-start(f32[320,64]{0,1:T(8,128)S(1)} %fusion.81), channel_id=1, source_target_pairs={{0,2},{1,3},{2,0},{3,1},{4,6},{5,7},{6,4},{7,5},{8,10},{9,11},{10,... | collective-permute-start | bytes 245768 | tf_op jit(solution)/shard_map/ppermute | solution.py:92
  235.9 5.4 %collective-permute-start.20 = (f32[320,64]{0,1:T(8,128)S(1)}, f32[320,64]{0,1:T(8,128)S(1)}, u32[]{:S(2)}, u32[]{:S(2)}) collective-permute-start(f32[320,64]{0,1:T(8,128)S(1)} %fusion.81), channel_id=1, source_target_pairs={{0,1},{1,0},{2,3},{3,2},{4,5},{5,4},{6,7},{7,6},{8,9},{9,8},{10,11... | collective-permute-start | bytes 245768 | tf_op jit(solution)/shard_map/ppermute | solution.py:92
  241.3 36.7 %copy-start.3 = (f32[64,1024]{1,0:T(8,128)S(1)}, f32[64,1024]{1,0:T(8,128)}, u32[]{:S(2)}) copy-start(f32[64,1024]{1,0:T(8,128)} %reduce-scatter.2.cloned.1.call-done) | copy-start | bytes 786436
  241.3 36.7 %copy-start.16 = (f32[1024]{0:T(1024)S(1)}, f32[1024]{0:T(1024)}, u32[]{:S(2)}) copy-start(f32[1024]{0:T(1024)} %param.7) | copy-start | bytes 12292
  241.4 11.1 %collective-permute-start.25 = (f32[320,64]{0,1:T(8,128)S(1)}, f32[320,64]{0,1:T(8,128)S(1)}, u32[]{:S(2)}, u32[]{:S(2)}) collective-permute-start(f32[320,64]{0,1:T(8,128)S(1)} %fusion.139), channel_id=1, source_target_pairs={{0,12},{1,13},{2,14},{3,15},{4,8},{5,9},{6,10},{7,11},{8,4},{9,5},... | collective-permute-start | bytes 245768 | tf_op jit(solution)/shard_map/ppermute | solution.py:92
  241.5 12.6 %collective-permute-start.24 = (f32[320,64]{0,1:T(8,128)S(1)}, f32[320,64]{0,1:T(8,128)S(1)}, u32[]{:S(2)}, u32[]{:S(2)}) collective-permute-start(f32[320,64]{0,1:T(8,128)S(1)} %fusion.139), channel_id=1, source_target_pairs={{0,8},{1,9},{2,10},{3,11},{4,12},{5,13},{6,14},{7,15},{8,0},{9,1},... | collective-permute-start | bytes 245768 | tf_op jit(solution)/shard_map/ppermute | solution.py:92
  246.5 10.6 %collective-permute-start.23 = (f32[320,64]{0,1:T(8,128)S(1)}, f32[320,64]{0,1:T(8,128)S(1)}, u32[]{:S(2)}, u32[]{:S(2)}) collective-permute-start(f32[320,64]{0,1:T(8,128)S(1)} %fusion.139), channel_id=1, source_target_pairs={{0,4},{1,5},{2,6},{3,7},{4,0},{5,1},{6,2},{7,3},{8,12},{9,13},{10,... | collective-permute-start | bytes 245768 | tf_op jit(solution)/shard_map/ppermute | solution.py:92
  257.2 7.3 %collective-permute-start.28 = (f32[320,64]{0,1:T(8,128)S(1)}, f32[320,64]{0,1:T(8,128)S(1)}, u32[]{:S(2)}, u32[]{:S(2)}) collective-permute-start(f32[320,64]{0,1:T(8,128)S(1)} %fusion.138), channel_id=1, source_target_pairs={{0,48},{16,32},{32,16},{48,0},{64,112},{80,96},{96,80},{112,64},{1... | collective-permute-start | bytes 245768 | tf_op jit(solution)/shard_map/ppermute | solution.py:92
  258.8 7.0 %collective-permute-start.27 = (f32[320,64]{0,1:T(8,128)S(1)}, f32[320,64]{0,1:T(8,128)S(1)}, u32[]{:S(2)}, u32[]{:S(2)}) collective-permute-start(f32[320,64]{0,1:T(8,128)S(1)} %fusion.138), channel_id=1, source_target_pairs={{0,32},{16,48},{32,0},{48,16},{64,96},{80,112},{96,64},{112,80},{1... | collective-permute-start | bytes 245768 | tf_op jit(solution)/shard_map/ppermute | solution.py:92
  259.9 6.0 %collective-permute-start.26 = (f32[320,64]{0,1:T(8,128)S(1)}, f32[320,64]{0,1:T(8,128)S(1)}, u32[]{:S(2)}, u32[]{:S(2)}) collective-permute-start(f32[320,64]{0,1:T(8,128)S(1)} %fusion.138), channel_id=1, source_target_pairs={{0,16},{16,0},{32,48},{48,32},{64,80},{80,64},{96,112},{112,96},{1... | collective-permute-start | bytes 245768 | tf_op jit(solution)/shard_map/ppermute | solution.py:92
  265.9 5.6 %collective-permute-start.31 = (f32[320,64]{0,1:T(8,128)S(1)}, f32[320,64]{0,1:T(8,128)S(1)}, u32[]{:S(2)}, u32[]{:S(2)}) collective-permute-start(f32[320,64]{0,1:T(8,128)S(1)} %fusion.137), channel_id=1, source_target_pairs={{0,192},{16,208},{32,224},{48,240},{64,128},{80,144},{96,160},{112... | collective-permute-start | bytes 245768 | tf_op jit(solution)/shard_map/ppermute | solution.py:92
  266.5 6.1 %collective-permute-start.30 = (f32[320,64]{0,1:T(8,128)S(1)}, f32[320,64]{0,1:T(8,128)S(1)}, u32[]{:S(2)}, u32[]{:S(2)}) collective-permute-start(f32[320,64]{0,1:T(8,128)S(1)} %fusion.137), channel_id=1, source_target_pairs={{0,128},{16,144},{32,160},{48,176},{64,192},{80,208},{96,224},{112... | collective-permute-start | bytes 245768 | tf_op jit(solution)/shard_map/ppermute | solution.py:92
  268.8 4.9 %collective-permute-start.29 = (f32[320,64]{0,1:T(8,128)S(1)}, f32[320,64]{0,1:T(8,128)S(1)}, u32[]{:S(2)}, u32[]{:S(2)}) collective-permute-start(f32[320,64]{0,1:T(8,128)S(1)} %fusion.137), channel_id=1, source_target_pairs={{0,64},{16,80},{32,96},{48,112},{64,0},{80,16},{96,32},{112,48},{1... | collective-permute-start | bytes 245768 | tf_op jit(solution)/shard_map/ppermute | solution.py:92
Sparse Core Ops, SparseCore 0:
  9.9 42.7 all-gather.4
  55.1 47.8 all-gather.2
  106.6 82.2 reduce-scatter.1

commit v5 on v4

--- a/solution.py
+++ b/solution.py
@@ -161,7 +161,6 @@
     row_part, col_part = tile_products(tile_values, tile_index, row_probes, col_probes, col_count)
     row_total = sum_rows(row_part)
     col_total = sum_columns(col_part)
-    row_total, col_total, inverses = lax.optimization_barrier((row_total, col_total, inverses))
     product = self_relatedness[None, :] * probe_block.astype(jnp.float32) + row_total + col_total
     along_local = jnp.dot(wide_basis, product.T, precision=highest)
     along = radix_sum(along_local, ("col", "row"))

time: 288 us -> 287 us (level)
    all_gather x1, waiting for transfers between devices: 0.11 us -> 3.28 us  [shards(): col_probes = lax.all_gather(probe_block, 'row', axis=1, tiled=True)]
    ppermute x8, waiting for transfers between devices: 10.3 us -> 7.15 us  [halving_sum(): flat = keep + lax.ppermute(give, axis, pairs)]
where the time goes in v5:
time: 287 us; the launch traced here: 286 us
  other arithmetic  78.5 us (27%)
  waiting for transfers between devices  66.9 us (23%)
  starting transfers between devices  59.3 us (21%)
  between operations  40.4 us (14%)
  matrix products  30.5 us (11%)
  local copies, waits for them, and re-layouts  10.1 us (4%)
    another operation x4, other arithmetic, inverse_factors(): factors = jnp.linalg.cholesky(gram_blocks)  30.8 us
    another operation x3, other arithmetic, inverse_factors(): return jax.scipy.linalg.solve_triangular(factors, identity, lower=True)  26 us
    ppermute x4, waiting for transfers between devices, sum_rows(): row_part = keep + lax.ppermute(give, 'col', pairs)  23.1 us
    ppermute x12, waiting for transfers between devices, radix_sum(): received.append(lax.ppermute(value, axis, pairs))  20.6 us
    ppermute x8, starting transfers between devices, halving_sum(): flat = keep + lax.ppermute(give, axis, pairs)  20 us
    ppermute x12, starting transfers between devices, radix_sum(): received.append(lax.ppermute(value, axis, pairs))  16.9 us
    ppermute x8, starting transfers between devices, halving_sum(): other = lax.ppermute(flat, axis, pairs)  14.1 us
    unnamed x28, other arithmetic  12.6 us
  transfers between devices with their start and end apart: 35, of which 23 were waited for; matrix products, arithmetic and copies ran while one was open for 38% of the time, Pallas kernels for 0%

profile of v5, /device:TPU:8, one launch (start us, length us, event | category | flops | bytes accessed | tf_op | source)
XLA Modules:
  0.0 285.8 jit_solution(2211178725254685527)
XLA Ops:
  8.0 1.2 pad_maximum_fusion
  10.8 1.3 collective-permute-done.4
  12.3 2.0 collective-permute-start.5
  14.3 2.3 collective-permute-done.5
  16.9 3.4 %collective-permute-start.6 = (f32[7680]{0:T(1024)S(1)}, f32[7680]{0:T(1024)S(1)}, u32[]{:S(2)}, u32[]{:S(2)}) collective-permute-start(f32[7680]{0:T(1024)S(1)} %get-tuple-element.10), channel_id=1, source_target_pairs={{0,4},{1,5},{2,6},{3,7},{4,0},{5,1},{6,2},{7,3},{8,12},{9,13},{10,... | collective-permute-start | bytes 92168 | tf_op jit(solution)/shard_map/ppermute | solution.py:126
  20.2 1.9 collective-permute-done.6
  22.3 6.9 %collective-permute-start.7 = (f32[3840]{0:T(1024)S(1)}, f32[3840]{0:T(1024)S(1)}, u32[]{:S(2)}, u32[]{:S(2)}) collective-permute-start(f32[3840]{0:T(1024)S(1)} %get-tuple-element.12), channel_id=1, source_target_pairs={{0,8},{1,9},{2,10},{3,11},{4,12},{5,13},{6,14},{7,15},{8,0},{9,1},... | collective-permute-start | bytes 46088 | tf_op jit(solution)/shard_map/ppermute | solution.py:126
  29.3 1.6 collective-permute-done.7
  31.0 1.6 collective-permute-start.8
  37.4 2.8 collective-permute-start.9
  49.2 2.7 collective-permute-start.11
  57.5 1.0 collective-permute-start.12
  63.1 1.6 collective-permute-start.13
  69.1 2.9 %collective-permute-done.14 = f32[960]{0:T(1024)S(1)} collective-permute-done((f32[960]{0:T(1024)S(1)}, f32[960]{0:T(1024)S(1)}, u32[]{:S(2)}, u32[]{:S(2)}) %collective-permute-start.14) | collective-permute-done | bytes 3872 | tf_op jit(solution)/shard_map/ppermute | solution.py:130
  72.8 3.3 %collective-permute-done.15 = f32[1920]{0:T(1024)S(1)} collective-permute-done((f32[1920]{0:T(1024)S(1)}, f32[1920]{0:T(1024)S(1)}, u32[]{:S(2)}, u32[]{:S(2)}) %collective-permute-start.15) | collective-permute-done | bytes 7712 | tf_op jit(solution)/shard_map/ppermute | solution.py:130
  76.1 2.1 fusion.4
  78.3 2.2 fusion.8
  80.4 2.2 fusion.12
  82.6 2.2 fusion.16
  84.7 2.9 %add_dynamic-update-slice_fusion.15 = (f32[64,16384]{1,0:T(8,128)}, f32[64,1024]{1,0:T(8,128)S(1)}) fusion(f32[64,1024]{1,0:T(8,128)S(1)} %fusion.4, f32[64,1024]{1,0:T(8,128)S(1)} %fusion.8, f32[64,1024]{1,0:T(8,128)S(1)} %fusion.12, f32[64,1024]{1,0:T(8,128)S(1)} %fusion.16, pred[]{:T(512)S(6)} %eq.619, pred[]{:T(512)S(6)} %eq.618, pred[]{:T(512)S(6)} %eq.617, ...), kind=kOutput, calls=%fused_computation.85 | convolution fusion | flops 134807552 | bytes 3801097 | tf_op jit(solution)/shard_map/dot_general | solution.py:22
  91.6 0.8 add_dynamic-update-slice_fusion.9
  99.7 3.3 %all-gather.3.cloned.1.call-done = bf16[64,16384]{1,0:T(8,128)(2,1)} async-done(((bf16[64,1024]{1,0:T(8,128)(2,1)}), bf16[64,16384]{1,0:T(8,128)(2,1)}) %all-gather.3.cloned.1.call-update) | async-done | bytes 2097168 | tf_op jit(solution)/shard_map/all_gather | solution.py:158
  102.9 2.4 fusion.6
  105.4 2.4 fusion.10
  107.8 2.4 fusion.14
  110.2 2.4 fusion.18
  112.7 2.5 bitcast_dynamic-update-slice_fusion.15
  116.7 2.0 copy-done
  119.1 5.8 %collective-permute-start.16 = (f32[3840]{0:T(1024)S(1)}, f32[3840]{0:T(1024)S(1)}, u32[]{:S(2)}, u32[]{:S(2)}) collective-permute-start(f32[3840]{0:T(1024)S(1)} %pad_maximum_fusion.10), channel_id=1, source_target_pairs={{0,8},{1,9},{2,10},{3,11},{4,12},{5,13},{6,14},{7,15},{8,0},{9,1},... | collective-permute-start | bytes 46088 | tf_op jit(solution)/shard_map/ppermute | solution.py:130
  124.9 1.9 collective-permute-done.16
  126.8 2.6 collective-permute-start.17
  130.0 1.7 collective-permute-done.17
  131.7 1.6 collective-permute-start.18
  134.0 2.1 collective-permute-done.18
  136.2 2.6 bitcast_add_fusion
  138.8 1.1 dynamic-slice_bitcast_fusion.1
  139.9 1.6 collective-permute-start.1
  142.8 23.1 %collective-permute-done.1 = f32[4,64,1024]{2,1,0:T(8,128)} collective-permute-done((f32[4,64,1024]{2,1,0:T(8,128)}, f32[4,64,1024]{2,1,0:T(8,128)}, u32[]{:S(2)}, u32[]{:S(2)}) %collective-permute-start.1) | collective-permute-done | bytes 1048608 | tf_op jit(solution)/shard_map/ppermute | solution.py:55
  165.9 1.4 bitcast_add_fusion.1
  167.3 1.0 copy-done.1
  168.4 2.7 collective-permute-start.2
  171.4 29.3 %custom-call.8 = f32[5,64,64]{2,1,0:T(8,128)S(1)} custom-call(f32[5,64,64]{2,1,0:T(8,128)S(1)} %fusion.38), custom_call_target="Cholesky" | custom-call | tf_op jit(solution)/shard_map/jit(cholesky)/cholesky | solution.py:138
  201.5 1.1 bitcast_add_fusion.2
  202.6 3.9 %collective-permute-start.3 = (f32[1,64,1024]{2,1,0:T(8,128)S(1)}, f32[1,64,1024]{2,1,0:T(8,128)S(1)}, u32[]{:S(2)}, u32[]{:S(2)}) collective-permute-start(f32[1,64,1024]{2,1,0:T(8,128)S(1)} %constant_dynamic-slice_fusion.12), channel_id=1, source_target_pairs={{0,8},{1,9},{2,10},{3,11},{4,12},{5,13},{6,14},{7,15},{8,0},{9,1},... | collective-permute-start | bytes 786440 | tf_op jit(solution)/shard_map/ppermute | solution.py:55
  207.4 24.6 %custom-call.9 = f32[5,1,64,64]{2,3,1,0:T(8,128)S(1)} custom-call(f32[5,1,64,64]{3,2,1,0:T(8,128)S(1)} %select_bitcast_fusion), custom_call_target="InvertDiagBlocksLowerTriangular" | custom-call | tf_op jit(solution)/shard_map/jit(_solve_triangular)/vmap()/triangular_solve | solution.py:140
  232.1 1.0 fusion.35
  233.9 0.9 collective-permute-start.21
  234.8 0.9 collective-permute-start.20
  237.1 1.9 collective-permute-done.22
  238.9 1.2 collective-permute-done.21
  240.2 1.1 collective-permute-start.25
  241.3 5.0 %collective-permute-start.24 = (f32[320,64]{0,1:T(8,128)S(1)}, f32[320,64]{0,1:T(8,128)S(1)}, u32[]{:S(2)}, u32[]{:S(2)}) collective-permute-start(f32[320,64]{0,1:T(8,128)S(1)} %fusion.121), channel_id=1, source_target_pairs={{0,8},{1,9},{2,10},{3,11},{4,12},{5,13},{6,14},{7,15},{8,0},{9,1},... | collective-permute-start | bytes 245768 | tf_op jit(solution)/shard_map/ppermute | solution.py:92
  247.5 5.7 %collective-permute-done.24 = f32[320,64]{0,1:T(8,128)S(1)} collective-permute-done((f32[320,64]{0,1:T(8,128)S(1)}, f32[320,64]{0,1:T(8,128)S(1)}, u32[]{:S(2)}, u32[]{:S(2)}) %collective-permute-start.24) | collective-permute-done | bytes 81952 | tf_op jit(solution)/shard_map/ppermute | solution.py:92
  253.1 3.4 %collective-permute-done.23 = f32[320,64]{0,1:T(8,128)S(1)} collective-permute-done((f32[320,64]{0,1:T(8,128)S(1)}, f32[320,64]{0,1:T(8,128)S(1)}, u32[]{:S(2)}, u32[]{:S(2)}) %collective-permute-start.23) | collective-permute-done | bytes 81952 | tf_op jit(solution)/shard_map/ppermute | solution.py:92
  256.6 1.2 collective-permute-start.28
  257.8 1.2 collective-permute-start.27
  259.0 1.8 collective-permute-start.26
  260.8 1.7 collective-permute-done.28
  262.5 1.4 collective-permute-done.27
  264.5 1.1 collective-permute-start.31
  265.6 2.7 collective-permute-start.30
  269.2 2.5 collective-permute-done.30
  271.7 1.2 collective-permute-done.29
  277.2 1.2 convolution_subtract_fusion
  (203 shorter events, 33.9 us)
Async XLA Ops:
  7.2 25.4 %copy-start.7 = (s32[5,3]{0,1:T(4,128)S(1)}, s32[5,3]{0,1:T(4,128)}, u32[]{:S(2)}) copy-start(s32[5,3]{0,1:T(4,128)} %param.9) | copy-start | bytes 184
  7.2 68.9 %all-gather.5.cloned.1.call-start = ((), (), s32[]{:S(2)}) async-start(), calls=%async_computation.2 | async-start | bytes 2228224 | tf_op jit(solution)/shard_map/all_gather | solution.py:157
  7.9 95.0 %all-gather.3.cloned.1.call-start = ((), (), s32[]{:S(2)}) async-start(), calls=%async_computation.1 | async-start | bytes 2228224 | tf_op jit(solution)/shard_map/all_gather | solution.py:158
  10.7 1.4 collective-permute-start.4
  12.3 4.3 %collective-permute-start.5 = (f32[15360]{0:T(1024)S(1)}, f32[15360]{0:T(1024)S(1)}, u32[]{:S(2)}, u32[]{:S(2)}) collective-permute-start(f32[15360]{0:T(1024)S(1)} %bitcast.314), channel_id=1, source_target_pairs={{0,2},{1,3},{2,0},{3,1},{4,6},{5,7},{6,4},{7,5},{8,10},{9,11},{10,... | collective-permute-start | bytes 184328 | tf_op jit(solution)/shard_map/ppermute | solution.py:126
  16.9 5.2 %collective-permute-start.6 = (f32[7680]{0:T(1024)S(1)}, f32[7680]{0:T(1024)S(1)}, u32[]{:S(2)}, u32[]{:S(2)}) collective-permute-start(f32[7680]{0:T(1024)S(1)} %get-tuple-element.10), channel_id=1, source_target_pairs={{0,4},{1,5},{2,6},{3,7},{4,0},{5,1},{6,2},{7,3},{8,12},{9,13},{10,... | collective-permute-start | bytes 92168 | tf_op jit(solution)/shard_map/ppermute | solution.py:126
  22.3 8.7 %collective-permute-start.7 = (f32[3840]{0:T(1024)S(1)}, f32[3840]{0:T(1024)S(1)}, u32[]{:S(2)}, u32[]{:S(2)}) collective-permute-start(f32[3840]{0:T(1024)S(1)} %get-tuple-element.12), channel_id=1, source_target_pairs={{0,8},{1,9},{2,10},{3,11},{4,12},{5,13},{6,14},{7,15},{8,0},{9,1},... | collective-permute-start | bytes 46088 | tf_op jit(solution)/shard_map/ppermute | solution.py:126
  29.2 202.8 %reduce-scatter.2.cloned.1.call-start = ((), (), s32[]{:S(2)}) async-start(), calls=%async_computation.3 | async-start | bytes 4456448 | tf_op jit(solution)/shard_map/reduce_scatter | solution.py:61
  31.0 6.3 %collective-permute-start.8 = (f32[1920]{0:T(1024)S(1)}, f32[1920]{0:T(1024)S(1)}, u32[]{:S(2)}, u32[]{:S(2)}) collective-permute-start(f32[1920]{0:T(1024)S(1)} %get-tuple-element.14), channel_id=1, source_target_pairs={{0,16},{16,0},{32,48},{48,32},{64,80},{80,64},{96,112},{112,96},{1... | collective-permute-start | bytes 23048 | tf_op jit(solution)/shard_map/ppermute | solution.py:126
  37.4 7.4 %collective-permute-start.9 = (f32[960]{0:T(1024)S(1)}, f32[960]{0:T(1024)S(1)}, u32[]{:S(2)}, u32[]{:S(2)}) collective-permute-start(f32[960]{0:T(1024)S(1)} %bitcast.317), channel_id=1, source_target_pairs={{0,32},{16,48},{32,0},{48,16},{64,96},{80,112},{96,64},{112,80},{1... | collective-permute-start | bytes 11528 | tf_op jit(solution)/shard_map/ppermute | solution.py:126
  45.0 4.1 %collective-permute-start.10 = (f32[480]{0:T(512)S(1)}, f32[480]{0:T(512)S(1)}, u32[]{:S(2)}, u32[]{:S(2)}) collective-permute-start(f32[480]{0:T(512)S(1)} %bitcast.319), channel_id=1, source_target_pairs={{0,64},{16,80},{32,96},{48,112},{64,0},{80,16},{96,32},{112,48},{1... | collective-permute-start | bytes 5768 | tf_op jit(solution)/shard_map/ppermute | solution.py:126
  49.2 8.3 %collective-permute-start.11 = (f32[240]{0:T(256)S(1)}, f32[240]{0:T(256)S(1)}, u32[]{:S(2)}, u32[]{:S(2)}) collective-permute-start(f32[240]{0:T(256)S(1)} %bitcast.320), channel_id=1, source_target_pairs={{0,128},{16,144},{32,160},{48,176},{64,192},{80,208},{96,224},{112... | collective-permute-start | bytes 2888 | tf_op jit(solution)/shard_map/ppermute | solution.py:126
  57.5 5.6 %collective-permute-start.12 = (f32[240]{0:T(256)S(1)}, f32[240]{0:T(256)S(1)}, u32[]{:S(2)}, u32[]{:S(2)}) collective-permute-start(f32[240]{0:T(256)S(1)} %add.907), channel_id=1, source_target_pairs={{0,128},{16,144},{32,160},{48,176},{64,192},{80,208},{96,224},{112... | collective-permute-start | bytes 2888 | tf_op jit(solution)/shard_map/ppermute | solution.py:130
  63.1 3.6 %collective-permute-start.13 = (f32[480]{0:T(512)S(1)}, f32[480]{0:T(512)S(1)}, u32[]{:S(2)}, u32[]{:S(2)}) collective-permute-start(f32[480]{0:T(512)S(1)} %pad_maximum_fusion.13), channel_id=1, source_target_pairs={{0,64},{16,80},{32,96},{48,112},{64,0},{80,16},{96,32},{112,48},{1... | collective-permute-start | bytes 5768 | tf_op jit(solution)/shard_map/ppermute | solution.py:130
  66.9 5.1 %collective-permute-start.14 = (f32[960]{0:T(1024)S(1)}, f32[960]{0:T(1024)S(1)}, u32[]{:S(2)}, u32[]{:S(2)}) collective-permute-start(f32[960]{0:T(1024)S(1)} %pad_maximum_fusion.12), channel_id=1, source_target_pairs={{0,32},{16,48},{32,0},{48,16},{64,96},{80,112},{96,64},{112,80},{1... | collective-permute-start | bytes 11528 | tf_op jit(solution)/shard_map/ppermute | solution.py:130
  72.2 3.9 %collective-permute-start.15 = (f32[1920]{0:T(1024)S(1)}, f32[1920]{0:T(1024)S(1)}, u32[]{:S(2)}, u32[]{:S(2)}) collective-permute-start(f32[1920]{0:T(1024)S(1)} %pad_maximum_fusion.11), channel_id=1, source_target_pairs={{0,16},{16,0},{32,48},{48,32},{64,80},{80,64},{96,112},{112,96},{1... | collective-permute-start | bytes 23048 | tf_op jit(solution)/shard_map/ppermute | solution.py:130
  116.7 2.0 copy-start
  118.9 17.3 %collective-permute-start = (f32[8,64,1024]{2,1,0:T(8,128)S(1)}, f32[8,64,1024]{2,1,0:T(8,128)}, u32[]{:S(2)}, u32[]{:S(2)}) collective-permute-start(f32[8,64,1024]{2,1,0:T(8,128)S(1)} %dynamic-slice_bitcast_fusion), channel_id=1, source_target_pairs={{0,1},{1,0},{2,3},{3,2},{4,5},{5,4},{6,7},{7,6},{8,9},{9,8},{10,11... | collective-permute-start | bytes 6291464 | tf_op jit(solution)/shard_map/ppermute | solution.py:55
  119.1 7.7 %collective-permute-start.16 = (f32[3840]{0:T(1024)S(1)}, f32[3840]{0:T(1024)S(1)}, u32[]{:S(2)}, u32[]{:S(2)}) collective-permute-start(f32[3840]{0:T(1024)S(1)} %pad_maximum_fusion.10), channel_id=1, source_target_pairs={{0,8},{1,9},{2,10},{3,11},{4,12},{5,13},{6,14},{7,15},{8,0},{9,1},... | collective-permute-start | bytes 46088 | tf_op jit(solution)/shard_map/ppermute | solution.py:130
  126.8 4.9 %collective-permute-start.17 = (f32[7680]{0:T(1024)S(1)}, f32[7680]{0:T(1024)S(1)}, u32[]{:S(2)}, u32[]{:S(2)}) collective-permute-start(f32[7680]{0:T(1024)S(1)} %pad_maximum_fusion.9), channel_id=1, source_target_pairs={{0,4},{1,5},{2,6},{3,7},{4,0},{5,1},{6,2},{7,3},{8,12},{9,13},{10,... | collective-permute-start | bytes 92168 | tf_op jit(solution)/shard_map/ppermute | solution.py:130
  131.7 4.3 %collective-permute-start.18 = (f32[15360]{0:T(1024)S(1)}, f32[15360]{0:T(1024)S(1)}, u32[]{:S(2)}, u32[]{:S(2)}) collective-permute-start(f32[15360]{0:T(1024)S(1)} %pad_maximum_fusion.6), channel_id=1, source_target_pairs={{0,2},{1,3},{2,0},{3,1},{4,6},{5,7},{6,4},{7,5},{8,10},{9,11},{10,... | collective-permute-start | bytes 184328 | tf_op jit(solution)/shard_map/ppermute | solution.py:130
  136.1 5.4 %collective-permute-start.19 = (f32[30720]{0:T(1024)S(1)}, f32[30720]{0:T(1024)S(1)}, u32[]{:S(2)}, u32[]{:S(2)}) collective-permute-start(f32[30720]{0:T(1024)S(1)} %pad_maximum_fusion.5), channel_id=1, source_target_pairs={{0,1},{1,0},{2,3},{3,2},{4,5},{5,4},{6,7},{7,6},{8,9},{9,8},{10,11... | collective-permute-start | bytes 368648 | tf_op jit(solution)/shard_map/ppermute | solution.py:130
  139.9 26.0 %collective-permute-start.1 = (f32[4,64,1024]{2,1,0:T(8,128)}, f32[4,64,1024]{2,1,0:T(8,128)}, u32[]{:S(2)}, u32[]{:S(2)}) collective-permute-start(f32[4,64,1024]{2,1,0:T(8,128)} %dynamic-slice_bitcast_fusion.1), channel_id=1, source_target_pairs={{0,2},{1,3},{2,0},{3,1},{4,6},{5,7},{6,4},{7,5},{8,10},{9,11},{10,... | collective-permute-start | bytes 3145736 | tf_op jit(solution)/shard_map/ppermute | solution.py:55
  142.4 89.7 %copy-start.2 = (bf16[64,1024]{1,0:T(8,128)(2,1)S(1)}, bf16[64,1024]{1,0:T(8,128)(2,1)}, u32[]{:S(2)}) copy-start(bf16[64,1024]{1,0:T(8,128)(2,1)} %param.5) | copy-start | bytes 393220
  142.8 28.3 %copy-start.6 = (f32[4096]{0:T(1024)S(1)}, f32[4096]{0:T(1024)}, u32[]{:S(2)}) copy-start(f32[4096]{0:T(1024)} %get-tuple-element.25) | copy-start | bytes 49156
  167.3 1.0 copy-start.1
  167.3 69.1 %copy-start.5 = (f32[4096]{0:T(1024)S(1)}, f32[4096]{0:T(1024)}, u32[]{:S(2)}) copy-start(f32[4096]{0:T(1024)} %get-tuple-element.88) | copy-start | bytes 49156
  167.3 69.2 %copy-start.4 = (f32[4096]{0:T(1024)S(1)}, f32[4096]{0:T(1024)}, u32[]{:S(2)}) copy-start(f32[4096]{0:T(1024)} %get-tuple-element.90) | copy-start | bytes 49156
  167.3 69.3 %copy-start.3 = (f32[4096]{0:T(1024)S(1)}, f32[4096]{0:T(1024)}, u32[]{:S(2)}) copy-start(f32[4096]{0:T(1024)} %get-tuple-element.89) | copy-start | bytes 49156
  168.4 33.1 %collective-permute-start.2 = (f32[2,64,1024]{2,1,0:T(8,128)S(1)}, f32[2,64,1024]{2,1,0:T(8,128)S(1)}, u32[]{:S(2)}, u32[]{:S(2)}) collective-permute-start(f32[2,64,1024]{2,1,0:T(8,128)S(1)} %dynamic-slice_bitcast_fusion.2), channel_id=1, source_target_pairs={{0,4},{1,5},{2,6},{3,7},{4,0},{5,1},{6,2},{7,3},{8,12},{9,13},{10,... | collective-permute-start | bytes 1572872 | tf_op jit(solution)/shard_map/ppermute | solution.py:55
  202.6 29.4 %collective-permute-start.3 = (f32[1,64,1024]{2,1,0:T(8,128)S(1)}, f32[1,64,1024]{2,1,0:T(8,128)S(1)}, u32[]{:S(2)}, u32[]{:S(2)}) collective-permute-start(f32[1,64,1024]{2,1,0:T(8,128)S(1)} %constant_dynamic-slice_fusion.12), channel_id=1, source_target_pairs={{0,8},{1,9},{2,10},{3,11},{4,12},{5,13},{6,14},{7,15},{8,0},{9,1},... | collective-permute-start | bytes 786440 | tf_op jit(solution)/shard_map/ppermute | solution.py:55
  233.8 5.1 %collective-permute-start.22 = (f32[320,64]{0,1:T(8,128)S(1)}, f32[320,64]{0,1:T(8,128)S(1)}, u32[]{:S(2)}, u32[]{:S(2)}) collective-permute-start(f32[320,64]{0,1:T(8,128)S(1)} %fusion.80), channel_id=1, source_target_pairs={{0,3},{1,2},{2,1},{3,0},{4,7},{5,6},{6,5},{7,4},{8,11},{9,10},{10,... | collective-permute-start | bytes 245768 | tf_op jit(solution)/shard_map/ppermute | solution.py:92
  233.9 6.2 %collective-permute-start.21 = (f32[320,64]{0,1:T(8,128)S(1)}, f32[320,64]{0,1:T(8,128)S(1)}, u32[]{:S(2)}, u32[]{:S(2)}) collective-permute-start(f32[320,64]{0,1:T(8,128)S(1)} %fusion.80), channel_id=1, source_target_pairs={{0,2},{1,3},{2,0},{3,1},{4,6},{5,7},{6,4},{7,5},{8,10},{9,11},{10,... | collective-permute-start | bytes 245768 | tf_op jit(solution)/shard_map/ppermute | solution.py:92
  234.8 5.3 %collective-permute-start.20 = (f32[320,64]{0,1:T(8,128)S(1)}, f32[320,64]{0,1:T(8,128)S(1)}, u32[]{:S(2)}, u32[]{:S(2)}) collective-permute-start(f32[320,64]{0,1:T(8,128)S(1)} %fusion.80), channel_id=1, source_target_pairs={{0,1},{1,0},{2,3},{3,2},{4,5},{5,4},{6,7},{7,6},{8,9},{9,8},{10,11... | collective-permute-start | bytes 245768 | tf_op jit(solution)/shard_map/ppermute | solution.py:92
  240.2 7.3 %collective-permute-start.25 = (f32[320,64]{0,1:T(8,128)S(1)}, f32[320,64]{0,1:T(8,128)S(1)}, u32[]{:S(2)}, u32[]{:S(2)}) collective-permute-start(f32[320,64]{0,1:T(8,128)S(1)} %fusion.121), channel_id=1, source_target_pairs={{0,12},{1,13},{2,14},{3,15},{4,8},{5,9},{6,10},{7,11},{8,4},{9,5},... | collective-permute-start | bytes 245768 | tf_op jit(solution)/shard_map/ppermute | solution.py:92
  241.3 11.9 %collective-permute-start.24 = (f32[320,64]{0,1:T(8,128)S(1)}, f32[320,64]{0,1:T(8,128)S(1)}, u32[]{:S(2)}, u32[]{:S(2)}) collective-permute-start(f32[320,64]{0,1:T(8,128)S(1)} %fusion.121), channel_id=1, source_target_pairs={{0,8},{1,9},{2,10},{3,11},{4,12},{5,13},{6,14},{7,15},{8,0},{9,1},... | collective-permute-start | bytes 245768 | tf_op jit(solution)/shard_map/ppermute | solution.py:92
  246.3 10.2 %collective-permute-start.23 = (f32[320,64]{0,1:T(8,128)S(1)}, f32[320,64]{0,1:T(8,128)S(1)}, u32[]{:S(2)}, u32[]{:S(2)}) collective-permute-start(f32[320,64]{0,1:T(8,128)S(1)} %fusion.121), channel_id=1, source_target_pairs={{0,4},{1,5},{2,6},{3,7},{4,0},{5,1},{6,2},{7,3},{8,12},{9,13},{10,... | collective-permute-start | bytes 245768 | tf_op jit(solution)/shard_map/ppermute | solution.py:92
  256.6 5.9 %collective-permute-start.28 = (f32[320,64]{0,1:T(8,128)S(1)}, f32[320,64]{0,1:T(8,128)S(1)}, u32[]{:S(2)}, u32[]{:S(2)}) collective-permute-start(f32[320,64]{0,1:T(8,128)S(1)} %fusion.120), channel_id=1, source_target_pairs={{0,48},{16,32},{32,16},{48,0},{64,112},{80,96},{96,80},{112,64},{1... | collective-permute-start | bytes 245768 | tf_op jit(solution)/shard_map/ppermute | solution.py:92
  257.8 6.1 %collective-permute-start.27 = (f32[320,64]{0,1:T(8,128)S(1)}, f32[320,64]{0,1:T(8,128)S(1)}, u32[]{:S(2)}, u32[]{:S(2)}) collective-permute-start(f32[320,64]{0,1:T(8,128)S(1)} %fusion.120), channel_id=1, source_target_pairs={{0,32},{16,48},{32,0},{48,16},{64,96},{80,112},{96,64},{112,80},{1... | collective-permute-start | bytes 245768 | tf_op jit(solution)/shard_map/ppermute | solution.py:92
  259.0 5.4 %collective-permute-start.26 = (f32[320,64]{0,1:T(8,128)S(1)}, f32[320,64]{0,1:T(8,128)S(1)}, u32[]{:S(2)}, u32[]{:S(2)}) collective-permute-start(f32[320,64]{0,1:T(8,128)S(1)} %fusion.120), channel_id=1, source_target_pairs={{0,16},{16,0},{32,48},{48,32},{64,80},{80,64},{96,112},{112,96},{1... | collective-permute-start | bytes 245768 | tf_op jit(solution)/shard_map/ppermute | solution.py:92
  264.5 4.7 %collective-permute-start.31 = (f32[320,64]{0,1:T(8,128)S(1)}, f32[320,64]{0,1:T(8,128)S(1)}, u32[]{:S(2)}, u32[]{:S(2)}) collective-permute-start(f32[320,64]{0,1:T(8,128)S(1)} %fusion.119), channel_id=1, source_target_pairs={{0,192},{16,208},{32,224},{48,240},{64,128},{80,144},{96,160},{112... | collective-permute-start | bytes 245768 | tf_op jit(solution)/shard_map/ppermute | solution.py:92
  265.6 6.1 %collective-permute-start.30 = (f32[320,64]{0,1:T(8,128)S(1)}, f32[320,64]{0,1:T(8,128)S(1)}, u32[]{:S(2)}, u32[]{:S(2)}) collective-permute-start(f32[320,64]{0,1:T(8,128)S(1)} %fusion.119), channel_id=1, source_target_pairs={{0,128},{16,144},{32,160},{48,176},{64,192},{80,208},{96,224},{112... | collective-permute-start | bytes 245768 | tf_op jit(solution)/shard_map/ppermute | solution.py:92
  268.3 4.6 %collective-permute-start.29 = (f32[320,64]{0,1:T(8,128)S(1)}, f32[320,64]{0,1:T(8,128)S(1)}, u32[]{:S(2)}, u32[]{:S(2)}) collective-permute-start(f32[320,64]{0,1:T(8,128)S(1)} %fusion.119), channel_id=1, source_target_pairs={{0,64},{16,80},{32,96},{48,112},{64,0},{80,16},{96,32},{112,48},{1... | collective-permute-start | bytes 245768 | tf_op jit(solution)/shard_map/ppermute | solution.py:92
Sparse Core Ops, SparseCore 0:
  9.9 42.7 all-gather.4
  55.1 47.7 all-gather.2
  106.6 82.2 reduce-scatter.1
